TPU v7x, 128 devices: a whole 4x4x4 slice. The times are simulated.
128 devices in a mesh: tm: 16 (over z_hi, y, core), tensor: 8 (over z_lo, x).
Axes of the slice: x: 4, y: 4, z: 4 (z_hi: 2, z_lo: 2; z = z_hi * 2 + z_lo), core: 2. Of those that a mesh axis runs over, the one named last changes fastest.
Arguments:
- hidden_in: bfloat16 [16, 2, 256, 5120], P('tm', None, None, 'tensor'), may hold values from -6 to 6
- noisy_queries: bfloat16 [16, 2, 256, 5120], P('tm', None, None, 'tensor'), may hold values from -28 to 28
- noisy_keys: bfloat16 [16, 2, 256, 5120], P('tm', None, None, 'tensor'), may hold values from -5 to 5
- noisy_values: bfloat16 [16, 2, 256, 5120], P('tm', None, None, 'tensor'), may hold values from -15 to 15
- clean_cache: bfloat16 [16, 2, 256, 5120], P('tm', None, None, 'tensor'), may hold values from -9 to 9
- out_proj: bfloat16 [5120, 5120], P('tensor'), may hold values from -0.078125 to 0.078125
- branch_in: bfloat16 [5120, 2560], P(None, 'tensor'), may hold values from -0.078125 to 0.078125
- branch_out: bfloat16 [2560, 5120], P('tensor'), may hold values from -0.125 to 0.125
- action_table: bfloat16 [128, 2560], P(None, 'tensor'), may hold values from -6 to 6
- actions: int32 [16, 4], P('tm'), may hold values from 0 to 127
- offsets: int32 [16], P('tm'), may hold values from 0 to 2, as said below
- out_grad: bfloat16 [16, 2, 256, 5120], P('tm', None, None, 'tensor'), may hold values from -6 to 6
Outputs:
- layer_out: bfloat16 [16, 2, 256, 5120], P('tm', None, None, 'tensor')
- input_grad: bfloat16 [16, 2, 256, 5120], P('tm', None, None, 'tensor')
- query_grad: bfloat16 [16, 2, 256, 5120], P('tm', None, None, 'tensor')
- key_grad: bfloat16 [16, 2, 256, 5120], P('tm', None, None, 'tensor')
- value_grad: bfloat16 [16, 2, 256, 5120], P('tm', None, None, 'tensor')
- cache_grad: float32 [16, 2, 256, 5120], P('tm', None, None, 'tensor')
- proj_weight_grad: float32 [5120, 5120], P('tensor', 'tm')
- branch_in_grad: float32 [5120, 2560], P('tm', 'tensor')
- branch_out_grad: float32 [2560, 5120], P('tensor', 'tm')
- table_grad: float32 [128, 2560], P('tm', 'tensor')
Inputs may be any that keep to these rules, and one draw needn't show every extreme that they name: offsets[c] <= c; spans 1, 2, 7, 8, 9 and the last reach min(c, 2).
All inputs are finite; a program needn't handle non-finite values.
Results may differ from a plain program's by a relative error of at most 0.013.
Values may be sent and summed in bfloat16 or wider, within the bound.
No kernel may reach another device: no remote copies, remote signals or barrier semaphores. Data moves between devices by JAX's collectives and lax.ppermute only.
A program may use at most 192 MiB of HBM per device.

v0:
```python
import jax
import jax.numpy as jnp
from jax import lax
from jax.sharding import PartitionSpec as P

HD = 128


GELU_C = 0.7978845608028654
GELU_A = 0.044715


def from_behind(value, axis, steps):
    count = lax.axis_size(axis)
    first, last = (max(0, -steps), min(count, count - steps))
    return lax.ppermute(value, axis, [(source, source + steps) for source in range(first, last)])


def gelu_value(inputs):
    inner = GELU_C * (inputs + GELU_A * inputs * inputs * inputs)
    return 0.5 * inputs * (1.0 + jnp.tanh(inner))


def gelu_slope(inputs):
    tangent = jnp.tanh(GELU_C * (inputs + GELU_A * inputs * inputs * inputs))
    return 0.5 * (1.0 + tangent) + 0.5 * inputs * (1.0 - tangent * tangent) * GELU_C * (
        1.0 + 3.0 * GELU_A * inputs * inputs
    )


def contract_rows(left, right):
    return lax.dot_general(
        left, right, (((0,), (0,)), ((), ())), preferred_element_type=jnp.float32
    )


def contract_cols(left, right):
    return lax.dot_general(
        left, right, (((1,), (1,)), ((), ())), preferred_element_type=jnp.float32
    )


def body(
    hidden_in,
    noisy_queries,
    noisy_keys,
    noisy_values,
    clean_cache,
    out_proj,
    branch_in,
    branch_out,
    action_table,
    actions,
    offsets,
    out_grad,
):
    steps_here = noisy_queries.shape[1]
    tokens_here = noisy_queries.shape[2]
    head_width = noisy_queries.shape[3]
    heads_here = head_width // HD
    model_width = out_proj.shape[1]
    row_count = steps_here * tokens_here
    action_count = actions.shape[1]
    score_scale = HD ** (-0.5)
    full_inputs, full_grads = (
        lax.all_gather(hidden_in, "tensor", axis=3, tiled=True),
        lax.all_gather(out_grad, "tensor", axis=3, tiled=True),
    )
    input_rows = full_inputs.reshape(row_count, model_width)
    grad_rows = full_grads.reshape(row_count, model_width)
    own_cache = clean_cache[0]
    nearer = from_behind(own_cache, "tm", 1)
    farther = from_behind(own_cache, "tm", 2)
    reach = offsets[0]
    allowed = jnp.concatenate(
        [
            jnp.full((tokens_here,), reach >= 2),
            jnp.full((tokens_here,), reach >= 1),
            jnp.ones((tokens_here,), bool),
        ]
    )
    block_shape = (steps_here, tokens_here, head_width)
    key_block = jnp.concatenate(
        [
            jnp.broadcast_to(farther[0], block_shape),
            jnp.broadcast_to(nearer[0], block_shape),
            noisy_keys[0],
        ],
        axis=1,
    )
    value_block = jnp.concatenate(
        [
            jnp.broadcast_to(farther[1], block_shape),
            jnp.broadcast_to(nearer[1], block_shape),
            noisy_values[0],
        ],
        axis=1,
    )
    query_heads = noisy_queries[0].reshape(steps_here, tokens_here, heads_here, HD)
    key_heads = key_block.reshape(steps_here, 3 * tokens_here, heads_here, HD)
    value_heads = value_block.reshape(steps_here, 3 * tokens_here, heads_here, HD)
    scores = (
        jnp.einsum("sqhe,skhe->shqk", query_heads, key_heads, preferred_element_type=jnp.float32)
        * score_scale
    )
    masked = jnp.where(allowed[None, None, None, :], scores, -1e30)
    largest = jnp.max(masked, axis=-1, keepdims=True)
    raised = jnp.exp(masked - largest)
    probs = raised / jnp.sum(raised, axis=-1, keepdims=True)
    probs_low = probs.astype(jnp.bfloat16)
    attended = (
        jnp.einsum("shqk,skhe->sqhe", probs_low, value_heads, preferred_element_type=jnp.float32)
        .astype(jnp.bfloat16)
        .reshape(row_count, head_width)
    )
    onehot = (actions[0][:, None] == jnp.arange(action_table.shape[0])[None, :]).astype(
        jnp.bfloat16
    )
    action_rows = jnp.dot(onehot, action_table, preferred_element_type=jnp.float32)
    branch_width = branch_in.shape[1]
    pre_act = (
        jnp.dot(input_rows, branch_in, preferred_element_type=jnp.float32).reshape(
            steps_here, action_count, tokens_here // action_count, branch_width
        )
        + action_rows[None, :, None, :]
    )
    pre_act = pre_act.reshape(row_count, branch_width)
    branch_act = gelu_value(pre_act).astype(jnp.bfloat16)
    partial_value = jnp.dot(attended, out_proj, preferred_element_type=jnp.float32) + jnp.dot(
        branch_act, branch_out, preferred_element_type=jnp.float32
    )
    layer_sum = lax.psum_scatter(
        partial_value.reshape(1, steps_here, tokens_here, model_width).astype(jnp.bfloat16),
        "tensor",
        scatter_dimension=3,
        tiled=True,
    ).astype(jnp.float32)
    layer_out = (hidden_in.astype(jnp.float32) + layer_sum).astype(jnp.bfloat16)
    attended_grad = contract_cols(grad_rows, out_proj).astype(jnp.bfloat16)
    pre_grad = (contract_cols(grad_rows, branch_out) * gelu_slope(pre_act)).astype(jnp.bfloat16)
    in_term = contract_rows(input_rows, pre_grad)
    out_term = contract_rows(branch_act, grad_rows)
    grouped = jnp.sum(
        pre_grad.reshape(
            steps_here, action_count, tokens_here // action_count, branch_width
        ).astype(jnp.float32),
        axis=(0, 2),
    )
    table_term = jnp.dot(onehot.astype(jnp.float32).T, grouped, precision=lax.Precision.HIGHEST)
    proj_term = contract_rows(attended, grad_rows)
    summed = (
        lax.psum_scatter(
            proj_term.astype(jnp.bfloat16), "tm", scatter_dimension=1, tiled=True
        ).astype(jnp.float32),
        lax.psum_scatter(
            in_term.astype(jnp.bfloat16), "tm", scatter_dimension=0, tiled=True
        ).astype(jnp.float32),
        lax.psum_scatter(
            out_term.astype(jnp.bfloat16), "tm", scatter_dimension=1, tiled=True
        ).astype(jnp.float32),
        lax.psum_scatter(
            table_term.astype(jnp.bfloat16), "tm", scatter_dimension=0, tiled=True
        ).astype(jnp.float32),
    )
    input_term = contract_cols(pre_grad, branch_in)
    input_sum = lax.psum_scatter(
        input_term.reshape(1, steps_here, tokens_here, model_width).astype(jnp.bfloat16),
        "tensor",
        scatter_dimension=3,
        tiled=True,
    ).astype(jnp.float32)
    input_grad = (out_grad.astype(jnp.float32) + input_sum).astype(jnp.bfloat16)
    weight_grads = (summed, input_grad)
    grad_heads = attended_grad.reshape(steps_here, tokens_here, heads_here, HD)
    value_all = jnp.einsum(
        "shqk,sqhe->skhe", probs_low, grad_heads, preferred_element_type=jnp.float32
    )
    prob_grad = jnp.einsum(
        "sqhe,skhe->shqk", grad_heads, value_heads, preferred_element_type=jnp.float32
    )
    centre = jnp.sum(prob_grad * probs, axis=-1, keepdims=True)
    score_grad = (probs * (prob_grad - centre) * score_scale).astype(jnp.bfloat16)
    query_grad = (
        jnp.einsum("shqk,skhe->sqhe", score_grad, key_heads, preferred_element_type=jnp.float32)
        .astype(jnp.bfloat16)
        .reshape(1, steps_here, tokens_here, head_width)
    )
    key_all = jnp.einsum(
        "shqk,sqhe->skhe", score_grad, query_heads, preferred_element_type=jnp.float32
    ).reshape(steps_here, 3 * tokens_here, head_width)
    value_all = value_all.reshape(steps_here, 3 * tokens_here, head_width)
    own_key = key_all[:, 2 * tokens_here :].astype(jnp.bfloat16)[None]
    own_value = value_all[:, 2 * tokens_here :].astype(jnp.bfloat16)[None]
    toward_far = jnp.stack(
        [jnp.sum(key_all[:, :tokens_here], axis=0), jnp.sum(value_all[:, :tokens_here], axis=0)]
    )
    toward_near = jnp.stack(
        [
            jnp.sum(key_all[:, tokens_here : 2 * tokens_here], axis=0),
            jnp.sum(value_all[:, tokens_here : 2 * tokens_here], axis=0),
        ]
    )
    from_next = from_behind(toward_near.astype(jnp.bfloat16), "tm", -1).astype(toward_near.dtype)
    from_after = from_behind(toward_far.astype(jnp.bfloat16), "tm", -2).astype(toward_far.dtype)
    received = from_next + from_after
    attention_grads = (query_grad, own_key, own_value, received[None])
    summed, input_grad = weight_grads
    query_grad, own_key, own_value, cache_grad = attention_grads
    return (
        layer_out,
        input_grad,
        query_grad,
        own_key,
        own_value,
        cache_grad,
        summed[0],
        summed[1],
        summed[2],
        summed[3],
    )


def solution(mesh):
    in_specs = (
        P("tm", None, None, "tensor"),
        P("tm", None, None, "tensor"),
        P("tm", None, None, "tensor"),
        P("tm", None, None, "tensor"),
        P("tm", None, None, "tensor"),
        P("tensor", None),
        P(None, "tensor"),
        P("tensor", None),
        P(None, "tensor"),
        P("tm", None),
        P("tm"),
        P("tm", None, None, "tensor"),
    )
    out_specs = (
        P("tm", None, None, "tensor"),
        P("tm", None, None, "tensor"),
        P("tm", None, None, "tensor"),
        P("tm", None, None, "tensor"),
        P("tm", None, None, "tensor"),
        P("tm", None, None, "tensor"),
        P("tensor", "tm"),
        P("tm", "tensor"),
        P("tensor", "tm"),
        P("tm", "tensor"),
    )
    return jax.shard_map(body, mesh=mesh, in_specs=in_specs, out_specs=out_specs, check_vma=False)
```

profile of v0, /device:TPU:0, one launch (start us, length us, event | category | flops | bytes accessed | tf_op | source)
XLA Modules:
  0.0 702.2 jit_solution(14903340942910305338)
XLA Ops:
  9.8 64.8 %all-gather.3.cloned.1.call-done = bf16[1,2,256,5120]{3,2,1,0:T(8,128)(2,1)} async-done(((bf16[1,2,256,640]{3,2,1,0:T(8,128)(2,1)}), bf16[1,2,256,5120]{3,2,1,0:T(8,128)(2,1)}) %all-gather.3.cloned.1.call-update) | async-done | bytes 5242896 | tf_op jit(solution)/shard_map/all_gather | solution.py:66
  74.6 6.5 fusion.44
  83.3 54.1 %all-gather.5.cloned.1.call-done = bf16[1,2,256,5120]{3,2,1,0:T(8,128)(2,1)} async-done(((bf16[1,2,256,640]{3,2,1,0:T(8,128)(2,1)}), bf16[1,2,256,5120]{3,2,1,0:T(8,128)(2,1)}) %all-gather.5.cloned.1.call-update) | async-done | bytes 5242896 | tf_op jit(solution)/shard_map/all_gather | solution.py:67
  137.4 6.4 fusion.39
  148.1 6.2 fusion.5
  154.3 5.9 copy.128
  160.2 6.2 convolution_convert_fusion.2
  166.4 5.9 copy.130
  213.9 6.3 convolution_convert_fusion
  220.3 5.7 convolution_convert_fusion.1
  225.9 13.6 %copy.126 = bf16[1,2,256,5120]{2,1,0,3:T(2,128)(2,1)} copy(bf16[1,2,256,5120]{3,2,1,0:T(8,128)(2,1)} %bitcast.116) | data formatting | bytes 10485760
  239.6 5.7 copy.138
  246.4 6.6 fusion.74
  257.8 13.6 %copy.124 = bf16[1,2,256,5120]{2,1,0,3:T(2,128)(2,1)} copy(bf16[1,2,256,5120]{3,2,1,0:T(8,128)(2,1)} %bitcast.113) | data formatting | bytes 10485760
  271.4 5.7 copy.137
  277.2 8.8 %convolution_convert_fusion.4 = bf16[512,640]{1,0:T(8,128)(2,1)S(1)} fusion(bf16[512,5120]{1,0:T(8,128)(2,1)} %bitcast.122, bf16[640,5120]{1,0:T(8,128)(2,1)} %param.17), kind=kOutput, calls=%fused_computation.34 | convolution fusion | flops 3355770880 | bytes 12451840 | tf_op jit(solution)/shard_map/dot_general | solution.py:38
  287.5 5.5 fusion.26
  293.1 15.6 %fusion.11 = f32[2,5,768,128]{2,3,1,0:T(8,128)} fusion(bf16[2,256,5,128]{1,3,2,0:T(8,128)(2,1)S(1)} %bitcast.132, f32[2,5,256,768]{2,3,1,0:T(8,128)} %fusion.26, f32[2,5,256,768]{2,3,1,0:T(8,128)} %copy-done.22, f32[2,5,256]{2,1,0:T(8,128)S(1)} %get-tuple-element.48), kind=kOutput, calls=%fused_computation.16 | convolution fusion | flops 517082368 | bytes 20326400 | tf_op jit(solution)/shard_map/shqk,sqhe->skhe/dot_general | solution.py:188
  325.9 13.6 %fusion.30 = bf16[2,5,128,256]{3,2,1,0:T(8,128)(2,1)} fusion(f32[2,5,256,768]{2,3,1,0:T(8,128)} %fusion.26, bf16[2,256,5,128]{3,1,2,0:T(8,128)(2,1)S(1)} %copy-done.5, bf16[2,256,5,128]{3,1,2,0:T(8,128)(2,1)S(1)} %copy-done.12, bf16[2,256,5,128]{3,1,2,0:T(8,128)(2,1)S(1)} %copy-done.14, f32[2,5,256,768]{2,3,1,0:T(8,128)} %copy-done.22, ...), kind=kOutput, calls=%fused_computation.33 | convolution fusion | flops 523308288 | bytes 18360320 | tf_op jit(solution)/shard_map/shqk,skhe->sqhe/dot_general | solution.py:184
  348.1 35.3 %reduce-scatter.20.cloned.1.call-done = bf16[320,320]{1,0:T(8,128)(2,1)} async-done(((bf16[5120,320]{1,0:T(8,128)(2,1)}), bf16[320,320]{1,0:T(8,128)(2,1)}) %reduce-scatter.20.cloned.1.call-update) | async-done | bytes 204816
  385.4 79.2 %reduce-scatter.22.cloned.1.call-done = bf16[320,320]{1,0:T(8,128)(2,1)} async-done(((bf16[5120,320]{1,0:T(8,128)(2,1)}), bf16[320,320]{1,0:T(8,128)(2,1)}) %reduce-scatter.22.cloned.1.call-update) | async-done | bytes 204816
  466.6 91.5 %reduce-scatter.14.cloned.1.call-done = bf16[640,320]{0,1:T(8,128)(2,1)} async-done(((bf16[640,5120]{0,1:T(8,128)(2,1)}), bf16[640,320]{0,1:T(8,128)(2,1)}) %reduce-scatter.14.cloned.1.call-update) | async-done | bytes 409616 | tf_op jit(solution)/shard_map/reduce_scatter | solution.py:152
  560.1 62.1 %reduce-scatter.18.cloned.1.call-done = bf16[640,512]{1,0:T(8,128)(2,1)} async-done(((bf16[5120,512]{1,0:T(8,128)(2,1)}), bf16[640,512]{1,0:T(8,128)(2,1)}) %reduce-scatter.18.cloned.1.call-update) | async-done | bytes 655376
  627.8 58.6 %reduce-scatter.16.cloned.1.call-done = bf16[640,512]{1,0:T(8,128)(2,1)} async-done(((bf16[5120,512]{1,0:T(8,128)(2,1)}), bf16[640,512]{1,0:T(8,128)(2,1)}) %reduce-scatter.16.cloned.1.call-update) | async-done | bytes 655376
  (130 shorter events, 102.6 us)
Async XLA Ops:
  7.2 67.4 %copy-start = (bf16[5120,320]{0,1:T(8,128)(2,1)S(1)}, bf16[5120,320]{0,1:T(8,128)(2,1)}, u32[]{:S(2)}) copy-start(bf16[5120,320]{0,1:T(8,128)(2,1)} %param.18) | copy-start | bytes 9830404
  7.2 67.4 %all-gather.3.cloned.1.call-start = ((), (), s32[]{:S(2)}) async-start(), calls=%async_computation.5 | async-start | bytes 5898240 | tf_op jit(solution)/shard_map/all_gather | solution.py:66
  7.9 129.4 %all-gather.5.cloned.1.call-start = ((), (), s32[]{:S(2)}) async-start(), calls=%async_computation.6 | async-start | bytes 5898240 | tf_op jit(solution)/shard_map/all_gather | solution.py:67
  8.7 335.2 %all-reduce.3.cloned.1.call-start = ((), (), s32[]{:S(2)}) async-start(), calls=%async_computation.12 | async-start | bytes 196608
  137.4 9.7 %copy-start.20 = (s32[1,4]{1,0:T(1,128)S(1)}, s32[1,4]{1,0:T(1,128)}, u32[]{:S(2)}) copy-start(s32[1,4]{1,0:T(1,128)} %param.21) | copy-start | bytes 52
  148.1 235.3 %reduce-scatter.20.cloned.1.call-start = ((), (), s32[]{:S(2)}) async-start(), calls=%async_computation.10 | async-start | bytes 4177920
  160.1 304.5 %reduce-scatter.22.cloned.1.call-start = ((), (), s32[]{:S(2)}) async-start(), calls=%async_computation.11 | async-start | bytes 4177920
  172.3 385.8 %reduce-scatter.14.cloned.1.call-start = ((), (), s32[]{:S(2)}) async-start(), calls=%async_computation.7 | async-start | bytes 6963200 | tf_op jit(solution)/shard_map/reduce_scatter | solution.py:152
  174.5 16.0 %collective-permute-start.1 = (bf16[2,256,640]{1,2,0:T(8,128)(2,1)}, bf16[2,256,640]{1,2,0:T(8,128)(2,1)}, u32[]{:S(2)}, u32[]{:S(2)}) collective-permute-start(bf16[2,256,640]{1,2,0:T(8,128)(2,1)} %bitcast.152), channel_id=1, source_target_pairs={{0,8},{8,16},{16,24},{24,32},{32,40},{40,48},{48,56},{56,64},{64,7... | collective-permute-start | bytes 1966088 | tf_op jit(solution)/shard_map/ppermute | solution.py:16
  176.9 18.5 %collective-permute-start = (bf16[2,256,640]{1,2,0:T(8,128)(2,1)}, bf16[2,256,640]{1,2,0:T(8,128)(2,1)}, u32[]{:S(2)}, u32[]{:S(2)}) collective-permute-start(bf16[2,256,640]{1,2,0:T(8,128)(2,1)} %bitcast.153), channel_id=1, source_target_pairs={{0,16},{8,24},{16,32},{24,40},{32,48},{40,56},{48,64},{56,72},{64,... | collective-permute-start | bytes 1966088 | tf_op jit(solution)/shard_map/ppermute | solution.py:16
  207.7 6.2 slice-start
  220.2 402.0 %reduce-scatter.18.cloned.1.call-start = ((), (), s32[]{:S(2)}) async-start(), calls=%async_computation.9 | async-start | bytes 5898240
  245.3 7.6 %copy-start.2 = (f32[512,320]{0,1:T(8,128)S(1)}, f32[512,320]{0,1:T(8,128)}, u32[]{:S(2)}) copy-start(f32[512,320]{0,1:T(8,128)} %copy.92) | copy-start | bytes 1966084
  245.3 441.1 %reduce-scatter.16.cloned.1.call-start = ((), (), s32[]{:S(2)}) async-start(), calls=%async_computation.8 | async-start | bytes 5898240
  246.4 6.6 copy-start.3
  277.1 10.3 %copy-start.8 = (bf16[1,2,256,640]{2,3,1,0:T(8,128)(2,1)S(1)}, bf16[1,2,256,640]{2,3,1,0:T(8,128)(2,1)}, u32[]{:S(2)}) copy-start(bf16[1,2,256,640]{2,3,1,0:T(8,128)(2,1)} %copy.83) | copy-start | bytes 1966084
  277.2 10.3 %copy-start.16 = (bf16[2,256,5,128]{1,3,2,0:T(8,128)(2,1)S(1)}, bf16[2,256,5,128]{1,3,2,0:T(8,128)(2,1)}, u32[]{:S(2)}) copy-start(bf16[2,256,5,128]{1,3,2,0:T(8,128)(2,1)} %copy-done.15) | copy-start | bytes 1966084
  315.4 6.5 copy-start.21
  315.4 10.5 %copy-start.5 = (bf16[2,256,5,128]{3,1,2,0:T(8,128)(2,1)S(1)}, bf16[2,256,5,128]{3,1,2,0:T(8,128)(2,1)}, u32[]{:S(2)}) copy-start(bf16[2,256,5,128]{3,1,2,0:T(8,128)(2,1)} %copy.87) | copy-start | bytes 1966084
  315.4 10.5 %copy-start.12 = (bf16[2,256,5,128]{3,1,2,0:T(8,128)(2,1)S(1)}, bf16[2,256,5,128]{3,1,2,0:T(8,128)(2,1)}, u32[]{:S(2)}) copy-start(bf16[2,256,5,128]{3,1,2,0:T(8,128)(2,1)} %copy-done.11) | copy-start | bytes 1966084
  315.4 10.5 %copy-start.14 = (bf16[2,256,5,128]{3,1,2,0:T(8,128)(2,1)S(1)}, bf16[2,256,5,128]{3,1,2,0:T(8,128)(2,1)}, u32[]{:S(2)}) copy-start(bf16[2,256,5,128]{3,1,2,0:T(8,128)(2,1)} %copy-done.13) | copy-start | bytes 1966084
  318.4 26.8 %collective-permute-start.3 = (bf16[2,256,640]{1,2,0:T(8,128)(2,1)}, bf16[2,256,640]{1,2,0:T(8,128)(2,1)}, u32[]{:S(2)}, u32[]{:S(2)}) collective-permute-start(bf16[2,256,640]{1,2,0:T(8,128)(2,1)} %pad_maximum_fusion.13), channel_id=1, source_target_pairs={{16,0},{24,8},{32,16},{40,24},{48,32},{56,40},{64,48},{72,56},{80,... | collective-permute-start | bytes 1966088 | tf_op jit(solution)/shard_map/ppermute | solution.py:16
  320.6 24.6 %collective-permute-start.2 = (bf16[2,256,640]{1,2,0:T(8,128)(2,1)}, bf16[2,256,640]{1,2,0:T(8,128)(2,1)}, u32[]{:S(2)}, u32[]{:S(2)}) collective-permute-start(bf16[2,256,640]{1,2,0:T(8,128)(2,1)} %pad_maximum_fusion.12), channel_id=1, source_target_pairs={{8,0},{16,8},{24,16},{32,24},{40,32},{48,40},{56,48},{64,56},{72,6... | collective-permute-start | bytes 1966088 | tf_op jit(solution)/shard_map/ppermute | solution.py:16
  465.8 229.3 %copy-start.1 = (bf16[5120,320]{0,1:T(8,128)(2,1)S(1)}, bf16[5120,320]{0,1:T(8,128)(2,1)}, u32[]{:S(2)}) copy-start(bf16[5120,320]{0,1:T(8,128)(2,1)} %param.18) | copy-start | bytes 9830404
  (13 other events, 38.7 us)
Sparse Core Ops, SparseCore 0:
  9.7 64.8 all-gather.2
  76.2 61.1 all-gather.4
  148.2 132.1 all-reduce.2
  284.4 98.9 reduce-scatter.19
  387.3 77.3 reduce-scatter.21
  468.7 89.4 reduce-scatter.13
  560.6 61.6 reduce-scatter.17
  624.6 61.7 reduce-scatter.15
where the time goes:
time: 713 us; the launch traced here: 702 us
  waiting for transfers between devices  448 us (63%)
  local copies, waits for them, and re-layouts  109 us (15%)
  matrix products  102 us (14%)
  other arithmetic  16.3 us (2%)
  between operations  16.2 us (2%)
  starting transfers between devices  9.66 us (1%)
    unnamed x13, waiting for transfers between devices  237 us
    reduce_scatter x1, waiting for transfers between devices, body(): lax.psum_scatter(proj_term.astype(jnp.bfloat16), 'tm', scatter_dimension=...  91.5 us
    unnamed x73, local copies, waits for them, and re-layouts  87.9 us
    all_gather x1, waiting for transfers between devices, body(): lax.all_gather(hidden_in, 'tensor', axis=3, tiled=True)  64.8 us
    all_gather x1, waiting for transfers between devices, body(): lax.all_gather(out_grad, 'tensor', axis=3, tiled=True)  54.1 us
    dot_general x3, matrix products, contract_cols(): lax.dot_general(left, right, (((1,), (1,)), ((), ())), preferred_element_...  20.9 us
    dot_general x3, matrix products, contract_rows(): lax.dot_general(left, right, (((0,), (0,)), ((), ())), preferred_element_...  18.7 us
    dot_general x1, matrix products, body(): jnp.einsum('shqk,sqhe->skhe', score_grad, query_heads, preferred_element_...  15.6 us
  transfers between devices with their start and end apart: 12, of which 8 were waited for; matrix products, arithmetic and copies ran while one was open for 29% of the time, Pallas kernels for 0%

commit v1 on v0

--- a/solution.py
+++ b/solution.py
@@ -62,12 +62,11 @@
     row_count = steps_here * tokens_here
     action_count = actions.shape[1]
     score_scale = HD ** (-0.5)
-    full_inputs, full_grads = (
-        lax.all_gather(hidden_in, "tensor", axis=3, tiled=True),
-        lax.all_gather(out_grad, "tensor", axis=3, tiled=True),
-    )
-    input_rows = full_inputs.reshape(row_count, model_width)
-    grad_rows = full_grads.reshape(row_count, model_width)
+    full_both = lax.all_gather(
+        jnp.concatenate([hidden_in, out_grad], axis=0), "tensor", axis=3, tiled=True
+    )
+    input_rows = full_both[0].reshape(row_count, model_width)
+    grad_rows = full_both[1].reshape(row_count, model_width)
     own_cache = clean_cache[0]
     nearer = from_behind(own_cache, "tm", 1)
     farther = from_behind(own_cache, "tm", 2)
@@ -138,8 +137,16 @@
     layer_out = (hidden_in.astype(jnp.float32) + layer_sum).astype(jnp.bfloat16)
     attended_grad = contract_cols(grad_rows, out_proj).astype(jnp.bfloat16)
     pre_grad = (contract_cols(grad_rows, branch_out) * gelu_slope(pre_act)).astype(jnp.bfloat16)
-    in_term = contract_rows(input_rows, pre_grad)
-    out_term = contract_rows(branch_act, grad_rows)
+    tm_count = lax.axis_size("tm")
+    col_block = model_width // tm_count
+    grad_split = grad_rows.reshape(row_count, tm_count, col_block)
+    in_term = jnp.einsum(
+        "rjk,rn->jkn",
+        input_rows.reshape(row_count, tm_count, model_width // tm_count),
+        pre_grad,
+        preferred_element_type=jnp.float32,
+    )
+    out_term = jnp.einsum("rk,rjn->jkn", branch_act, grad_split, preferred_element_type=jnp.float32)
     grouped = jnp.sum(
         pre_grad.reshape(
             steps_here, action_count, tokens_here // action_count, branch_width
@@ -147,21 +154,21 @@
         axis=(0, 2),
     )
     table_term = jnp.dot(onehot.astype(jnp.float32).T, grouped, precision=lax.Precision.HIGHEST)
-    proj_term = contract_rows(attended, grad_rows)
-    summed = (
-        lax.psum_scatter(
-            proj_term.astype(jnp.bfloat16), "tm", scatter_dimension=1, tiled=True
-        ).astype(jnp.float32),
-        lax.psum_scatter(
-            in_term.astype(jnp.bfloat16), "tm", scatter_dimension=0, tiled=True
-        ).astype(jnp.float32),
-        lax.psum_scatter(
-            out_term.astype(jnp.bfloat16), "tm", scatter_dimension=1, tiled=True
-        ).astype(jnp.float32),
-        lax.psum_scatter(
-            table_term.astype(jnp.bfloat16), "tm", scatter_dimension=0, tiled=True
-        ).astype(jnp.float32),
-    )
+    proj_term = jnp.einsum("rk,rjn->jkn", attended, grad_split, preferred_element_type=jnp.float32)
+    table_rows = table_term.shape[0] // tm_count
+    pieces = (
+        proj_term.astype(jnp.bfloat16),
+        in_term.astype(jnp.bfloat16),
+        out_term.astype(jnp.bfloat16),
+        table_term.reshape(tm_count, table_rows, branch_width).astype(jnp.bfloat16),
+    )
+    merged = lax.psum_scatter(
+        jnp.concatenate(pieces, axis=1), "tm", scatter_dimension=0, tiled=True
+    )[0].astype(jnp.float32)
+    bounds = [0]
+    for piece in pieces:
+        bounds.append(bounds[-1] + piece.shape[1])
+    summed = tuple(merged[bounds[i] : bounds[i + 1]] for i in range(4))
     input_term = contract_cols(pre_grad, branch_in)
     input_sum = lax.psum_scatter(
         input_term.reshape(1, steps_here, tokens_here, model_width).astype(jnp.bfloat16),

time: 713 us -> 511 us (0.72)
  waiting for transfers between devices: 448 us -> 211 us
  local copies, waits for them, and re-layouts: 109 us -> 149 us
    unnamed x13 -> x6, waiting for transfers between devices: 237 us -> 0.07 us
    another operation x0 -> x3, local copies, waits for them, and re-layouts: none -> 31.2 us  [the longest x2 20.1 us: body(): grad_split = grad_rows.reshape(row_count, tm_count, col_block)]
    concatenate x0 -> x1, local copies, waits for them, and re-layouts: none -> 22.6 us  [body(): jnp.concatenate(pieces, axis=1)]
    unnamed x73 -> x84, local copies, waits for them, and re-layouts: 87.9 us -> 67.9 us
    slice x0 -> x4, local copies, waits for them, and re-layouts: none -> 10.8 us  [the longest x1 8.73 us: body(): grad_rows = full_both[1].reshape(row_count, model_width)]
    ppermute x4, waiting for transfers between devices: 1.11 us -> 9.45 us  [from_behind(): lax.ppermute(value, axis, [(source, source + steps) for source in range(f...]
    all_gather x2 -> x1, waiting for transfers between devices: 119 us -> 113 us  [body(): lax.all_gather(jnp.concatenate([hidden_in, out_grad], axis=0), 'tensor',...]
  transfers between devices with their start and end apart: 12 -> 8, of which waited for: 8 -> 3; matrix products, arithmetic and copies ran while one was open for 29% -> 40% of each run, Pallas kernels for 0% -> 0%
where the time goes in v1:
time: 511 us; the launch traced here: 501 us
  waiting for transfers between devices  211 us (41%)
  local copies, waits for them, and re-layouts  149 us (29%)
  matrix products  99.9 us (20%)
  other arithmetic  16.7 us (3%)
  between operations  15.2 us (3%)
  starting transfers between devices  9.06 us (2%)
    all_gather x1, waiting for transfers between devices, body(): lax.all_gather(jnp.concatenate([hidden_in, out_grad], axis=0), 'tensor',...  113 us
    reduce_scatter x1, waiting for transfers between devices, body(): lax.psum_scatter(jnp.concatenate(pieces, axis=1), 'tm', scatter_dimension...  88.6 us
    unnamed x84, local copies, waits for them, and re-layouts  67.9 us
    concatenate x1, local copies, waits for them, and re-layouts, body(): jnp.concatenate(pieces, axis=1)  22.6 us
    another operation x2, local copies, waits for them, and re-layouts, body(): grad_split = grad_rows.reshape(row_count, tm_count, col_block)  20.1 us
    dot_general x3, matrix products, contract_cols(): lax.dot_general(left, right, (((1,), (1,)), ((), ())), preferred_element_...  20.1 us
    dot_general x1, matrix products, body(): jnp.einsum('shqk,sqhe->skhe', score_grad, query_heads, preferred_element_...  14.9 us
    dot_general x1, matrix products, body(): jnp.einsum('shqk,skhe->sqhe', score_grad, key_heads, preferred_element_ty...  14 us
  transfers between devices with their start and end apart: 8, of which 3 were waited for; matrix products, arithmetic and copies ran while one was open for 40% of the time, Pallas kernels for 0%

profile of v1, /device:TPU:0, one launch (start us, length us, event | category | flops | bytes accessed | tf_op | source)
XLA Modules:
  0.0 501.3 jit_solution(12382191441929231244)
XLA Ops:
  11.0 113.4 %all-gather.2.cloned.1.call-done = bf16[2,2,256,5120]{3,2,1,0:T(8,128)(2,1)} async-done(((bf16[2,2,256,640]{3,2,1,0:T(8,128)(2,1)}), bf16[2,2,256,5120]{3,2,1,0:T(8,128)(2,1)}) %all-gather.2.cloned.1.call-update) | async-done | bytes 10485776 | tf_op jit(solution)/shard_map/all_gather | solution.py:65
  124.4 8.7 %fusion.81 = (bf16[1,2,256,5120]{3,2,1,0:T(8,128)(2,1)}, bf16[1,2,256,5120]{3,2,1,0:T(8,128)(2,1)}) fusion(bf16[2,2,256,5120]{3,2,1,0:T(8,128)(2,1)} %all-gather.2.cloned.1.call-done), kind=kLoop, calls=%fused_computation.105 | loop fusion | bytes 20971520 | tf_op jit(solution)/shard_map/slice | solution.py:69
  133.1 6.5 %fusion.49 = (bf16[2,4,64,320]{3,2,1,0:T(8,128)(2,1)}, f32[2,4,64,320]{3,2,1,0:T(8,128)}) fusion(f32[4,320]{1,0:T(4,128)S(1)} %fusion.65, bf16[2,4,64,5120]{3,2,1,0:T(8,128)(2,1)} %bitcast.132, bf16[5120,320]{0,1:T(8,128)(2,1)S(1)} %copy-done), kind=kOutput, calls=%fused_computation.58 | convolution fusion | flops 1679360000 | bytes 9507840 | tf_op jit(solution)/shard_map/dot_general | solution.py:121
  141.8 5.7 %fusion.44 = bf16[512,320]{0,1:T(8,128)(2,1)S(1)} fusion(bf16[512,5120]{1,0:T(8,128)(2,1)} %bitcast.130, bf16[320,5120]{1,0:T(8,128)(2,1)} %param.19, f32[512,320]{0,1:T(8,128)} %copy.145), kind=kOutput, calls=%fused_computation.48 | convolution fusion | flops 1680834560 | bytes 9502720 | tf_op jit(solution)/shard_map/dot_general | solution.py:38
  148.3 4.7 convolution_convert_fusion
  153.0 13.6 %copy.192 = bf16[1,2,256,5120]{2,1,0,3:T(2,128)(2,1)} copy(bf16[1,2,256,5120]{3,2,1,0:T(8,128)(2,1)} %bitcast.137) | data formatting | bytes 10485760
  166.6 5.7 %copy.200 = bf16[640,8,2,256]{3,1,2,0:T(8,128)(2,1)} copy(bf16[640,8,2,256]{3,2,1,0:T(2,128)(2,1)} %bitcast.135) | data formatting | bytes 10485760
  185.8 9.4 %collective-permute-done = bf16[2,256,640]{1,2,0:T(8,128)(2,1)} collective-permute-done((bf16[2,256,640]{1,2,0:T(8,128)(2,1)}, bf16[2,256,640]{1,2,0:T(8,128)(2,1)}, u32[]{:S(2)}, u32[]{:S(2)}) %collective-permute-start) | collective-permute-done | bytes 655392 | tf_op jit(solution)/shard_map/ppermute | solution.py:16
  213.9 4.9 add_convert_fusion
  218.8 13.6 %copy.190 = bf16[1,2,256,5120]{2,1,0,3:T(2,128)(2,1)} copy(bf16[1,2,256,5120]{3,2,1,0:T(8,128)(2,1)} %bitcast.129) | data formatting | bytes 10485760
  232.4 5.7 %copy.199 = bf16[640,8,2,256]{3,1,2,0:T(8,128)(2,1)} copy(bf16[640,8,2,256]{3,2,1,0:T(2,128)(2,1)} %bitcast.136) | data formatting | bytes 10485760
  238.2 11.5 %reshape.134 = bf16[512,16,320]{2,1,0:T(8,128)(2,1)} reshape(bf16[1,2,256,5120]{3,2,1,0:T(8,128)(2,1)} %get-tuple-element.54) | data formatting | bytes 10485760 | tf_op jit(solution)/shard_map/reshape;reshape;squeeze | solution.py:142
  249.7 11.0 %reshape.135 = bf16[512,16,320]{2,1,0:T(8,128)(2,1)} reshape(bf16[1,2,256,5120]{3,2,1,0:T(8,128)(2,1)} %get-tuple-element.55) | data formatting | bytes 10485760 | tf_op jit(solution)/shard_map/reshape;reshape;squeeze | solution.py:145
  260.9 8.6 %copy.186 = bf16[512,16,320]{0,2,1:T(8,128)(2,1)} copy(bf16[512,16,320]{2,1,0:T(8,128)(2,1)} %reshape.134) | data formatting | bytes 10485760 | tf_op jit(solution)/shard_map/reshape;reshape;squeeze | solution.py:142
  270.6 8.0 %convert_bitcast_fusion = bf16[16,320,320]{1,2,0:T(8,128)(2,1)} fusion(bf16[512,16,320]{0,2,1:T(8,128)(2,1)} %copy.186, bf16[512,320,1]{1,0,2:T(8,128)(2,1)} %bitcast.171), kind=kOutput, calls=%fused_computation.16 | convolution fusion | flops 1679360000 | bytes 8847360 | tf_op jit(solution)/shard_map/rk,rjn->jkn/dot_general | solution.py:149
  278.6 7.5 %fusion.23 = bf16[16,320,320]{1,2,0:T(8,128)(2,1)} fusion(bf16[512,16,320]{2,1,0:T(8,128)(2,1)} %reshape.135, bf16[512,320]{0,1:T(8,128)(2,1)S(1)} %copy-done.18), kind=kOutput, calls=%fused_computation.25 | convolution fusion | flops 1679360000 | bytes 8847360 | tf_op jit(solution)/shard_map/rjk,rn->jkn/dot_general | solution.py:143
  286.2 6.3 %fusion.9 = bf16[16,640,320]{1,2,0:T(8,128)(2,1)} fusion(bf16[512,16,320]{0,2,1:T(8,128)(2,1)S(1)} %bitcast.141, bf16[512,640]{0,1:T(8,128)(2,1)S(1)} %bitcast.152), kind=kOutput, calls=%fused_computation.15 | convolution fusion | flops 3358720000 | bytes 12451840 | tf_op jit(solution)/shard_map/rk,rjn->jkn/dot_general | solution.py:157
  292.5 22.6 %concatenate.27 = bf16[16,1288,320]{1,2,0:T(8,128)(2,1)} concatenate(bf16[16,640,320]{1,2,0:T(8,128)(2,1)} %fusion.9, bf16[16,320,320]{1,2,0:T(8,128)(2,1)} %fusion.23, bf16[16,320,320]{1,2,0:T(8,128)(2,1)} %convert_bitcast_fusion, bf16[16,8,320]{1,2,0:T(8,128)(2,1)S(1)} %copy.169), dimensions={1} | concatenate | bytes 26378240 | tf_op jit(solution)/shard_map/concatenate | solution.py:166
  315.1 9.6 %convolution_convert_fusion.2 = bf16[512,640]{1,0:T(8,128)(2,1)} fusion(bf16[512,5120]{1,0:T(8,128)(2,1)} %bitcast.131, bf16[640,5120]{1,0:T(8,128)(2,1)} %param.17), kind=kOutput, calls=%fused_computation.36 | convolution fusion | flops 3355770880 | bytes 12451840 | tf_op jit(solution)/shard_map/dot_general | solution.py:38
  327.9 5.0 fusion.26
  335.9 4.4 fusion.31
  340.4 14.9 %fusion.13 = f32[2,5,768,128]{2,3,1,0:T(8,128)} fusion(bf16[2,256,5,128]{1,3,2,0:T(8,128)(2,1)S(1)} %bitcast.148, f32[2,5,256,768]{2,3,1,0:T(8,128)} %fusion.31, f32[2,5,256,768]{2,3,1,0:T(8,128)} %copy-done.27, f32[2,5,256]{2,1,0:T(8,128)S(1)} %get-tuple-element.62), kind=kOutput, calls=%fused_computation.17 | convolution fusion | flops 517082368 | bytes 20326400 | tf_op jit(solution)/shard_map/shqk,sqhe->skhe/dot_general | solution.py:195
  365.4 14.0 %fusion.35 = bf16[2,5,128,256]{3,2,1,0:T(8,128)(2,1)} fusion(f32[2,5,256,768]{2,3,1,0:T(8,128)} %fusion.31, bf16[2,256,5,128]{3,1,2,0:T(8,128)(2,1)S(1)} %copy.140, bf16[2,256,5,128]{3,1,2,0:T(8,128)(2,1)S(1)} %copy-done.9, bf16[2,256,5,128]{3,1,2,0:T(8,128)(2,1)S(1)} %copy-done.11, f32[2,5,256,768]{2,3,1,0:T(8,128)} %copy-done.27, ...), kind=kOutput, calls=%fused_computation.35 | convolution fusion | flops 523308288 | bytes 18360320 | tf_op jit(solution)/shard_map/shqk,skhe->sqhe/dot_general | solution.py:191
  397.8 88.6 %reduce-scatter.8.cloned.1.call-done = bf16[1,1288,320]{1,2,0:T(8,128)(2,1)} async-done(((bf16[16,1288,320]{1,2,0:T(8,128)(2,1)}), bf16[1,1288,320]{1,2,0:T(8,128)(2,1)}) %reduce-scatter.8.cloned.1.call-update) | async-done | bytes 824336 | tf_op jit(solution)/shard_map/reduce_scatter | solution.py:165
  (139 shorter events, 81.9 us)
Async XLA Ops:
  7.2 125.9 %copy-start = (bf16[5120,320]{0,1:T(8,128)(2,1)S(1)}, bf16[5120,320]{0,1:T(8,128)(2,1)}, u32[]{:S(2)}) copy-start(bf16[5120,320]{0,1:T(8,128)(2,1)} %param.18) | copy-start | bytes 9830404
  7.2 117.2 %all-gather.2.cloned.1.call-start = ((), (), s32[]{:S(2)}) async-start(), calls=%async_computation.3 | async-start | bytes 11796480 | tf_op jit(solution)/shard_map/all_gather | solution.py:65
  9.9 376.8 %reduce-scatter.12.cloned.1.call-start = ((), (), s32[]{:S(2)}) async-start(), calls=%async_computation.6 | async-start | bytes 5898240
  172.3 8.5 %copy-start.24 = (bf16[1,2,256,640]{3,2,1,0:T(8,128)(2,1)S(1)}, bf16[1,2,256,640]{3,2,1,0:T(8,128)(2,1)}, u32[]{:S(2)}) copy-start(bf16[1,2,256,640]{3,2,1,0:T(8,128)(2,1)} %param.15) | copy-start | bytes 1966084
  172.3 8.8 %copy-start.25 = (bf16[1,2,256,640]{3,2,1,0:T(8,128)(2,1)S(1)}, bf16[1,2,256,640]{3,2,1,0:T(8,128)(2,1)}, u32[]{:S(2)}) copy-start(bf16[1,2,256,640]{3,2,1,0:T(8,128)(2,1)} %param.13) | copy-start | bytes 1966084
  172.3 218.3 %reduce-scatter.10.cloned.1.call-start = ((), (), s32[]{:S(2)}) async-start(), calls=%async_computation.5 | async-start | bytes 5898240
  174.5 9.2 %collective-permute-start.1 = (bf16[2,256,640]{1,2,0:T(8,128)(2,1)}, bf16[2,256,640]{1,2,0:T(8,128)(2,1)}, u32[]{:S(2)}, u32[]{:S(2)}) collective-permute-start(bf16[2,256,640]{1,2,0:T(8,128)(2,1)} %bitcast), channel_id=1, source_target_pairs={{0,8},{8,16},{16,24},{24,32},{32,40},{40,48},{48,56},{56,64},{64,7... | collective-permute-start | bytes 1966088 | tf_op jit(solution)/shard_map/ppermute | solution.py:16
  176.9 18.3 %collective-permute-start = (bf16[2,256,640]{1,2,0:T(8,128)(2,1)}, bf16[2,256,640]{1,2,0:T(8,128)(2,1)}, u32[]{:S(2)}, u32[]{:S(2)}) collective-permute-start(bf16[2,256,640]{1,2,0:T(8,128)(2,1)} %bitcast), channel_id=1, source_target_pairs={{0,16},{8,24},{16,32},{24,40},{32,48},{40,56},{48,64},{56,72},{64,... | collective-permute-start | bytes 1966088 | tf_op jit(solution)/shard_map/ppermute | solution.py:16
  238.2 248.2 %reduce-scatter.8.cloned.1.call-start = ((), (), s32[]{:S(2)}) async-start(), calls=%async_computation.4 | async-start | bytes 15319040 | tf_op jit(solution)/shard_map/reduce_scatter | solution.py:165
  249.7 11.0 %copy-start.17 = (bf16[512,320]{0,1:T(8,128)(2,1)S(1)}, bf16[512,320]{0,1:T(8,128)(2,1)}, u32[]{:S(2)}) copy-start(bf16[512,320]{0,1:T(8,128)(2,1)} %copy-done.16) | copy-start | bytes 983044
  260.9 8.7 %copy-start.26 = (s32[1,4]{1,0:T(1,128)S(1)}, s32[1,4]{1,0:T(1,128)}, u32[]{:S(2)}) copy-start(s32[1,4]{1,0:T(1,128)} %param.21) | copy-start | bytes 52
  270.6 8.1 %copy-start.18 = (bf16[512,320]{0,1:T(8,128)(2,1)S(1)}, bf16[512,320]{0,1:T(8,128)(2,1)}, u32[]{:S(2)}) copy-start(bf16[512,320]{0,1:T(8,128)(2,1)} %copy-done.16) | copy-start | bytes 983044
  270.6 15.6 %slice-start.2 = ((s8[5242880]{0:T(1024)(128)(4,1)}), s8[4194304]{0:T(1024)(128)(4,1)S(1)}, s32[]{:S(2)}) async-start(s8[5242880]{0:T(1024)(128)(4,1)} %bitcast.140), calls=%async_computation.9 | async-start | bytes 8388608
  278.6 7.5 %copy-start.6 = (bf16[80,8,2,256]{3,1,2,0:T(8,128)(2,1)S(1)}, bf16[80,8,2,256]{3,1,2,0:T(8,128)(2,1)}, u32[]{:S(2)}) copy-start(bf16[80,8,2,256]{3,1,2,0:T(8,128)(2,1)} %copy-done.5) | copy-start | bytes 1966084
  327.9 8.0 %copy-start.7 = (bf16[2,256,5,128]{1,3,2,0:T(8,128)(2,1)S(1)}, bf16[2,256,5,128]{1,3,2,0:T(8,128)(2,1)}, u32[]{:S(2)}) copy-start(bf16[2,256,5,128]{1,3,2,0:T(8,128)(2,1)} %copy.161) | copy-start | bytes 1966084
  327.9 8.0 %copy-start.13 = (bf16[2,256,5,128]{1,3,2,0:T(8,128)(2,1)S(1)}, bf16[2,256,5,128]{1,3,2,0:T(8,128)(2,1)}, u32[]{:S(2)}) copy-start(bf16[2,256,5,128]{1,3,2,0:T(8,128)(2,1)} %copy-done.12) | copy-start | bytes 1966084
  327.9 8.0 %copy-start.15 = (bf16[2,256,5,128]{1,3,2,0:T(8,128)(2,1)S(1)}, bf16[2,256,5,128]{1,3,2,0:T(8,128)(2,1)}, u32[]{:S(2)}) copy-start(bf16[2,256,5,128]{1,3,2,0:T(8,128)(2,1)} %copy-done.14) | copy-start | bytes 1966084
  340.4 17.5 %copy-start.20 = (bf16[256,640]{0,1:T(8,128)(2,1)S(1)}, bf16[256,640]{0,1:T(8,128)(2,1)}, u32[]{:S(2)}) copy-start(bf16[256,640]{0,1:T(8,128)(2,1)} %get-tuple-element.53) | copy-start | bytes 983044
  340.4 19.6 %copy-start.19 = (bf16[256,640]{0,1:T(8,128)(2,1)S(1)}, bf16[256,640]{0,1:T(8,128)(2,1)}, u32[]{:S(2)}) copy-start(bf16[256,640]{0,1:T(8,128)(2,1)} %get-tuple-element.52) | copy-start | bytes 983044
  355.3 10.2 %copy-start.9 = (bf16[2,256,5,128]{3,1,2,0:T(8,128)(2,1)S(1)}, bf16[2,256,5,128]{3,1,2,0:T(8,128)(2,1)}, u32[]{:S(2)}) copy-start(bf16[2,256,5,128]{3,1,2,0:T(8,128)(2,1)} %copy-done.8) | copy-start | bytes 1966084
  355.3 10.2 %copy-start.11 = (bf16[2,256,5,128]{3,1,2,0:T(8,128)(2,1)S(1)}, bf16[2,256,5,128]{3,1,2,0:T(8,128)(2,1)}, u32[]{:S(2)}) copy-start(bf16[2,256,5,128]{3,1,2,0:T(8,128)(2,1)} %copy-done.10) | copy-start | bytes 1966084
  358.7 25.0 %collective-permute-start.3 = (bf16[2,256,640]{1,2,0:T(8,128)(2,1)}, bf16[2,256,640]{1,2,0:T(8,128)(2,1)}, u32[]{:S(2)}, u32[]{:S(2)}) collective-permute-start(bf16[2,256,640]{1,2,0:T(8,128)(2,1)} %pad_maximum_fusion.14), channel_id=1, source_target_pairs={{16,0},{24,8},{32,16},{40,24},{48,32},{56,40},{64,48},{72,56},{80,... | collective-permute-start | bytes 1966088 | tf_op jit(solution)/shard_map/ppermute | solution.py:16
  360.9 22.8 %collective-permute-start.2 = (bf16[2,256,640]{1,2,0:T(8,128)(2,1)}, bf16[2,256,640]{1,2,0:T(8,128)(2,1)}, u32[]{:S(2)}, u32[]{:S(2)}) collective-permute-start(bf16[2,256,640]{1,2,0:T(8,128)(2,1)} %pad_maximum_fusion.13), channel_id=1, source_target_pairs={{8,0},{16,8},{24,16},{32,24},{40,32},{48,40},{56,48},{64,56},{72,6... | collective-permute-start | bytes 1966088 | tf_op jit(solution)/shard_map/ppermute | solution.py:16
  394.6 99.9 %copy-start.1 = (bf16[5120,320]{0,1:T(8,128)(2,1)S(1)}, bf16[5120,320]{0,1:T(8,128)(2,1)}, u32[]{:S(2)}) copy-start(bf16[5120,320]{0,1:T(8,128)(2,1)} %param.18) | copy-start | bytes 9830404
  (16 other events, 58.5 us)
Sparse Core Ops, SparseCore 0:
  10.2 114.0 all-gather.1
  172.4 81.6 reduce-scatter.11
  256.5 70.4 reduce-scatter.9
  331.4 154.9 reduce-scatter.7

commit v2 on v1

--- a/solution.py
+++ b/solution.py
@@ -38,6 +38,15 @@
     return lax.dot_general(
         left, right, (((1,), (1,)), ((), ())), preferred_element_type=jnp.float32
     )
+
+
+def sum_over_groups(partial, steps_here, tokens_here):
+    count = lax.axis_size("tensor")
+    rows, width = partial.shape
+    blocks = partial.reshape(rows, count, width // count)
+    received = lax.all_to_all(blocks, "tensor", 1, 1, tiled=True)
+    total = jnp.sum(received.astype(jnp.float32), axis=1)
+    return total.reshape(1, steps_here, tokens_here, width // count)
 
 
 def body(
@@ -128,12 +137,7 @@
     partial_value = jnp.dot(attended, out_proj, preferred_element_type=jnp.float32) + jnp.dot(
         branch_act, branch_out, preferred_element_type=jnp.float32
     )
-    layer_sum = lax.psum_scatter(
-        partial_value.reshape(1, steps_here, tokens_here, model_width).astype(jnp.bfloat16),
-        "tensor",
-        scatter_dimension=3,
-        tiled=True,
-    ).astype(jnp.float32)
+    layer_sum = sum_over_groups(partial_value.astype(jnp.bfloat16), steps_here, tokens_here)
     layer_out = (hidden_in.astype(jnp.float32) + layer_sum).astype(jnp.bfloat16)
     attended_grad = contract_cols(grad_rows, out_proj).astype(jnp.bfloat16)
     pre_grad = (contract_cols(grad_rows, branch_out) * gelu_slope(pre_act)).astype(jnp.bfloat16)
@@ -170,12 +174,7 @@
         bounds.append(bounds[-1] + piece.shape[1])
     summed = tuple(merged[bounds[i] : bounds[i + 1]] for i in range(4))
     input_term = contract_cols(pre_grad, branch_in)
-    input_sum = lax.psum_scatter(
-        input_term.reshape(1, steps_here, tokens_here, model_width).astype(jnp.bfloat16),
-        "tensor",
-        scatter_dimension=3,
-        tiled=True,
-    ).astype(jnp.float32)
+    input_sum = sum_over_groups(input_term.astype(jnp.bfloat16), steps_here, tokens_here)
     input_grad = (out_grad.astype(jnp.float32) + input_sum).astype(jnp.bfloat16)
     weight_grads = (summed, input_grad)
     grad_heads = attended_grad.reshape(steps_here, tokens_here, heads_here, HD)

time: 511 us -> 478 us (0.935)
  local copies, waits for them, and re-layouts: 149 us -> 114 us
  starting transfers between devices: 9.06 us -> 36.2 us
  waiting for transfers between devices: 211 us -> 185 us
  other arithmetic: 16.7 us -> 23 us
    all_to_all x0 -> x2, waiting for transfers between devices: none -> 50.3 us  [sum_over_groups(): received = lax.all_to_all(blocks, 'tensor', 1, 1, tiled=True)]
    reduce_scatter x1, waiting for transfers between devices: 88.6 us -> 41.8 us  [body(): lax.psum_scatter(jnp.concatenate(pieces, axis=1), 'tm', scatter_dimension...]
    unnamed x84 -> x62, local copies, waits for them, and re-layouts: 67.9 us -> 23.3 us
    all_to_all x0 -> x2, starting transfers between devices: none -> 27.2 us  [sum_over_groups(): received = lax.all_to_all(blocks, 'tensor', 1, 1, tiled=True)]
    all_gather x1, waiting for transfers between devices: 113 us -> 91.8 us  [body(): lax.all_gather(jnp.concatenate([hidden_in, out_grad], axis=0), 'tensor',...]
    ppermute x4, waiting for transfers between devices: 9.45 us -> 1.14 us  [from_behind(): lax.ppermute(value, axis, [(source, source + steps) for source in range(f...]
    reduce_sum x0 -> x2, other arithmetic: none -> 6.69 us  [sum_over_groups(): total = jnp.sum(received.astype(jnp.float32), axis=1)]
    reshape x0 -> x2, local copies, waits for them, and re-layouts: none -> 5.68 us  [sum_over_groups(): blocks = partial.reshape(rows, count, width // count)]
  transfers between devices with their start and end apart: 8 -> 8, of which waited for: 3 -> 5; matrix products, arithmetic and copies ran while one was open for 40% -> 25% of each run, Pallas kernels for 0% -> 0%
where the time goes in v2:
time: 478 us; the launch traced here: 471 us
  waiting for transfers between devices  185 us (39%)
  local copies, waits for them, and re-layouts  114 us (24%)
  matrix products  97 us (20%)
  starting transfers between devices  36.2 us (8%)
  other arithmetic  23 us (5%)
  between operations  15.4 us (3%)
    all_gather x1, waiting for transfers between devices, body(): lax.all_gather(jnp.concatenate([hidden_in, out_grad], axis=0), 'tensor',...  91.8 us
    all_to_all x2, waiting for transfers between devices, sum_over_groups(): received = lax.all_to_all(blocks, 'tensor', 1, 1, tiled=True)  50.3 us
    reduce_scatter x1, waiting for transfers between devices, body(): lax.psum_scatter(jnp.concatenate(pieces, axis=1), 'tm', scatter_dimension...  41.8 us
    all_to_all x2, starting transfers between devices, sum_over_groups(): received = lax.all_to_all(blocks, 'tensor', 1, 1, tiled=True)  27.2 us
    unnamed x62, local copies, waits for them, and re-layouts  23.3 us
    concatenate x1, local copies, waits for them, and re-layouts, body(): jnp.concatenate(pieces, axis=1)  21.9 us
    another operation x2, local copies, waits for them, and re-layouts, body(): grad_split = grad_rows.reshape(row_count, tm_count, col_block)  19.9 us
    dot_general x3, matrix products, contract_cols(): lax.dot_general(left, right, (((1,), (1,)), ((), ())), preferred_element_...  19.3 us
  transfers between devices with their start and end apart: 8, of which 5 were waited for; matrix products, arithmetic and copies ran while one was open for 25% of the time, Pallas kernels for 0%

profile of v2, /device:TPU:0, one launch (start us, length us, event | category | flops | bytes accessed | tf_op | source)
XLA Modules:
  0.0 470.7 jit_solution(6993501877709725878)
XLA Ops:
  14.3 4.2 collective-permute-start
  50.5 91.8 %all-gather.2.cloned.1.call-done = bf16[2,2,256,5120]{3,2,1,0:T(8,128)(2,1)} async-done(((bf16[2,2,256,640]{3,2,1,0:T(8,128)(2,1)}), bf16[2,2,256,5120]{3,2,1,0:T(8,128)(2,1)}) %all-gather.2.cloned.1.call-update) | async-done | bytes 10485776 | tf_op jit(solution)/shard_map/all_gather | solution.py:74
  142.3 8.7 %fusion.81 = (bf16[1,2,256,5120]{3,2,1,0:T(8,128)(2,1)}, bf16[1,2,256,5120]{3,2,1,0:T(8,128)(2,1)}) fusion(bf16[2,2,256,5120]{3,2,1,0:T(8,128)(2,1)} %all-gather.2.cloned.1.call-done), kind=kLoop, calls=%fused_computation.109 | loop fusion | bytes 20971520 | tf_op jit(solution)/shard_map/slice | solution.py:78
  151.0 11.0 %reshape.123 = bf16[512,16,320]{2,1,0:T(8,128)(2,1)} reshape(bf16[1,2,256,5120]{3,2,1,0:T(8,128)(2,1)} %get-tuple-element.55) | data formatting | bytes 10485760 | tf_op jit(solution)/shard_map/reshape;reshape;squeeze | solution.py:149
  162.0 6.5 %fusion.49 = (bf16[2,4,64,320]{3,2,1,0:T(8,128)(2,1)}, f32[2,4,64,320]{3,2,1,0:T(8,128)}) fusion(f32[4,320]{1,0:T(4,128)S(1)} %fusion.65, bf16[2,4,64,5120]{3,2,1,0:T(8,128)(2,1)} %bitcast.130, bf16[5120,320]{0,1:T(8,128)(2,1)S(1)} %copy-done), kind=kOutput, calls=%fused_computation.62 | convolution fusion | flops 1679360000 | bytes 9507840 | tf_op jit(solution)/shard_map/dot_general | solution.py:130
  170.7 11.0 %reshape.122 = bf16[512,16,320]{2,1,0:T(8,128)(2,1)} reshape(bf16[1,2,256,5120]{3,2,1,0:T(8,128)(2,1)} %get-tuple-element.54) | data formatting | bytes 10485760 | tf_op jit(solution)/shard_map/reshape;reshape;squeeze | solution.py:146
  181.7 6.4 %fusion.44 = bf16[512,320]{0,1:T(8,128)(2,1)} fusion(bf16[512,5120]{1,0:T(8,128)(2,1)} %bitcast.128, bf16[320,5120]{1,0:T(8,128)(2,1)} %param.19, f32[512,320]{0,1:T(8,128)} %copy.147), kind=kOutput, calls=%fused_computation.52 | convolution fusion | flops 1680834560 | bytes 9502720 | tf_op jit(solution)/shard_map/dot_general | solution.py:38
  193.2 8.9 %copy.190 = bf16[512,16,320]{0,2,1:T(8,128)(2,1)} copy(bf16[512,16,320]{2,1,0:T(8,128)(2,1)} %reshape.122) | data formatting | bytes 10485760 | tf_op jit(solution)/shard_map/reshape;reshape;squeeze | solution.py:146
  202.1 7.7 %fusion.23 = bf16[16,320,320]{1,2,0:T(8,128)(2,1)} fusion(bf16[512,16,320]{2,1,0:T(8,128)(2,1)} %reshape.123, bf16[512,320]{0,1:T(8,128)(2,1)} %fusion.44), kind=kOutput, calls=%fused_computation.29 | convolution fusion | flops 1679360000 | bytes 8847360 | tf_op jit(solution)/shard_map/rjk,rn->jkn/dot_general | solution.py:147
  209.8 4.5 convert_bitcast_fusion
  214.3 6.3 %fusion.9 = bf16[16,640,320]{1,2,0:T(8,128)(2,1)} fusion(bf16[512,16,320]{0,2,1:T(8,128)(2,1)S(1)} %copy-done.2, bf16[512,640]{0,1:T(8,128)(2,1)S(1)} %bitcast.145), kind=kOutput, calls=%fused_computation.17 | convolution fusion | flops 3358720000 | bytes 12451840 | tf_op jit(solution)/shard_map/rk,rjn->jkn/dot_general | solution.py:161
  220.5 21.9 %concatenate.27 = bf16[16,1288,320]{1,2,0:T(8,128)(2,1)} concatenate(bf16[16,640,320]{1,2,0:T(8,128)(2,1)} %fusion.9, bf16[16,320,320]{1,2,0:T(8,128)(2,1)} %fusion.23, bf16[16,320,320]{1,2,0:T(8,128)(2,1)} %convert_bitcast_fusion, bf16[16,8,320]{1,2,0:T(8,128)(2,1)} %copy.173), dimensions={1} | concatenate | bytes 26378240 | tf_op jit(solution)/shard_map/concatenate | solution.py:170
  242.5 4.1 convolution_convert_fusion
  249.5 4.9 %all-to-all-start.1 = ((bf16[512,8,640]{2,0,1:T(8,128)(2,1)}), bf16[512,8,640]{2,0,1:T(8,128)(2,1)}, u32[]{:S(2)}, u32[]{:S(2)}) async-start(bf16[512,8,640]{2,0,1:T(8,128)(2,1)} %bitcast.132), calls=%async_computation.1 | async-start | bytes 10485760 | tf_op jit(solution)/shard_map/all_to_all | solution.py:47
  254.4 7.1 %fusion.85 = f32[512,5120]{1,0:T(8,128)S(1)} fusion(bf16[512,640]{0,1:T(8,128)(2,1)S(1)} %bitcast.146, bf16[640,5120]{1,0:T(8,128)(2,1)} %param.17), kind=kOutput, calls=%fused_computation.113 | convolution fusion | flops 3355443200 | bytes 17694720 | tf_op jit(solution)/shard_map/dot_general | solution.py:137
  267.7 47.4 %all-to-all-done.1 = bf16[512,8,640]{2,0,1:T(8,128)(2,1)} async-done(((bf16[512,8,640]{2,0,1:T(8,128)(2,1)}), bf16[512,8,640]{2,0,1:T(8,128)(2,1)}, u32[]{:S(2)}, u32[]{:S(2)}) %all-to-all-start.1) | async-done | bytes 5242912 | tf_op jit(solution)/shard_map/all_to_all | solution.py:47
  315.1 22.3 %all-to-all-start = ((bf16[512,8,640]{2,0,1:T(8,128)(2,1)}), bf16[512,8,640]{2,0,1:T(8,128)(2,1)}, u32[]{:S(2)}, u32[]{:S(2)}) async-start(bf16[512,8,640]{2,0,1:T(8,128)(2,1)} %bitcast.131), calls=%async_computation | async-start | bytes 10485760 | tf_op jit(solution)/shard_map/all_to_all | solution.py:47
  337.5 8.8 %convolution_convert_fusion.2 = bf16[512,640]{1,0:T(8,128)(2,1)S(1)} fusion(bf16[512,5120]{1,0:T(8,128)(2,1)} %bitcast.129, bf16[640,5120]{1,0:T(8,128)(2,1)} %param.17), kind=kOutput, calls=%fused_computation.40 | convolution fusion | flops 3355770880 | bytes 12451840 | tf_op jit(solution)/shard_map/dot_general | solution.py:38
  347.6 5.5 %fusion.31 = f32[2,5,256,768]{2,3,1,0:T(8,128)} fusion(bf16[2,256,5,128]{1,3,2,0:T(8,128)(2,1)S(1)} %copy.165, bf16[2,256,5,128]{1,3,2,0:T(8,128)(2,1)S(1)} %bitcast.144, bf16[2,256,5,128]{1,3,2,0:T(8,128)(2,1)S(1)} %copy-done.16, bf16[2,256,5,128]{1,3,2,0:T(8,128)(2,1)} %copy-done.17), kind=kOutput, calls=%fused_computation.37 | convolution fusion | flops 509214720 | bytes 10485760 | tf_op jit(solution)/shard_map/sqhe,skhe->shqk/dot_general | solution.py:184
  353.1 14.1 %fusion.13 = f32[2,5,768,128]{2,3,1,0:T(8,128)} fusion(bf16[2,256,5,128]{1,3,2,0:T(8,128)(2,1)S(1)} %bitcast.142, f32[2,5,256,768]{2,3,1,0:T(8,128)} %fusion.31, f32[2,5,256,768]{2,3,1,0:T(8,128)} %copy-done.24, f32[2,5,256]{2,1,0:T(8,128)S(1)} %get-tuple-element.62), kind=kOutput, calls=%fused_computation.21 | convolution fusion | flops 517082368 | bytes 20326400 | tf_op jit(solution)/shard_map/shqk,sqhe->skhe/dot_general | solution.py:194
  369.3 4.6 fusion.26
  379.9 13.8 %fusion.35 = bf16[2,5,128,256]{3,2,1,0:T(8,128)(2,1)} fusion(f32[2,5,256,768]{2,3,1,0:T(8,128)} %fusion.31, bf16[2,256,5,128]{3,1,2,0:T(8,128)(2,1)S(1)} %copy-done.5, bf16[2,256,5,128]{3,1,2,0:T(8,128)(2,1)S(1)} %copy-done.12, bf16[2,256,5,128]{3,1,2,0:T(8,128)(2,1)S(1)} %copy-done.14, f32[2,5,256,768]{2,3,1,0:T(8,128)} %copy-done.24, ...), kind=kOutput, calls=%fused_computation.39 | convolution fusion | flops 523308288 | bytes 18360320 | tf_op jit(solution)/shard_map/shqk,skhe->sqhe/dot_general | solution.py:190
  408.2 3.4 convert_reduce_fusion.1
  413.8 41.8 %reduce-scatter.2.cloned.1.call-done = bf16[1,1288,320]{1,2,0:T(8,128)(2,1)} async-done(((bf16[16,1288,320]{1,2,0:T(8,128)(2,1)}), bf16[1,1288,320]{1,2,0:T(8,128)(2,1)}) %reduce-scatter.2.cloned.1.call-update) | async-done | bytes 824336 | tf_op jit(solution)/shard_map/reduce_scatter | solution.py:169
  (118 shorter events, 88.5 us)
Async XLA Ops:
  7.2 154.8 %copy-start = (bf16[5120,320]{0,1:T(8,128)(2,1)S(1)}, bf16[5120,320]{0,1:T(8,128)(2,1)}, u32[]{:S(2)}) copy-start(bf16[5120,320]{0,1:T(8,128)(2,1)} %param.18) | copy-start | bytes 9830404
  7.2 20.7 %copy-start.21 = (s32[1,4]{1,0:T(1,128)S(1)}, s32[1,4]{1,0:T(1,128)}, u32[]{:S(2)}) copy-start(s32[1,4]{1,0:T(1,128)} %param.21) | copy-start | bytes 52
  7.2 20.7 %copy-start.22 = (bf16[128,320]{0,1:T(8,128)(2,1)S(1)}, bf16[128,320]{0,1:T(8,128)(2,1)}, u32[]{:S(2)}) copy-start(bf16[128,320]{0,1:T(8,128)(2,1)} %param.20) | copy-start | bytes 245764
  7.2 135.1 %all-gather.2.cloned.1.call-start = ((), (), s32[]{:S(2)}) async-start(), calls=%async_computation.3 | async-start | bytes 11796480 | tf_op jit(solution)/shard_map/all_gather | solution.py:74
  9.9 445.7 %reduce-scatter.2.cloned.1.call-start = ((), (), s32[]{:S(2)}) async-start(), calls=%async_computation.4 | async-start | bytes 15319040 | tf_op jit(solution)/shard_map/reduce_scatter | solution.py:169
  12.1 16.0 %collective-permute-start.1 = (bf16[2,256,640]{1,2,0:T(8,128)(2,1)}, bf16[2,256,640]{1,2,0:T(8,128)(2,1)}, u32[]{:S(2)}, u32[]{:S(2)}) collective-permute-start(bf16[2,256,640]{1,2,0:T(8,128)(2,1)} %bitcast.160), channel_id=1, source_target_pairs={{0,8},{8,16},{16,24},{24,32},{32,40},{40,48},{48,56},{56,64},{64,7... | collective-permute-start | bytes 1966088 | tf_op jit(solution)/shard_map/ppermute | solution.py:16
  14.3 18.8 %collective-permute-start = (bf16[2,256,640]{1,2,0:T(8,128)(2,1)}, bf16[2,256,640]{1,2,0:T(8,128)(2,1)}, u32[]{:S(2)}, u32[]{:S(2)}) collective-permute-start(bf16[2,256,640]{1,2,0:T(8,128)(2,1)} %bitcast.161), channel_id=1, source_target_pairs={{0,16},{8,24},{16,32},{24,40},{32,48},{40,56},{48,64},{56,72},{64,... | collective-permute-start | bytes 1966088 | tf_op jit(solution)/shard_map/ppermute | solution.py:16
  202.1 7.7 %copy-start.2 = (bf16[512,16,320]{0,2,1:T(8,128)(2,1)S(1)}, bf16[512,16,320]{0,2,1:T(8,128)(2,1)}, u32[]{:S(2)}) copy-start(bf16[512,16,320]{0,2,1:T(8,128)(2,1)} %copy.190) | copy-start | bytes 15728644
  202.1 7.7 %copy-start.23 = (bf16[2,4,64,320]{3,2,1,0:T(8,128)(2,1)S(1)}, bf16[2,4,64,320]{3,2,1,0:T(8,128)(2,1)}, u32[]{:S(2)}) copy-start(bf16[2,4,64,320]{3,2,1,0:T(8,128)(2,1)} %get-tuple-element.64) | copy-start | bytes 983044
  249.5 4.9 %copy-start.10 = (bf16[80,8,2,256]{3,1,2,0:T(8,128)(2,1)S(1)}, bf16[80,8,2,256]{3,1,2,0:T(8,128)(2,1)}, u32[]{:S(2)}) copy-start(bf16[80,8,2,256]{3,1,2,0:T(8,128)(2,1)} %copy.200) | copy-start | bytes 1966084
  249.5 65.7 %all-to-all-start.1 = ((bf16[512,8,640]{2,0,1:T(8,128)(2,1)}), bf16[512,8,640]{2,0,1:T(8,128)(2,1)}, u32[]{:S(2)}, u32[]{:S(2)}) async-start(bf16[512,8,640]{2,0,1:T(8,128)(2,1)} %bitcast.132), calls=%async_computation.1 | async-start | bytes 10485760 | tf_op jit(solution)/shard_map/all_to_all | solution.py:47
  254.4 7.1 %copy-start.3 = (f32[512,320]{0,1:T(8,128)S(1)}, f32[512,320]{0,1:T(8,128)}, u32[]{:S(2)}) copy-start(f32[512,320]{0,1:T(8,128)} %copy.147) | copy-start | bytes 1966084
  254.4 7.1 %copy-start.4 = (bf16[320,5120]{1,0:T(8,128)(2,1)S(1)}, bf16[320,5120]{1,0:T(8,128)(2,1)}, u32[]{:S(2)}) copy-start(bf16[320,5120]{1,0:T(8,128)(2,1)} %param.19) | copy-start | bytes 9830404
  315.1 93.1 %all-to-all-start = ((bf16[512,8,640]{2,0,1:T(8,128)(2,1)}), bf16[512,8,640]{2,0,1:T(8,128)(2,1)}, u32[]{:S(2)}, u32[]{:S(2)}) async-start(bf16[512,8,640]{2,0,1:T(8,128)(2,1)} %bitcast.131), calls=%async_computation | async-start | bytes 10485760 | tf_op jit(solution)/shard_map/all_to_all | solution.py:47
  337.4 10.1 %copy-start.8 = (bf16[1,2,256,640]{2,3,1,0:T(8,128)(2,1)S(1)}, bf16[1,2,256,640]{2,3,1,0:T(8,128)(2,1)}, u32[]{:S(2)}) copy-start(bf16[1,2,256,640]{2,3,1,0:T(8,128)(2,1)} %copy.138) | copy-start | bytes 1966084
  337.5 10.1 %copy-start.16 = (bf16[2,256,5,128]{1,3,2,0:T(8,128)(2,1)S(1)}, bf16[2,256,5,128]{1,3,2,0:T(8,128)(2,1)}, u32[]{:S(2)}) copy-start(bf16[2,256,5,128]{1,3,2,0:T(8,128)(2,1)} %copy-done.15) | copy-start | bytes 1966084
  347.6 5.6 %copy-start.6 = (bf16[1,2,256,640]{2,3,1,0:T(8,128)(2,1)S(1)}, bf16[1,2,256,640]{2,3,1,0:T(8,128)(2,1)}, u32[]{:S(2)}) copy-start(bf16[1,2,256,640]{2,3,1,0:T(8,128)(2,1)} %copy.143) | copy-start | bytes 1966084
  373.9 6.0 %copy-start.5 = (bf16[2,256,5,128]{3,1,2,0:T(8,128)(2,1)S(1)}, bf16[2,256,5,128]{3,1,2,0:T(8,128)(2,1)}, u32[]{:S(2)}) copy-start(bf16[2,256,5,128]{3,1,2,0:T(8,128)(2,1)} %copy.142) | copy-start | bytes 1966084
  373.9 6.0 %copy-start.12 = (bf16[2,256,5,128]{3,1,2,0:T(8,128)(2,1)S(1)}, bf16[2,256,5,128]{3,1,2,0:T(8,128)(2,1)}, u32[]{:S(2)}) copy-start(bf16[2,256,5,128]{3,1,2,0:T(8,128)(2,1)} %copy-done.11) | copy-start | bytes 1966084
  373.9 6.0 %copy-start.14 = (bf16[2,256,5,128]{3,1,2,0:T(8,128)(2,1)S(1)}, bf16[2,256,5,128]{3,1,2,0:T(8,128)(2,1)}, u32[]{:S(2)}) copy-start(bf16[2,256,5,128]{3,1,2,0:T(8,128)(2,1)} %copy-done.13) | copy-start | bytes 1966084
  375.0 23.1 %collective-permute-start.3 = (bf16[2,256,640]{1,2,0:T(8,128)(2,1)}, bf16[2,256,640]{1,2,0:T(8,128)(2,1)}, u32[]{:S(2)}, u32[]{:S(2)}) collective-permute-start(bf16[2,256,640]{1,2,0:T(8,128)(2,1)} %pad_maximum_fusion.14), channel_id=1, source_target_pairs={{16,0},{24,8},{32,16},{40,24},{48,32},{56,40},{64,48},{72,56},{80,... | collective-permute-start | bytes 1966088 | tf_op jit(solution)/shard_map/ppermute | solution.py:16
  377.2 20.9 %collective-permute-start.2 = (bf16[2,256,640]{1,2,0:T(8,128)(2,1)}, bf16[2,256,640]{1,2,0:T(8,128)(2,1)}, u32[]{:S(2)}, u32[]{:S(2)}) collective-permute-start(bf16[2,256,640]{1,2,0:T(8,128)(2,1)} %pad_maximum_fusion.13), channel_id=1, source_target_pairs={{8,0},{16,8},{24,16},{32,24},{40,32},{48,40},{56,48},{64,56},{72,6... | collective-permute-start | bytes 1966088 | tf_op jit(solution)/shard_map/ppermute | solution.py:16
  399.5 4.8 %copy-start.18 = (bf16[1,2,256,640]{3,2,1,0:T(8,128)(2,1)S(1)}, bf16[1,2,256,640]{3,2,1,0:T(8,128)(2,1)}, u32[]{:S(2)}) copy-start(bf16[1,2,256,640]{3,2,1,0:T(8,128)(2,1)} %param.23) | copy-start | bytes 1966084
  411.5 52.2 %copy-start.1 = (bf16[5120,320]{0,1:T(8,128)(2,1)S(1)}, bf16[5120,320]{0,1:T(8,128)(2,1)}, u32[]{:S(2)}) copy-start(bf16[5120,320]{0,1:T(8,128)(2,1)} %param.18) | copy-start | bytes 9830404
  (9 other events, 24.7 us)
Sparse Core Ops, SparseCore 0:
  10.2 131.9 all-gather.1
  242.6 212.9 reduce-scatter.1

commit v3 on v2

--- a/solution.py
+++ b/solution.py
@@ -71,11 +71,12 @@
     row_count = steps_here * tokens_here
     action_count = actions.shape[1]
     score_scale = HD ** (-0.5)
-    full_both = lax.all_gather(
-        jnp.concatenate([hidden_in, out_grad], axis=0), "tensor", axis=3, tiled=True
-    )
-    input_rows = full_both[0].reshape(row_count, model_width)
-    grad_rows = full_both[1].reshape(row_count, model_width)
+    group_count = lax.axis_size("tensor")
+    full_inputs = lax.all_gather(hidden_in, "tensor", axis=3, tiled=True)
+    copies = jnp.broadcast_to(out_grad, (group_count,) + out_grad.shape[1:])
+    gathered = lax.all_to_all(copies, "tensor", 0, 0, tiled=True)
+    input_rows = full_inputs.reshape(row_count, model_width)
+    grad_rows = jnp.transpose(gathered, (1, 2, 0, 3)).reshape(row_count, model_width)
     own_cache = clean_cache[0]
     nearer = from_behind(own_cache, "tm", 1)
     farther = from_behind(own_cache, "tm", 2)
@@ -166,13 +167,16 @@
         out_term.astype(jnp.bfloat16),
         table_term.reshape(tm_count, table_rows, branch_width).astype(jnp.bfloat16),
     )
+    proj_sum = lax.psum_scatter(pieces[0], "tm", scatter_dimension=0, tiled=True)[0]
     merged = lax.psum_scatter(
-        jnp.concatenate(pieces, axis=1), "tm", scatter_dimension=0, tiled=True
-    )[0].astype(jnp.float32)
+        jnp.concatenate(pieces[1:], axis=1), "tm", scatter_dimension=0, tiled=True
+    )[0]
     bounds = [0]
-    for piece in pieces:
+    for piece in pieces[1:]:
         bounds.append(bounds[-1] + piece.shape[1])
-    summed = tuple(merged[bounds[i] : bounds[i + 1]] for i in range(4))
+    summed = (proj_sum.astype(jnp.float32),) + tuple(
+        merged[bounds[i] : bounds[i + 1]].astype(jnp.float32) for i in range(3)
+    )
     input_term = contract_cols(pre_grad, branch_in)
     input_sum = sum_over_groups(input_term.astype(jnp.bfloat16), steps_here, tokens_here)
     input_grad = (out_grad.astype(jnp.float32) + input_sum).astype(jnp.bfloat16)

time: 478 us -> 488 us (1.021)
  local copies, waits for them, and re-layouts: 114 us -> 87.7 us
  waiting for transfers between devices: 185 us -> 209 us
  other arithmetic: 23 us -> 30 us
    all_gather x1, waiting for transfers between devices: 91.8 us -> 0.01 us  [body(): full_inputs = lax.all_gather(hidden_in, 'tensor', axis=3, tiled=True)]
    all_to_all x0 -> x1, waiting for transfers between devices: none -> 87.1 us  [body(): gathered = lax.all_to_all(copies, 'tensor', 0, 0, tiled=True)]
    reduce_scatter x1 -> x2, waiting for transfers between devices: 41.8 us -> 94 us  [the longest x1 94 us: body(): lax.psum_scatter(jnp.concatenate(pieces[1:], axis=1), 'tm', scatter_dimen...]
    all_to_all x2, waiting for transfers between devices: 50.3 us -> 26.1 us  [sum_over_groups(): received = lax.all_to_all(blocks, 'tensor', 1, 1, tiled=True)]
    concatenate x1 -> x0, local copies, waits for them, and re-layouts: 21.9 us -> none  [body(): jnp.concatenate(pieces, axis=1)]
    slice x4 -> x0, local copies, waits for them, and re-layouts: 10.7 us -> none  [the longest x1 8.71 us: body(): grad_rows = full_both[1].reshape(row_count, model_width)]
    another operation x2 -> x1, local copies, waits for them, and re-layouts: 19.9 us -> 9.22 us  [body(): grad_split = grad_rows.reshape(row_count, tm_count, col_block)]
    broadcast_in_dim x0 -> x2, local copies, waits for them, and re-layouts: none -> 9.26 us  [body(): copies = jnp.broadcast_to(out_grad, (group_count,) + out_grad.shape[1:])]
  transfers between devices with their start and end apart: 8 -> 10, of which waited for: 5 -> 4; matrix products, arithmetic and copies ran while one was open for 25% -> 42% of each run, Pallas kernels for 0% -> 0%
where the time goes in v3:
time: 488 us; the launch traced here: 479 us
  waiting for transfers between devices  209 us (43%)
  matrix products  97.1 us (20%)
  local copies, waits for them, and re-layouts  87.7 us (18%)
  starting transfers between devices  37.6 us (8%)
  other arithmetic  30 us (6%)
  between operations  17.1 us (4%)
    reduce_scatter x1, waiting for transfers between devices, body(): lax.psum_scatter(jnp.concatenate(pieces[1:], axis=1), 'tm', scatter_dimen...  94 us
    all_to_all x1, waiting for transfers between devices, body(): gathered = lax.all_to_all(copies, 'tensor', 0, 0, tiled=True)  87.1 us
    unnamed x65, local copies, waits for them, and re-layouts  31.1 us
    all_to_all x2, waiting for transfers between devices, sum_over_groups(): received = lax.all_to_all(blocks, 'tensor', 1, 1, tiled=True)  26.1 us
    all_to_all x2, starting transfers between devices, sum_over_groups(): received = lax.all_to_all(blocks, 'tensor', 1, 1, tiled=True)  22.9 us
    dot_general x3, matrix products, contract_cols(): lax.dot_general(left, right, (((1,), (1,)), ((), ())), preferred_element_...  19.7 us
    dot_general x1, matrix products, body(): jnp.einsum('shqk,sqhe->skhe', score_grad, query_heads, preferred_element_...  14.1 us
    dot_general x1, matrix products, body(): jnp.einsum('shqk,skhe->sqhe', score_grad, key_heads, preferred_element_ty...  14 us
  transfers between devices with their start and end apart: 10, of which 4 were waited for; matrix products, arithmetic and copies ran while one was open for 42% of the time, Pallas kernels for 0%

profile of v3, /device:TPU:0, one launch (start us, length us, event | category | flops | bytes accessed | tf_op | source)
XLA Modules:
  0.0 478.8 jit_solution(10334543720475659739)
XLA Ops:
  11.9 6.1 %broadcast_in_dim.77 = bf16[8,2,256,640]{2,1,3,0:T(2,128)(2,1)} broadcast(bf16[2,256,640]{1,0,2:T(2,128)(2,1)} %copy.153), dimensions={1,2,3} | broadcast | bytes 5898240 | tf_op jit(solution)/shard_map/broadcast_in_dim | solution.py:76
  18.0 5.8 %all-to-all-start.1 = ((bf16[8,2,256,640]{2,1,3,0:T(2,128)(2,1)}), bf16[8,2,256,640]{2,1,3,0:T(2,128)(2,1)}, u32[]{:S(2)}, u32[]{:S(2)}) async-start(bf16[8,2,256,640]{2,1,3,0:T(2,128)(2,1)} %broadcast_in_dim.77), calls=%async_computation.1 | async-start | bytes 10485760 | tf_op jit(solution)/shard_map/all_to_all | solution.py:77
  28.3 3.9 collective-permute-start
  64.4 87.1 %all-to-all-done.1 = bf16[8,2,256,640]{2,1,3,0:T(2,128)(2,1)} async-done(((bf16[8,2,256,640]{2,1,3,0:T(2,128)(2,1)}), bf16[8,2,256,640]{2,1,3,0:T(2,128)(2,1)}, u32[]{:S(2)}, u32[]{:S(2)}) %all-to-all-start.1) | async-done | bytes 5242912 | tf_op jit(solution)/shard_map/all_to_all | solution.py:77
  151.5 9.2 %reshape_reshape.6 = bf16[512,16,320]{0,2,1:T(8,128)(2,1)} reshape(bf16[2,256,8,640]{1,0,3,2:T(2,128)(2,1)} %bitcast.19) | data formatting | bytes 10485760 | tf_op jit(solution)/shard_map/reshape;reshape | solution.py:147
  160.7 9.7 %fusion.9 = bf16[16,640,320]{1,2,0:T(8,128)(2,1)} fusion(bf16[512,16,320]{0,2,1:T(8,128)(2,1)} %reshape_reshape.6, bf16[512,640]{0,1:T(8,128)(2,1)} %bitcast.163), kind=kOutput, calls=%fused_computation.18 | convolution fusion | flops 3358720000 | bytes 12451840 | tf_op jit(solution)/shard_map/rk,rjn->jkn/dot_general | solution.py:162
  171.5 6.1 %copy.199 = bf16[640,8,2,256]{3,1,2,0:T(8,128)(2,1)} copy(bf16[640,8,2,256]{3,2,1,0:T(2,128)(2,1)} %bitcast.62) | data formatting | bytes 10485760
  177.5 6.9 %fusion.48 = (bf16[2,4,64,320]{3,2,1,0:T(8,128)(2,1)}, f32[2,4,64,320]{3,2,1,0:T(8,128)}) fusion(f32[4,320]{1,0:T(4,128)S(1)} %fusion.67, bf16[2,4,64,5120]{3,2,1,0:T(8,128)(2,1)} %bitcast.149, bf16[5120,320]{0,1:T(8,128)(2,1)S(1)} %copy-done), kind=kOutput, calls=%fused_computation.61 | convolution fusion | flops 1679360000 | bytes 9507840 | tf_op jit(solution)/shard_map/dot_general | solution.py:131
  186.7 6.6 %fusion.43 = bf16[512,320]{0,1:T(8,128)(2,1)} fusion(bf16[320,5120]{1,0:T(8,128)(2,1)} %param.19, bf16[512,5120]{0,1:T(8,128)(2,1)} %bitcast.150, f32[512,320]{0,1:T(8,128)} %copy.147), kind=kOutput, calls=%fused_computation.52 | convolution fusion | flops 1680834560 | bytes 9502720 | tf_op jit(solution)/shard_map/dot_general | solution.py:38
  198.5 4.3 convolution_convert_fusion
  205.5 4.7 all-to-all-start.2
  210.3 11.1 %reshape.137 = bf16[512,16,320]{2,1,0:T(8,128)(2,1)} reshape(bf16[1,2,256,5120]{3,2,1,0:T(8,128)(2,1)} %all-gather.2.cloned.1.call-done) | data formatting | bytes 10485760 | tf_op jit(solution)/shard_map/reshape;reshape | solution.py:150
  221.3 5.5 %convert_bitcast_fusion = bf16[16,320,320]{1,2,0:T(8,128)(2,1)S(1)} fusion(bf16[512,320,1]{1,0,2:T(8,128)(2,1)S(1)} %bitcast.184, bf16[512,16,320]{0,2,1:T(8,128)(2,1)} %reshape_reshape.6), kind=kOutput, calls=%fused_computation.21 | convolution fusion | flops 1679360000 | bytes 8847360 | tf_op jit(solution)/shard_map/rk,rjn->jkn/dot_general | solution.py:154
  229.6 6.0 %pad_maximum_fusion = bf16[16,648,320]{1,2,0:T(8,128)(2,1)} fusion(bf16[16,8,320]{1,2,0:T(8,128)(2,1)S(1)} %copy-done.3, bf16[16,320,320]{1,2,0:T(8,128)(2,1)S(1)} %convert_bitcast_fusion, bf16[16,320,320]{1,2,0:T(8,128)(2,1)S(1)} %convert_bitcast_fusion.1), kind=kLoop, calls=%fused_computation.5 | loop fusion | flops 19906560 | bytes 13271040 | tf_op jit(solution)/shard_map/concatenate | solution.py:172
  236.6 6.6 %fusion.86 = f32[512,5120]{1,0:T(8,128)S(1)} fusion(bf16[512,640]{0,1:T(8,128)(2,1)S(1)} %bitcast.164, bf16[640,5120]{1,0:T(8,128)(2,1)} %param.17), kind=kOutput, calls=%fused_computation.115 | convolution fusion | flops 3355443200 | bytes 17694720 | tf_op jit(solution)/shard_map/dot_general | solution.py:138
  249.3 26.1 %all-to-all-done.2 = bf16[512,8,640]{2,0,1:T(8,128)(2,1)} async-done(((bf16[512,8,640]{2,0,1:T(8,128)(2,1)}), bf16[512,8,640]{2,0,1:T(8,128)(2,1)}, u32[]{:S(2)}, u32[]{:S(2)}) %all-to-all-start.2) | async-done | bytes 5242912 | tf_op jit(solution)/shard_map/all_to_all | solution.py:47
  275.4 18.2 %all-to-all-start = ((bf16[512,8,640]{2,0,1:T(8,128)(2,1)}), bf16[512,8,640]{2,0,1:T(8,128)(2,1)}, u32[]{:S(2)}, u32[]{:S(2)}) async-start(bf16[512,8,640]{2,0,1:T(8,128)(2,1)} %bitcast.146), calls=%async_computation | async-start | bytes 10485760 | tf_op jit(solution)/shard_map/all_to_all | solution.py:47
  293.7 8.8 %convolution_convert_fusion.2 = bf16[512,640]{1,0:T(8,128)(2,1)S(1)} fusion(bf16[512,5120]{0,1:T(8,128)(2,1)} %bitcast.151, bf16[640,5120]{1,0:T(8,128)(2,1)} %param.17), kind=kOutput, calls=%fused_computation.41 | convolution fusion | flops 3355770880 | bytes 12451840 | tf_op jit(solution)/shard_map/dot_general | solution.py:38
  303.8 5.5 %fusion.30 = f32[2,5,256,768]{2,3,1,0:T(8,128)} fusion(bf16[2,256,5,128]{1,3,2,0:T(8,128)(2,1)S(1)} %copy.166, bf16[2,256,5,128]{1,3,2,0:T(8,128)(2,1)S(1)} %bitcast.162, bf16[2,256,5,128]{1,3,2,0:T(8,128)(2,1)S(1)} %copy-done.16, bf16[2,256,5,128]{1,3,2,0:T(8,128)(2,1)} %copy-done.17), kind=kOutput, calls=%fused_computation.38 | convolution fusion | flops 509214720 | bytes 10485760 | tf_op jit(solution)/shard_map/sqhe,skhe->shqk/dot_general | solution.py:188
  309.3 14.1 %fusion.13 = f32[2,5,768,128]{2,3,1,0:T(8,128)} fusion(bf16[2,256,5,128]{1,3,2,0:T(8,128)(2,1)S(1)} %bitcast.160, f32[2,5,256,768]{2,3,1,0:T(8,128)} %fusion.30, f32[2,5,256,768]{2,3,1,0:T(8,128)} %copy-done.25, f32[2,5,256]{2,1,0:T(8,128)S(1)} %get-tuple-element.60), kind=kOutput, calls=%fused_computation.23 | convolution fusion | flops 517082368 | bytes 20326400 | tf_op jit(solution)/shard_map/shqk,sqhe->skhe/dot_general | solution.py:198
  325.4 4.6 fusion.25
  336.1 14.0 %fusion.34 = bf16[2,5,128,256]{3,2,1,0:T(8,128)(2,1)} fusion(f32[2,5,256,768]{2,3,1,0:T(8,128)} %fusion.30, bf16[2,256,5,128]{3,1,2,0:T(8,128)(2,1)S(1)} %copy-done.6, bf16[2,256,5,128]{3,1,2,0:T(8,128)(2,1)S(1)} %copy-done.12, bf16[2,256,5,128]{3,1,2,0:T(8,128)(2,1)S(1)} %copy-done.14, f32[2,5,256,768]{2,3,1,0:T(8,128)} %copy-done.25, ...), kind=kOutput, calls=%fused_computation.40 | convolution fusion | flops 523308288 | bytes 18360320 | tf_op jit(solution)/shard_map/shqk,skhe->sqhe/dot_general | solution.py:194
  361.7 3.6 convert_reduce_fusion.1
  369.3 94.0 %reduce-scatter.5.cloned.1.call-done = bf16[1,648,320]{1,2,0:T(8,128)(2,1)} async-done(((bf16[16,648,320]{1,2,0:T(8,128)(2,1)}), bf16[1,648,320]{1,2,0:T(8,128)(2,1)}) %reduce-scatter.5.cloned.1.call-update) | async-done | bytes 414736 | tf_op jit(solution)/shard_map/reduce_scatter | solution.py:171
  (124 shorter events, 93.4 us)
Async XLA Ops:
  8.0 169.5 %copy-start = (bf16[5120,320]{0,1:T(8,128)(2,1)S(1)}, bf16[5120,320]{0,1:T(8,128)(2,1)}, u32[]{:S(2)}) copy-start(bf16[5120,320]{0,1:T(8,128)(2,1)} %param.18) | copy-start | bytes 9830404
  8.0 169.5 %all-gather.2.cloned.1.call-start = ((), (), s32[]{:S(2)}) async-start(), calls=%async_computation.5 | async-start | bytes 5898240 | tf_op jit(solution)/shard_map/all_gather | solution.py:75
  18.0 133.4 %all-to-all-start.1 = ((bf16[8,2,256,640]{2,1,3,0:T(2,128)(2,1)}), bf16[8,2,256,640]{2,1,3,0:T(2,128)(2,1)}, u32[]{:S(2)}, u32[]{:S(2)}) async-start(bf16[8,2,256,640]{2,1,3,0:T(2,128)(2,1)} %broadcast_in_dim.77), calls=%async_computation.1 | async-start | bytes 10485760 | tf_op jit(solution)/shard_map/all_to_all | solution.py:77
  23.8 343.5 %reduce-scatter.3.cloned.1.call-start = ((), (), s32[]{:S(2)}) async-start(), calls=%async_computation.6 | async-start | bytes 6963200 | tf_op jit(solution)/shard_map/reduce_scatter | solution.py:170
  26.0 15.6 %collective-permute-start.1 = (bf16[2,256,640]{1,2,0:T(8,128)(2,1)}, bf16[2,256,640]{1,2,0:T(8,128)(2,1)}, u32[]{:S(2)}, u32[]{:S(2)}) collective-permute-start(bf16[2,256,640]{1,2,0:T(8,128)(2,1)} %bitcast.179), channel_id=1, source_target_pairs={{0,8},{8,16},{16,24},{24,32},{32,40},{40,48},{48,56},{56,64},{64,7... | collective-permute-start | bytes 1966088 | tf_op jit(solution)/shard_map/ppermute | solution.py:16
  28.3 18.5 %collective-permute-start = (bf16[2,256,640]{1,2,0:T(8,128)(2,1)}, bf16[2,256,640]{1,2,0:T(8,128)(2,1)}, u32[]{:S(2)}, u32[]{:S(2)}) collective-permute-start(bf16[2,256,640]{1,2,0:T(8,128)(2,1)} %bitcast.180), channel_id=1, source_target_pairs={{0,16},{8,24},{16,32},{24,40},{32,48},{40,56},{48,64},{56,72},{64,... | collective-permute-start | bytes 1966088 | tf_op jit(solution)/shard_map/ppermute | solution.py:16
  205.5 69.9 %all-to-all-start.2 = ((bf16[512,8,640]{2,0,1:T(8,128)(2,1)}), bf16[512,8,640]{2,0,1:T(8,128)(2,1)}, u32[]{:S(2)}, u32[]{:S(2)}) async-start(bf16[512,8,640]{2,0,1:T(8,128)(2,1)} %bitcast.147), calls=%async_computation.2 | async-start | bytes 10485760 | tf_op jit(solution)/shard_map/all_to_all | solution.py:47
  210.2 11.1 %copy-start.24 = (bf16[2,4,64,320]{3,2,1,0:T(8,128)(2,1)S(1)}, bf16[2,4,64,320]{3,2,1,0:T(8,128)(2,1)}, u32[]{:S(2)}) copy-start(bf16[2,4,64,320]{3,2,1,0:T(8,128)(2,1)} %get-tuple-element.62) | copy-start | bytes 983044
  210.2 253.0 %reduce-scatter.5.cloned.1.call-start = ((), (), s32[]{:S(2)}) async-start(), calls=%async_computation.7 | async-start | bytes 8355840 | tf_op jit(solution)/shard_map/reduce_scatter | solution.py:171
  221.3 5.5 %copy-start.2 = (bf16[512,16,320]{2,1,0:T(8,128)(2,1)S(1)}, bf16[512,16,320]{2,1,0:T(8,128)(2,1)}, u32[]{:S(2)}) copy-start(bf16[512,16,320]{2,1,0:T(8,128)(2,1)} %reshape.137) | copy-start | bytes 15728644
  221.3 5.5 %copy-start.19 = (bf16[512,320]{0,1:T(8,128)(2,1)S(1)}, bf16[512,320]{0,1:T(8,128)(2,1)}, u32[]{:S(2)}) copy-start(bf16[512,320]{0,1:T(8,128)(2,1)} %fusion.43) | copy-start | bytes 983044
  236.6 6.6 %copy-start.4 = (f32[512,320]{0,1:T(8,128)S(1)}, f32[512,320]{0,1:T(8,128)}, u32[]{:S(2)}) copy-start(f32[512,320]{0,1:T(8,128)} %copy.147) | copy-start | bytes 1966084
  236.6 6.6 %copy-start.5 = (bf16[320,5120]{1,0:T(8,128)(2,1)S(1)}, bf16[320,5120]{1,0:T(8,128)(2,1)}, u32[]{:S(2)}) copy-start(bf16[320,5120]{1,0:T(8,128)(2,1)} %param.19) | copy-start | bytes 9830404
  275.4 86.2 %all-to-all-start = ((bf16[512,8,640]{2,0,1:T(8,128)(2,1)}), bf16[512,8,640]{2,0,1:T(8,128)(2,1)}, u32[]{:S(2)}, u32[]{:S(2)}) async-start(bf16[512,8,640]{2,0,1:T(8,128)(2,1)} %bitcast.146), calls=%async_computation | async-start | bytes 10485760 | tf_op jit(solution)/shard_map/all_to_all | solution.py:47
  293.7 10.1 %copy-start.9 = (bf16[1,2,256,640]{2,3,1,0:T(8,128)(2,1)S(1)}, bf16[1,2,256,640]{2,3,1,0:T(8,128)(2,1)}, u32[]{:S(2)}) copy-start(bf16[1,2,256,640]{2,3,1,0:T(8,128)(2,1)} %copy.138) | copy-start | bytes 1966084
  293.7 10.1 %copy-start.16 = (bf16[2,256,5,128]{1,3,2,0:T(8,128)(2,1)S(1)}, bf16[2,256,5,128]{1,3,2,0:T(8,128)(2,1)}, u32[]{:S(2)}) copy-start(bf16[2,256,5,128]{1,3,2,0:T(8,128)(2,1)} %copy-done.15) | copy-start | bytes 1966084
  303.8 5.5 %copy-start.7 = (bf16[1,2,256,640]{2,3,1,0:T(8,128)(2,1)S(1)}, bf16[1,2,256,640]{2,3,1,0:T(8,128)(2,1)}, u32[]{:S(2)}) copy-start(bf16[1,2,256,640]{2,3,1,0:T(8,128)(2,1)} %copy.143) | copy-start | bytes 1966084
  330.1 6.0 %copy-start.6 = (bf16[2,256,5,128]{3,1,2,0:T(8,128)(2,1)S(1)}, bf16[2,256,5,128]{3,1,2,0:T(8,128)(2,1)}, u32[]{:S(2)}) copy-start(bf16[2,256,5,128]{3,1,2,0:T(8,128)(2,1)} %copy.142) | copy-start | bytes 1966084
  330.1 6.0 %copy-start.12 = (bf16[2,256,5,128]{3,1,2,0:T(8,128)(2,1)S(1)}, bf16[2,256,5,128]{3,1,2,0:T(8,128)(2,1)}, u32[]{:S(2)}) copy-start(bf16[2,256,5,128]{3,1,2,0:T(8,128)(2,1)} %copy-done.11) | copy-start | bytes 1966084
  330.1 6.0 %copy-start.14 = (bf16[2,256,5,128]{3,1,2,0:T(8,128)(2,1)S(1)}, bf16[2,256,5,128]{3,1,2,0:T(8,128)(2,1)}, u32[]{:S(2)}) copy-start(bf16[2,256,5,128]{3,1,2,0:T(8,128)(2,1)} %copy-done.13) | copy-start | bytes 1966084
  331.2 23.3 %collective-permute-start.3 = (bf16[2,256,640]{1,2,0:T(8,128)(2,1)}, bf16[2,256,640]{1,2,0:T(8,128)(2,1)}, u32[]{:S(2)}, u32[]{:S(2)}) collective-permute-start(bf16[2,256,640]{1,2,0:T(8,128)(2,1)} %pad_maximum_fusion.14), channel_id=1, source_target_pairs={{16,0},{24,8},{32,16},{40,24},{48,32},{56,40},{64,48},{72,56},{80,... | collective-permute-start | bytes 1966088 | tf_op jit(solution)/shard_map/ppermute | solution.py:16
  333.3 21.1 %collective-permute-start.2 = (bf16[2,256,640]{1,2,0:T(8,128)(2,1)}, bf16[2,256,640]{1,2,0:T(8,128)(2,1)}, u32[]{:S(2)}, u32[]{:S(2)}) collective-permute-start(bf16[2,256,640]{1,2,0:T(8,128)(2,1)} %pad_maximum_fusion.13), channel_id=1, source_target_pairs={{8,0},{16,8},{24,16},{32,24},{40,32},{48,40},{56,48},{64,56},{72,6... | collective-permute-start | bytes 1966088 | tf_op jit(solution)/shard_map/ppermute | solution.py:16
  355.9 4.8 %copy-start.18 = (bf16[1,2,256,640]{3,2,1,0:T(8,128)(2,1)S(1)}, bf16[1,2,256,640]{3,2,1,0:T(8,128)(2,1)}, u32[]{:S(2)}) copy-start(bf16[1,2,256,640]{3,2,1,0:T(8,128)(2,1)} %param.23) | copy-start | bytes 1966084
  361.7 109.3 %copy-start.1 = (bf16[5120,320]{0,1:T(8,128)(2,1)S(1)}, bf16[5120,320]{0,1:T(8,128)(2,1)}, u32[]{:S(2)}) copy-start(bf16[5120,320]{0,1:T(8,128)(2,1)} %param.18) | copy-start | bytes 9830404
  (12 other events, 25.8 us)
Sparse Core Ops, SparseCore 0:
  10.5 143.8 all-gather.1
Sparse Core Ops, SparseCore 1:
  170.5 193.4 reduce-scatter.2
  368.0 95.1 reduce-scatter.4

commit v4 on v2

--- a/solution.py
+++ b/solution.py
@@ -142,15 +142,6 @@
     attended_grad = contract_cols(grad_rows, out_proj).astype(jnp.bfloat16)
     pre_grad = (contract_cols(grad_rows, branch_out) * gelu_slope(pre_act)).astype(jnp.bfloat16)
     tm_count = lax.axis_size("tm")
-    col_block = model_width // tm_count
-    grad_split = grad_rows.reshape(row_count, tm_count, col_block)
-    in_term = jnp.einsum(
-        "rjk,rn->jkn",
-        input_rows.reshape(row_count, tm_count, model_width // tm_count),
-        pre_grad,
-        preferred_element_type=jnp.float32,
-    )
-    out_term = jnp.einsum("rk,rjn->jkn", branch_act, grad_split, preferred_element_type=jnp.float32)
     grouped = jnp.sum(
         pre_grad.reshape(
             steps_here, action_count, tokens_here // action_count, branch_width
@@ -158,21 +149,27 @@
         axis=(0, 2),
     )
     table_term = jnp.dot(onehot.astype(jnp.float32).T, grouped, precision=lax.Precision.HIGHEST)
-    proj_term = jnp.einsum("rk,rjn->jkn", attended, grad_split, preferred_element_type=jnp.float32)
-    table_rows = table_term.shape[0] // tm_count
-    pieces = (
-        proj_term.astype(jnp.bfloat16),
-        in_term.astype(jnp.bfloat16),
-        out_term.astype(jnp.bfloat16),
-        table_term.reshape(tm_count, table_rows, branch_width).astype(jnp.bfloat16),
-    )
-    merged = lax.psum_scatter(
-        jnp.concatenate(pieces, axis=1), "tm", scatter_dimension=0, tiled=True
-    )[0].astype(jnp.float32)
-    bounds = [0]
-    for piece in pieces:
-        bounds.append(bounds[-1] + piece.shape[1])
-    summed = tuple(merged[bounds[i] : bounds[i + 1]] for i in range(4))
+    head_cols = attended.shape[1]
+    input_side = jnp.concatenate(
+        [jnp.zeros((row_count, head_cols + branch_width), jnp.bfloat16), pre_grad], axis=1
+    )
+    grad_side = jnp.concatenate(
+        [attended, branch_act, jnp.zeros((row_count, branch_width), jnp.bfloat16)], axis=1
+    )
+    terms = contract_rows(
+        full_both.reshape(2 * row_count, model_width),
+        jnp.concatenate([input_side, grad_side], axis=0),
+    ).astype(jnp.bfloat16)
+    merged = lax.psum_scatter(terms, "tm", scatter_dimension=0, tiled=True).astype(jnp.float32)
+    table_blocks = lax.all_to_all(
+        table_term.astype(jnp.bfloat16).reshape(tm_count, -1, branch_width), "tm", 0, 0, tiled=True
+    )
+    summed = (
+        merged[:, :head_cols].T,
+        merged[:, head_cols + branch_width :],
+        merged[:, head_cols : head_cols + branch_width].T,
+        jnp.sum(table_blocks.astype(jnp.float32), axis=0),
+    )
     input_term = contract_cols(pre_grad, branch_in)
     input_sum = sum_over_groups(input_term.astype(jnp.bfloat16), steps_here, tokens_here)
     input_grad = (out_grad.astype(jnp.float32) + input_sum).astype(jnp.bfloat16)

time: 478 us -> 469 us (0.981)
  local copies, waits for them, and re-layouts: 114 us -> 63.1 us
  waiting for transfers between devices: 185 us -> 215 us
  matrix products: 97 us -> 115 us
  starting transfers between devices: 36.2 us -> 28.1 us
    another operation x3 -> x0, local copies, waits for them, and re-layouts: 30.8 us -> none  [the longest x2 19.9 us: body(): grad_split = grad_rows.reshape(row_count, tm_count, col_block)]
    concatenate x1 -> x0, local copies, waits for them, and re-layouts: 21.9 us -> none  [body(): jnp.concatenate(pieces, axis=1)]
    all_to_all x2, waiting for transfers between devices: 50.3 us -> 66.6 us  [sum_over_groups(): received = lax.all_to_all(blocks, 'tensor', 1, 1, tiled=True)]
    reduce_scatter x1, waiting for transfers between devices: 41.8 us -> 55.3 us  [body(): lax.psum_scatter(terms, 'tm', scatter_dimension=0, tiled=True)]
    all_to_all x2, starting transfers between devices: 27.2 us -> 15.5 us  [sum_over_groups(): received = lax.all_to_all(blocks, 'tensor', 1, 1, tiled=True)]
    dot_general x3 -> x1, matrix products: 18.4 us -> 28.4 us  [contract_rows(): lax.dot_general(left, right, (((0,), (0,)), ((), ())), preferred_element_...]
    dot_general x1, matrix products: 7.1 us -> 12.6 us  [body(): jnp.dot(attended, out_proj, preferred_element_type=jnp.float32)]
    unnamed x62 -> x64, local copies, waits for them, and re-layouts: 23.3 us -> 23 us
  transfers between devices with their start and end apart: 8 -> 9, of which waited for: 5 -> 4; matrix products, arithmetic and copies ran while one was open for 25% -> 29% of each run, Pallas kernels for 0% -> 0%
where the time goes in v4:
time: 469 us; the launch traced here: 463 us
  waiting for transfers between devices  215 us (46%)
  matrix products  115 us (25%)
  local copies, waits for them, and re-layouts  63.1 us (13%)
  starting transfers between devices  28.1 us (6%)
  other arithmetic  26 us (6%)
  between operations  15.7 us (3%)
    all_gather x1, waiting for transfers between devices, body(): lax.all_gather(jnp.concatenate([hidden_in, out_grad], axis=0), 'tensor',...  91.9 us
    all_to_all x2, waiting for transfers between devices, sum_over_groups(): received = lax.all_to_all(blocks, 'tensor', 1, 1, tiled=True)  66.6 us
    reduce_scatter x1, waiting for transfers between devices, body(): lax.psum_scatter(terms, 'tm', scatter_dimension=0, tiled=True)  55.3 us
    dot_general x1, matrix products, contract_rows(): lax.dot_general(left, right, (((0,), (0,)), ((), ())), preferred_element_...  28.4 us
    unnamed x64, local copies, waits for them, and re-layouts  23 us
    dot_general x3, matrix products, contract_cols(): lax.dot_general(left, right, (((1,), (1,)), ((), ())), preferred_element_...  17.8 us
    all_to_all x2, starting transfers between devices, sum_over_groups(): received = lax.all_to_all(blocks, 'tensor', 1, 1, tiled=True)  15.5 us
    dot_general x1, matrix products, body(): jnp.einsum('shqk,sqhe->skhe', score_grad, query_heads, preferred_element_...  14.6 us
  transfers between devices with their start and end apart: 9, of which 4 were waited for; matrix products, arithmetic and copies ran while one was open for 29% of the time, Pallas kernels for 0%

profile of v4, /device:TPU:0, one launch (start us, length us, event | category | flops | bytes accessed | tf_op | source)
XLA Modules:
  0.0 462.6 jit_solution(4390569697795421752)
XLA Ops:
  14.3 4.2 collective-permute-start
  42.6 2.6 fusion.74
  50.4 91.9 %all-gather.2.cloned.1.call-done = bf16[2,2,256,5120]{3,2,1,0:T(8,128)(2,1)} async-done(((bf16[2,2,256,640]{3,2,1,0:T(8,128)(2,1)}), bf16[2,2,256,5120]{3,2,1,0:T(8,128)(2,1)}) %all-gather.2.cloned.1.call-update) | async-done | bytes 10485776 | tf_op jit(solution)/shard_map/all_gather | solution.py:74
  142.3 8.7 %fusion.71 = (bf16[1,2,256,5120]{3,2,1,0:T(8,128)(2,1)}, bf16[1,2,256,5120]{3,2,1,0:T(8,128)(2,1)}) fusion(bf16[2,2,256,5120]{3,2,1,0:T(8,128)(2,1)} %all-gather.2.cloned.1.call-done), kind=kLoop, calls=%fused_computation.97 | loop fusion | bytes 20971520 | tf_op jit(solution)/shard_map/slice | solution.py:78
  151.0 7.3 %fusion.46 = f32[2,4,64,320]{3,2,1,0:T(8,128)} fusion(bf16[2,4,64,5120]{3,2,1,0:T(8,128)(2,1)} %bitcast.110, bf16[5120,320]{0,1:T(8,128)(2,1)} %param.18, f32[4,320]{1,0:T(4,128)S(1)} %fusion.55), kind=kOutput, calls=%fused_computation.57 | convolution fusion | flops 1677885440 | bytes 9180160 | tf_op jit(solution)/shard_map/dot_general | solution.py:130
  161.8 4.9 %fusion.49 = bf16[512,320]{0,1:T(8,128)(2,1)S(1)} fusion(bf16[512,5120]{1,0:T(8,128)(2,1)} %bitcast.108, bf16[320,5120]{1,0:T(8,128)(2,1)S(1)} %copy-done, f32[512,320]{0,1:T(8,128)} %copy.93), kind=kOutput, calls=%fused_computation.58 | convolution fusion | flops 1680834560 | bytes 9502720 | tf_op jit(solution)/shard_map/dot_general | solution.py:38
  167.5 28.4 %convolution_convert_fusion = bf16[5120,1280]{1,0:T(8,128)(2,1)} fusion(bf16[1024,5120]{1,0:T(8,128)(2,1)} %bitcast.107, bf16[512,320]{0,1:T(8,128)(2,1)S(1)} %fusion.49, bf16[512,320]{0,1:T(8,128)(2,1)S(1)} %broadcast_in_dim.76, bf16[512,320]{0,1:T(8,128)(2,1)S(1)} %multiply_convert_fusion.1, bf16[512,640]{0,1:T(8,128)(2,1)S(1)} %bitcast.123), kind=kOutput, calls=%fused_computation.2 | convolution fusion | flops 13441433600 | bytes 25231360 | tf_op jit(solution)/shard_map/dot_general | solution.py:32
  195.9 12.6 %fusion.75 = f32[512,5120]{1,0:T(8,128)} fusion(bf16[512,640]{0,1:T(8,128)(2,1)} %bitcast.122, bf16[640,5120]{1,0:T(8,128)(2,1)} %param.17), kind=kOutput, calls=%fused_computation.101 | convolution fusion | flops 3355443200 | bytes 17694720 | tf_op jit(solution)/shard_map/dot_general | solution.py:137
  213.0 3.5 all-to-all-start.2
  216.5 6.8 %add_convert_fusion = bf16[512,5120]{1,0:T(8,128)(2,1)S(1)} fusion(f32[512,5120]{1,0:T(8,128)} %fusion.75, bf16[512,320]{0,1:T(8,128)(2,1)} %copy-done.18, bf16[320,5120]{1,0:T(8,128)(2,1)S(1)} %copy-done), kind=kOutput, calls=%fused_computation.5 | convolution fusion | flops 1682964480 | bytes 19333120 | tf_op jit(solution)/shard_map/dot_general | solution.py:137
  223.3 2.9 copy.138
  226.2 4.9 %all-to-all-start = ((bf16[512,8,640]{2,0,1:T(8,128)(2,1)}), bf16[512,8,640]{2,0,1:T(8,128)(2,1)}, u32[]{:S(2)}, u32[]{:S(2)}) async-start(bf16[512,8,640]{2,0,1:T(8,128)(2,1)} %bitcast.105), calls=%async_computation | async-start | bytes 10485760 | tf_op jit(solution)/shard_map/all_to_all | solution.py:47
  231.1 4.1 convolution_convert_fusion.1
  235.2 2.8 copy.137
  238.0 66.6 %all-to-all-done = bf16[512,8,640]{2,0,1:T(8,128)(2,1)} async-done(((bf16[512,8,640]{2,0,1:T(8,128)(2,1)}), bf16[512,8,640]{2,0,1:T(8,128)(2,1)}, u32[]{:S(2)}, u32[]{:S(2)}) %all-to-all-start) | async-done | bytes 5242912 | tf_op jit(solution)/shard_map/all_to_all | solution.py:47
  304.6 10.6 %all-to-all-start.1 = ((bf16[512,8,640]{2,0,1:T(8,128)(2,1)}), bf16[512,8,640]{2,0,1:T(8,128)(2,1)}, u32[]{:S(2)}, u32[]{:S(2)}) async-start(bf16[512,8,640]{2,0,1:T(8,128)(2,1)} %bitcast.104), calls=%async_computation.1 | async-start | bytes 10485760 | tf_op jit(solution)/shard_map/all_to_all | solution.py:47
  315.2 8.8 %convolution_convert_fusion.2 = bf16[512,640]{1,0:T(8,128)(2,1)S(1)} fusion(bf16[512,5120]{1,0:T(8,128)(2,1)} %bitcast.109, bf16[640,5120]{1,0:T(8,128)(2,1)} %param.17), kind=kOutput, calls=%fused_computation.45 | convolution fusion | flops 3355770880 | bytes 12451840 | tf_op jit(solution)/shard_map/dot_general | solution.py:38
  325.3 5.0 %fusion.30 = f32[2,5,128,768]{3,2,1,0:T(8,128)S(1)} fusion(bf16[2,256,5,128]{1,3,2,0:T(8,128)(2,1)S(1)} %copy.111, f32[2,5,256,768]{2,3,1,0:T(8,128)} %copy-done.26, f32[2,5,256]{2,1,0:T(8,128)S(1)} %get-tuple-element.50), kind=kOutput, calls=%fused_computation.37 | convolution fusion | flops 507248640 | bytes 12462080 | tf_op jit(solution)/shard_map/shqk,sqhe->skhe/dot_general | solution.py:178
  333.3 4.3 fusion.35
  337.6 14.6 %fusion.11 = f32[2,5,768,128]{2,3,1,0:T(8,128)} fusion(bf16[2,256,5,128]{1,3,2,0:T(8,128)(2,1)S(1)} %bitcast.119, f32[2,5,256,768]{2,3,1,0:T(8,128)} %fusion.35, f32[2,5,256,768]{2,3,1,0:T(8,128)} %copy-done.26, f32[2,5,256]{2,1,0:T(8,128)S(1)} %get-tuple-element.50), kind=kOutput, calls=%fused_computation.19 | convolution fusion | flops 517082368 | bytes 20326400 | tf_op jit(solution)/shard_map/shqk,sqhe->skhe/dot_general | solution.py:191
  361.4 13.9 %fusion.39 = bf16[2,5,128,256]{3,2,1,0:T(8,128)(2,1)} fusion(f32[2,5,256,768]{2,3,1,0:T(8,128)} %fusion.35, bf16[2,256,5,128]{3,1,2,0:T(8,128)(2,1)S(1)} %copy-done.4, bf16[2,256,5,128]{3,1,2,0:T(8,128)(2,1)S(1)} %copy-done.10, bf16[2,256,5,128]{3,1,2,0:T(8,128)(2,1)S(1)} %copy-done.12, f32[2,5,256,768]{2,3,1,0:T(8,128)} %copy-done.26, ...), kind=kOutput, calls=%fused_computation.44 | convolution fusion | flops 523308288 | bytes 18360320 | tf_op jit(solution)/shard_map/shqk,skhe->sqhe/dot_general | solution.py:187
  383.2 3.3 convert_reduce_fusion.1
  387.5 3.5 convert_reduce_fusion
  393.1 55.3 %reduce-scatter.2.cloned.1.call-done = bf16[320,1280]{1,0:T(8,128)(2,1)} async-done(((bf16[5120,1280]{1,0:T(8,128)(2,1)}), bf16[320,1280]{1,0:T(8,128)(2,1)}) %reduce-scatter.2.cloned.1.call-update) | async-done | bytes 819216 | tf_op jit(solution)/shard_map/reduce_scatter | solution.py:163
  (118 shorter events, 75.4 us)
Async XLA Ops:
  7.2 154.6 %copy-start = (bf16[320,5120]{1,0:T(8,128)(2,1)S(1)}, bf16[320,5120]{1,0:T(8,128)(2,1)}, u32[]{:S(2)}) copy-start(bf16[320,5120]{1,0:T(8,128)(2,1)} %param.19) | copy-start | bytes 9830404
  7.2 20.7 %copy-start.24 = (bf16[128,320]{0,1:T(8,128)(2,1)S(1)}, bf16[128,320]{0,1:T(8,128)(2,1)}, u32[]{:S(2)}) copy-start(bf16[128,320]{0,1:T(8,128)(2,1)} %param.20) | copy-start | bytes 245764
  7.2 20.7 %copy-start.25 = (s32[1,4]{1,0:T(1,128)S(1)}, s32[1,4]{1,0:T(1,128)}, u32[]{:S(2)}) copy-start(s32[1,4]{1,0:T(1,128)} %param.21) | copy-start | bytes 52
  7.2 135.1 %all-gather.2.cloned.1.call-start = ((), (), s32[]{:S(2)}) async-start(), calls=%async_computation.4 | async-start | bytes 11796480 | tf_op jit(solution)/shard_map/all_gather | solution.py:74
  9.9 438.5 %reduce-scatter.2.cloned.1.call-start = ((), (), s32[]{:S(2)}) async-start(), calls=%async_computation.5 | async-start | bytes 13926400 | tf_op jit(solution)/shard_map/reduce_scatter | solution.py:163
  12.1 16.0 %collective-permute-start.1 = (bf16[2,256,640]{1,2,0:T(8,128)(2,1)}, bf16[2,256,640]{1,2,0:T(8,128)(2,1)}, u32[]{:S(2)}, u32[]{:S(2)}) collective-permute-start(bf16[2,256,640]{1,2,0:T(8,128)(2,1)} %bitcast.137), channel_id=1, source_target_pairs={{0,8},{8,16},{16,24},{24,32},{32,40},{40,48},{48,56},{56,64},{64,7... | collective-permute-start | bytes 1966088 | tf_op jit(solution)/shard_map/ppermute | solution.py:16
  14.3 18.8 %collective-permute-start = (bf16[2,256,640]{1,2,0:T(8,128)(2,1)}, bf16[2,256,640]{1,2,0:T(8,128)(2,1)}, u32[]{:S(2)}, u32[]{:S(2)}) collective-permute-start(bf16[2,256,640]{1,2,0:T(8,128)(2,1)} %bitcast.138), channel_id=1, source_target_pairs={{0,16},{8,24},{16,32},{24,40},{32,48},{40,56},{48,64},{56,72},{64,... | collective-permute-start | bytes 1966088 | tf_op jit(solution)/shard_map/ppermute | solution.py:16
  161.8 5.0 %copy-start.18 = (bf16[512,320]{0,1:T(8,128)(2,1)}, bf16[512,320]{0,1:T(8,128)(2,1)S(1)}, u32[]{:S(2)}) copy-start(bf16[512,320]{0,1:T(8,128)(2,1)S(1)} %multiply_convert_fusion.1) | copy-start | bytes 983044
  161.8 5.6 %copy-start.8 = (bf16[80,8,2,256]{3,1,2,0:T(8,128)(2,1)S(1)}, bf16[80,8,2,256]{3,1,2,0:T(8,128)(2,1)}, u32[]{:S(2)}) copy-start(bf16[80,8,2,256]{3,1,2,0:T(8,128)(2,1)} %copy.134) | copy-start | bytes 1966084
  213.0 13.2 %all-to-all-start.2 = ((bf16[16,8,320]{2,1,0:T(8,128)(2,1)}), bf16[16,8,320]{2,1,0:T(8,128)(2,1)S(1)}, u32[]{:S(2)}, u32[]{:S(2)}) async-start(bf16[16,8,320]{2,1,0:T(8,128)(2,1)} %bitcast.39), calls=%async_computation.3 | async-start | bytes 196608 | tf_op jit(solution)/shard_map/all_to_all | solution.py:164
  226.2 4.9 %copy-start.2 = (bf16[5120,320]{0,1:T(8,128)(2,1)S(1)}, bf16[5120,320]{0,1:T(8,128)(2,1)}, u32[]{:S(2)}) copy-start(bf16[5120,320]{0,1:T(8,128)(2,1)} %param.18) | copy-start | bytes 9830404
  226.2 78.4 %all-to-all-start = ((bf16[512,8,640]{2,0,1:T(8,128)(2,1)}), bf16[512,8,640]{2,0,1:T(8,128)(2,1)}, u32[]{:S(2)}, u32[]{:S(2)}) async-start(bf16[512,8,640]{2,0,1:T(8,128)(2,1)} %bitcast.105), calls=%async_computation | async-start | bytes 10485760 | tf_op jit(solution)/shard_map/all_to_all | solution.py:47
  304.6 82.9 %all-to-all-start.1 = ((bf16[512,8,640]{2,0,1:T(8,128)(2,1)}), bf16[512,8,640]{2,0,1:T(8,128)(2,1)}, u32[]{:S(2)}, u32[]{:S(2)}) async-start(bf16[512,8,640]{2,0,1:T(8,128)(2,1)} %bitcast.104), calls=%async_computation.1 | async-start | bytes 10485760 | tf_op jit(solution)/shard_map/all_to_all | solution.py:47
  325.3 8.0 %copy-start.7 = (bf16[1,2,256,640]{2,3,1,0:T(8,128)(2,1)S(1)}, bf16[1,2,256,640]{2,3,1,0:T(8,128)(2,1)}, u32[]{:S(2)}) copy-start(bf16[1,2,256,640]{2,3,1,0:T(8,128)(2,1)} %copy.84) | copy-start | bytes 1966084
  325.3 7.9 %copy-start.14 = (bf16[2,256,5,128]{1,3,2,0:T(8,128)(2,1)S(1)}, bf16[2,256,5,128]{1,3,2,0:T(8,128)(2,1)}, u32[]{:S(2)}) copy-start(bf16[2,256,5,128]{1,3,2,0:T(8,128)(2,1)} %copy-done.13) | copy-start | bytes 1966084
  325.3 7.9 %copy-start.16 = (bf16[2,256,5,128]{1,3,2,0:T(8,128)(2,1)S(1)}, bf16[2,256,5,128]{1,3,2,0:T(8,128)(2,1)}, u32[]{:S(2)}) copy-start(bf16[2,256,5,128]{1,3,2,0:T(8,128)(2,1)} %copy-done.15) | copy-start | bytes 1966084
  337.6 16.7 %copy-start.21 = (bf16[256,640]{0,1:T(8,128)(2,1)S(1)}, bf16[256,640]{0,1:T(8,128)(2,1)}, u32[]{:S(2)}) copy-start(bf16[256,640]{0,1:T(8,128)(2,1)} %get-tuple-element.43) | copy-start | bytes 983044
  337.6 18.9 %copy-start.20 = (bf16[256,640]{0,1:T(8,128)(2,1)S(1)}, bf16[256,640]{0,1:T(8,128)(2,1)}, u32[]{:S(2)}) copy-start(bf16[256,640]{0,1:T(8,128)(2,1)} %get-tuple-element.42) | copy-start | bytes 983044
  352.1 9.3 %copy-start.4 = (bf16[2,256,5,128]{3,1,2,0:T(8,128)(2,1)S(1)}, bf16[2,256,5,128]{3,1,2,0:T(8,128)(2,1)}, u32[]{:S(2)}) copy-start(bf16[2,256,5,128]{3,1,2,0:T(8,128)(2,1)} %copy.88) | copy-start | bytes 1966084
  352.1 9.3 %copy-start.10 = (bf16[2,256,5,128]{3,1,2,0:T(8,128)(2,1)S(1)}, bf16[2,256,5,128]{3,1,2,0:T(8,128)(2,1)}, u32[]{:S(2)}) copy-start(bf16[2,256,5,128]{3,1,2,0:T(8,128)(2,1)} %copy-done.9) | copy-start | bytes 1966084
  352.1 9.3 %copy-start.12 = (bf16[2,256,5,128]{3,1,2,0:T(8,128)(2,1)S(1)}, bf16[2,256,5,128]{3,1,2,0:T(8,128)(2,1)}, u32[]{:S(2)}) copy-start(bf16[2,256,5,128]{3,1,2,0:T(8,128)(2,1)} %copy-done.11) | copy-start | bytes 1966084
  355.2 25.1 %collective-permute-start.3 = (bf16[2,256,640]{1,2,0:T(8,128)(2,1)}, bf16[2,256,640]{1,2,0:T(8,128)(2,1)}, u32[]{:S(2)}, u32[]{:S(2)}) collective-permute-start(bf16[2,256,640]{1,2,0:T(8,128)(2,1)} %pad_maximum_fusion.14), channel_id=1, source_target_pairs={{16,0},{24,8},{32,16},{40,24},{48,32},{56,40},{64,48},{72,56},{80,... | collective-permute-start | bytes 1966088 | tf_op jit(solution)/shard_map/ppermute | solution.py:16
  357.4 22.9 %collective-permute-start.2 = (bf16[2,256,640]{1,2,0:T(8,128)(2,1)}, bf16[2,256,640]{1,2,0:T(8,128)(2,1)}, u32[]{:S(2)}, u32[]{:S(2)}) collective-permute-start(bf16[2,256,640]{1,2,0:T(8,128)(2,1)} %pad_maximum_fusion.13), channel_id=1, source_target_pairs={{8,0},{16,8},{24,16},{32,24},{40,32},{48,40},{56,48},{64,56},{72,6... | collective-permute-start | bytes 1966088 | tf_op jit(solution)/shard_map/ppermute | solution.py:16
  387.5 67.8 %copy-start.1 = (bf16[320,5120]{1,0:T(8,128)(2,1)S(1)}, bf16[320,5120]{1,0:T(8,128)(2,1)}, u32[]{:S(2)}) copy-start(bf16[320,5120]{1,0:T(8,128)(2,1)} %param.19) | copy-start | bytes 9830404
  (12 other events, 31.7 us)
Sparse Core Ops, SparseCore 0:
  10.2 131.9 all-gather.1
  196.0 252.3 reduce-scatter.1

commit v5 on v4

--- a/solution.py
+++ b/solution.py
@@ -38,6 +38,22 @@
     return lax.dot_general(
         left, right, (((1,), (1,)), ((), ())), preferred_element_type=jnp.float32
     )
+
+
+TM = ("tmo", "core")
+
+
+def two_stage_scatter(terms):
+    outer = lax.axis_size("tmo")
+    pairs = lax.axis_size("core")
+    side = lax.axis_index("core")
+    rows, width = terms.shape
+    split = terms.reshape(outer, pairs, rows // (outer * pairs), width)
+    given = lax.dynamic_index_in_dim(split, pairs - 1 - side, axis=1, keepdims=False)
+    kept = lax.dynamic_index_in_dim(split, side, axis=1, keepdims=False)
+    got = lax.ppermute(given, "core", [(0, 1), (1, 0)])
+    paired = (kept.astype(jnp.float32) + got.astype(jnp.float32)).astype(jnp.bfloat16)
+    return lax.psum_scatter(paired, "tmo", scatter_dimension=0, tiled=True)[0]
 
 
 def sum_over_groups(partial, steps_here, tokens_here):
@@ -77,8 +93,8 @@
     input_rows = full_both[0].reshape(row_count, model_width)
     grad_rows = full_both[1].reshape(row_count, model_width)
     own_cache = clean_cache[0]
-    nearer = from_behind(own_cache, "tm", 1)
-    farther = from_behind(own_cache, "tm", 2)
+    nearer = from_behind(own_cache, TM, 1)
+    farther = from_behind(own_cache, TM, 2)
     reach = offsets[0]
     allowed = jnp.concatenate(
         [
@@ -141,7 +157,7 @@
     layer_out = (hidden_in.astype(jnp.float32) + layer_sum).astype(jnp.bfloat16)
     attended_grad = contract_cols(grad_rows, out_proj).astype(jnp.bfloat16)
     pre_grad = (contract_cols(grad_rows, branch_out) * gelu_slope(pre_act)).astype(jnp.bfloat16)
-    tm_count = lax.axis_size("tm")
+    tm_count = lax.axis_size(TM)
     grouped = jnp.sum(
         pre_grad.reshape(
             steps_here, action_count, tokens_here // action_count, branch_width
@@ -160,9 +176,9 @@
         full_both.reshape(2 * row_count, model_width),
         jnp.concatenate([input_side, grad_side], axis=0),
     ).astype(jnp.bfloat16)
-    merged = lax.psum_scatter(terms, "tm", scatter_dimension=0, tiled=True).astype(jnp.float32)
+    merged = two_stage_scatter(terms).astype(jnp.float32)
     table_blocks = lax.all_to_all(
-        table_term.astype(jnp.bfloat16).reshape(tm_count, -1, branch_width), "tm", 0, 0, tiled=True
+        table_term.astype(jnp.bfloat16).reshape(tm_count, -1, branch_width), TM, 0, 0, tiled=True
     )
     summed = (
         merged[:, :head_cols].T,
@@ -203,8 +219,8 @@
             jnp.sum(value_all[:, tokens_here : 2 * tokens_here], axis=0),
         ]
     )
-    from_next = from_behind(toward_near.astype(jnp.bfloat16), "tm", -1).astype(toward_near.dtype)
-    from_after = from_behind(toward_far.astype(jnp.bfloat16), "tm", -2).astype(toward_far.dtype)
+    from_next = from_behind(toward_near.astype(jnp.bfloat16), TM, -1).astype(toward_near.dtype)
+    from_after = from_behind(toward_far.astype(jnp.bfloat16), TM, -2).astype(toward_far.dtype)
     received = from_next + from_after
     attention_grads = (query_grad, own_key, own_value, received[None])
     summed, input_grad = weight_grads
@@ -250,4 +266,15 @@
         P("tensor", "tm"),
         P("tm", "tensor"),
     )
-    return jax.shard_map(body, mesh=mesh, in_specs=in_specs, out_specs=out_specs, check_vma=False)
+    shape = mesh.devices.shape
+    inner = jax.sharding.Mesh(
+        mesh.devices.reshape(shape[0] // 2, 2, shape[1]), ("tmo", "core", "tensor")
+    )
+    swap = lambda spec: P(*[TM if part == "tm" else part for part in spec])
+    return jax.shard_map(
+        body,
+        mesh=inner,
+        in_specs=tuple(swap(s) for s in in_specs),
+        out_specs=tuple(swap(s) for s in out_specs),
+        check_vma=False,
+    )

time: 469 us -> 458 us (0.977)
  waiting for transfers between devices: 215 us -> 187 us
  other arithmetic: 26 us -> 35.2 us
  starting transfers between devices: 28.1 us -> 34.4 us
    reduce_scatter x1, waiting for transfers between devices: 55.3 us -> 22.8 us  [two_stage_scatter(): return lax.psum_scatter(paired, 'tmo', scatter_dimension=0, tiled=True)[0]]
    ppermute x0 -> x1, waiting for transfers between devices: none -> 10.9 us  [two_stage_scatter(): got = lax.ppermute(given, 'core', [(0, 1), (1, 0)])]
    convert_element_type x1 -> x2, other arithmetic: 1.25 us -> 10.4 us  [the longest x1 9.17 us: two_stage_scatter(): (kept.astype(jnp.float32) + got.astype(jnp.float32)).astype(jnp.bfloat16)]
    all_to_all x2, starting transfers between devices: 15.5 us -> 21.9 us  [sum_over_groups(): received = lax.all_to_all(blocks, 'tensor', 1, 1, tiled=True)]
    all_to_all x2, waiting for transfers between devices: 66.6 us -> 60.5 us  [sum_over_groups(): received = lax.all_to_all(blocks, 'tensor', 1, 1, tiled=True)]
    squeeze x0 -> x1, local copies, waits for them, and re-layouts: none -> 5.98 us  [two_stage_scatter(): lax.dynamic_index_in_dim(split, pairs - 1 - side, axis=1, keepdims=False)]
  transfers between devices with their start and end apart: 9 -> 10, of which waited for: 4 -> 5; matrix products, arithmetic and copies ran while one was open for 29% -> 30% of each run, Pallas kernels for 0% -> 0%
where the time goes in v5:
time: 458 us; the launch traced here: 452 us
  waiting for transfers between devices  187 us (41%)
  matrix products  113 us (25%)
  local copies, waits for them, and re-layouts  67.1 us (15%)
  other arithmetic  35.2 us (8%)
  starting transfers between devices  34.4 us (8%)
  between operations  15.4 us (3%)
    all_gather x1, waiting for transfers between devices, body(): lax.all_gather(jnp.concatenate([hidden_in, out_grad], axis=0), 'tensor',...  91.8 us
    all_to_all x2, waiting for transfers between devices, sum_over_groups(): received = lax.all_to_all(blocks, 'tensor', 1, 1, tiled=True)  60.5 us
    dot_general x1, matrix products, contract_rows(): lax.dot_general(left, right, (((0,), (0,)), ((), ())), preferred_element_...  28.6 us
    reduce_scatter x1, waiting for transfers between devices, two_stage_scatter(): return lax.psum_scatter(paired, 'tmo', scatter_dimension=0, tiled=True)[0]  22.8 us
    unnamed x64, local copies, waits for them, and re-layouts  22.5 us
    all_to_all x2, starting transfers between devices, sum_over_groups(): received = lax.all_to_all(blocks, 'tensor', 1, 1, tiled=True)  21.9 us
    dot_general x3, matrix products, contract_cols(): lax.dot_general(left, right, (((1,), (1,)), ((), ())), preferred_element_...  17.8 us
    dot_general x1, matrix products, body(): jnp.einsum('shqk,sqhe->skhe', score_grad, query_heads, preferred_element_...  14.2 us
  transfers between devices with their start and end apart: 10, of which 5 were waited for; matrix products, arithmetic and copies ran while one was open for 30% of the time, Pallas kernels for 0%

profile of v5, /device:TPU:0, one launch (start us, length us, event | category | flops | bytes accessed | tf_op | source)
XLA Modules:
  0.0 451.7 jit_solution(7921665048019111369)
XLA Ops:
  14.3 4.3 collective-permute-start
  50.5 91.8 %all-gather.2.cloned.1.call-done = bf16[2,2,256,5120]{3,2,1,0:T(8,128)(2,1)} async-done(((bf16[2,2,256,640]{3,2,1,0:T(8,128)(2,1)}), bf16[2,2,256,5120]{3,2,1,0:T(8,128)(2,1)}) %all-gather.2.cloned.1.call-update) | async-done | bytes 10485776 | tf_op jit(solution)/shard_map/all_gather | solution.py:90
  142.3 8.9 %fusion.72 = (bf16[1,2,256,5120]{3,2,1,0:T(8,128)(2,1)}, bf16[1,2,256,5120]{3,2,1,0:T(8,128)(2,1)}) fusion(bf16[2,2,256,5120]{3,2,1,0:T(8,128)(2,1)} %all-gather.2.cloned.1.call-done), kind=kLoop, calls=%fused_computation.101 | loop fusion | bytes 20971520 | tf_op jit(solution)/shard_map/slice | solution.py:94
  151.1 7.3 %fusion.47 = f32[2,4,64,320]{3,2,1,0:T(8,128)} fusion(bf16[2,4,64,5120]{3,2,1,0:T(8,128)(2,1)} %bitcast.123, bf16[5120,320]{0,1:T(8,128)(2,1)} %param.18, f32[4,320]{1,0:T(4,128)S(1)} %fusion.56), kind=kOutput, calls=%fused_computation.60 | convolution fusion | flops 1677885440 | bytes 9180160 | tf_op jit(solution)/shard_map/dot_general | solution.py:146
  162.0 4.9 %fusion.50 = bf16[512,320]{0,1:T(8,128)(2,1)S(1)} fusion(bf16[512,5120]{1,0:T(8,128)(2,1)} %bitcast.121, bf16[320,5120]{1,0:T(8,128)(2,1)S(1)} %copy-done, f32[512,320]{0,1:T(8,128)} %copy.99), kind=kOutput, calls=%fused_computation.61 | convolution fusion | flops 1680834560 | bytes 9502720 | tf_op jit(solution)/shard_map/dot_general | solution.py:38
  166.9 28.6 %convolution_convert_fusion = bf16[5120,1280]{1,0:T(8,128)(2,1)} fusion(bf16[1024,5120]{1,0:T(8,128)(2,1)} %bitcast.120, bf16[512,320]{0,1:T(8,128)(2,1)S(1)} %fusion.50, bf16[512,320]{0,1:T(8,128)(2,1)S(1)} %broadcast_in_dim.76, bf16[512,320]{0,1:T(8,128)(2,1)S(1)} %multiply_convert_fusion.1, bf16[512,640]{0,1:T(8,128)(2,1)S(1)} %bitcast.136), kind=kOutput, calls=%fused_computation.2 | convolution fusion | flops 13441433600 | bytes 25231360 | tf_op jit(solution)/shard_map/dot_general | solution.py:32
  195.5 6.0 %dynamic-slice_bitcast_fusion = bf16[8,320,1280]{2,1,0:T(8,128)(2,1)} fusion(bf16[8,2,320,1280]{3,2,1,0:T(8,128)(2,1)} %bitcast.118, s32[]{:T(128)S(6)} %select_n.17), kind=kLoop, calls=%fused_computation.17 | loop fusion | bytes 13107204 | tf_op jit(solution)/shard_map/jit(dynamic_index_in_dim)/squeeze | solution.py:52
  201.5 10.9 %collective-permute-done.4 = bf16[8,320,1280]{2,1,0:T(8,128)(2,1)} collective-permute-done((bf16[8,320,1280]{2,1,0:T(8,128)(2,1)}, bf16[8,320,1280]{2,1,0:T(8,128)(2,1)}, u32[]{:S(2)}, u32[]{:S(2)}) %collective-permute-start.4) | collective-permute-done | bytes 6553632 | tf_op jit(solution)/shard_map/ppermute | solution.py:54
  212.4 9.2 %fusion.2 = bf16[8,320,1280]{2,1,0:T(8,128)(2,1)} fusion(bf16[8,320,1280]{2,1,0:T(8,128)(2,1)} %collective-permute-done.4, bf16[8,2,320,1280]{3,2,1,0:T(8,128)(2,1)} %bitcast.119, s32[]{:T(128)S(6)} %select_n.16), kind=kLoop, calls=%fused_computation.4 | loop fusion | flops 13107200 | bytes 19660804 | tf_op jit(solution)/shard_map/convert_element_type | solution.py:55
  221.6 11.4 %fusion.76 = f32[512,5120]{1,0:T(8,128)} fusion(bf16[512,640]{0,1:T(8,128)(2,1)} %bitcast.135, bf16[640,5120]{1,0:T(8,128)(2,1)} %param.17), kind=kOutput, calls=%fused_computation.105 | convolution fusion | flops 3355443200 | bytes 17694720 | tf_op jit(solution)/shard_map/dot_general | solution.py:153
  237.3 3.5 all-to-all-start.2
  240.8 6.0 %add_convert_fusion = bf16[512,5120]{1,0:T(8,128)(2,1)S(1)} fusion(f32[512,5120]{1,0:T(8,128)} %fusion.76, bf16[512,320]{0,1:T(8,128)(2,1)} %copy-done.18, bf16[320,5120]{1,0:T(8,128)(2,1)S(1)} %copy-done), kind=kOutput, calls=%fused_computation.7 | convolution fusion | flops 1682964480 | bytes 19333120 | tf_op jit(solution)/shard_map/dot_general | solution.py:153
  249.5 5.0 %all-to-all-start = ((bf16[512,8,640]{2,0,1:T(8,128)(2,1)}), bf16[512,8,640]{2,0,1:T(8,128)(2,1)}, u32[]{:S(2)}, u32[]{:S(2)}) async-start(bf16[512,8,640]{2,0,1:T(8,128)(2,1)} %bitcast.116), calls=%async_computation | async-start | bytes 10485760 | tf_op jit(solution)/shard_map/all_to_all | solution.py:63
  254.5 4.1 convolution_convert_fusion.1
  261.5 60.5 %all-to-all-done = bf16[512,8,640]{2,0,1:T(8,128)(2,1)} async-done(((bf16[512,8,640]{2,0,1:T(8,128)(2,1)}), bf16[512,8,640]{2,0,1:T(8,128)(2,1)}, u32[]{:S(2)}, u32[]{:S(2)}) %all-to-all-start) | async-done | bytes 5242912 | tf_op jit(solution)/shard_map/all_to_all | solution.py:63
  321.9 16.9 %all-to-all-start.1 = ((bf16[512,8,640]{2,0,1:T(8,128)(2,1)}), bf16[512,8,640]{2,0,1:T(8,128)(2,1)}, u32[]{:S(2)}, u32[]{:S(2)}) async-start(bf16[512,8,640]{2,0,1:T(8,128)(2,1)} %bitcast.115), calls=%async_computation.1 | async-start | bytes 10485760 | tf_op jit(solution)/shard_map/all_to_all | solution.py:63
  338.8 8.8 %convolution_convert_fusion.2 = bf16[512,640]{1,0:T(8,128)(2,1)S(1)} fusion(bf16[512,5120]{1,0:T(8,128)(2,1)} %bitcast.122, bf16[640,5120]{1,0:T(8,128)(2,1)} %param.17), kind=kOutput, calls=%fused_computation.48 | convolution fusion | flops 3355770880 | bytes 12451840 | tf_op jit(solution)/shard_map/dot_general | solution.py:38
  349.0 5.2 %fusion.31 = f32[2,5,128,768]{3,2,1,0:T(8,128)S(1)} fusion(bf16[2,256,5,128]{1,3,2,0:T(8,128)(2,1)S(1)} %copy.117, f32[2,5,256,768]{2,3,1,0:T(8,128)} %copy-done.26, f32[2,5,256]{2,1,0:T(8,128)S(1)} %get-tuple-element.52), kind=kOutput, calls=%fused_computation.40 | convolution fusion | flops 507248640 | bytes 12462080 | tf_op jit(solution)/shard_map/shqk,sqhe->skhe/dot_general | solution.py:194
  357.2 4.3 fusion.36
  361.5 14.2 %fusion.12 = f32[2,5,768,128]{2,3,1,0:T(8,128)} fusion(bf16[2,256,5,128]{1,3,2,0:T(8,128)(2,1)S(1)} %bitcast.132, f32[2,5,256,768]{2,3,1,0:T(8,128)} %fusion.36, f32[2,5,256,768]{2,3,1,0:T(8,128)} %copy-done.26, f32[2,5,256]{2,1,0:T(8,128)S(1)} %get-tuple-element.52), kind=kOutput, calls=%fused_computation.22 | convolution fusion | flops 517082368 | bytes 20326400 | tf_op jit(solution)/shard_map/shqk,sqhe->skhe/dot_general | solution.py:207
  385.0 13.7 %fusion.40 = bf16[2,5,128,256]{3,2,1,0:T(8,128)(2,1)} fusion(f32[2,5,256,768]{2,3,1,0:T(8,128)} %fusion.36, bf16[2,256,5,128]{3,1,2,0:T(8,128)(2,1)S(1)} %copy-done.4, bf16[2,256,5,128]{3,1,2,0:T(8,128)(2,1)S(1)} %copy-done.10, bf16[2,256,5,128]{3,1,2,0:T(8,128)(2,1)S(1)} %copy-done.12, f32[2,5,256,768]{2,3,1,0:T(8,128)} %copy-done.26, ...), kind=kOutput, calls=%fused_computation.47 | convolution fusion | flops 523308288 | bytes 18360320 | tf_op jit(solution)/shard_map/shqk,skhe->sqhe/dot_general | solution.py:203
  406.6 3.4 convert_reduce_fusion.1
  411.0 3.5 convert_reduce_fusion
  416.6 22.8 %reduce-scatter.2.cloned.1.call-done = bf16[1,320,1280]{2,1,0:T(8,128)(2,1)} async-done(((bf16[8,320,1280]{2,1,0:T(8,128)(2,1)}), bf16[1,320,1280]{2,1,0:T(8,128)(2,1)}) %reduce-scatter.2.cloned.1.call-update) | async-done | bytes 819216 | tf_op jit(solution)/shard_map/reduce_scatter | solution.py:56
  (121 shorter events, 81.4 us)
Async XLA Ops:
  7.2 154.8 %copy-start = (bf16[320,5120]{1,0:T(8,128)(2,1)S(1)}, bf16[320,5120]{1,0:T(8,128)(2,1)}, u32[]{:S(2)}) copy-start(bf16[320,5120]{1,0:T(8,128)(2,1)} %param.19) | copy-start | bytes 9830404
  7.2 20.7 %copy-start.24 = (bf16[128,320]{0,1:T(8,128)(2,1)S(1)}, bf16[128,320]{0,1:T(8,128)(2,1)}, u32[]{:S(2)}) copy-start(bf16[128,320]{0,1:T(8,128)(2,1)} %param.20) | copy-start | bytes 245764
  7.2 20.7 %copy-start.25 = (s32[1,4]{1,0:T(1,128)S(1)}, s32[1,4]{1,0:T(1,128)}, u32[]{:S(2)}) copy-start(s32[1,4]{1,0:T(1,128)} %param.21) | copy-start | bytes 52
  7.2 135.1 %all-gather.2.cloned.1.call-start = ((), (), s32[]{:S(2)}) async-start(), calls=%async_computation.4 | async-start | bytes 11796480 | tf_op jit(solution)/shard_map/all_gather | solution.py:90
  9.9 429.5 %reduce-scatter.2.cloned.1.call-start = ((), (), s32[]{:S(2)}) async-start(), calls=%async_computation.5 | async-start | bytes 7372800 | tf_op jit(solution)/shard_map/reduce_scatter | solution.py:56
  12.1 16.0 %collective-permute-start.1 = (bf16[2,256,640]{1,2,0:T(8,128)(2,1)}, bf16[2,256,640]{1,2,0:T(8,128)(2,1)}, u32[]{:S(2)}, u32[]{:S(2)}) collective-permute-start(bf16[2,256,640]{1,2,0:T(8,128)(2,1)} %bitcast.150), channel_id=1, source_target_pairs={{0,8},{8,16},{16,24},{24,32},{32,40},{40,48},{48,56},{56,64},{64,7... | collective-permute-start | bytes 1966088 | tf_op jit(solution)/shard_map/ppermute | solution.py:16
  14.3 18.8 %collective-permute-start = (bf16[2,256,640]{1,2,0:T(8,128)(2,1)}, bf16[2,256,640]{1,2,0:T(8,128)(2,1)}, u32[]{:S(2)}, u32[]{:S(2)}) collective-permute-start(bf16[2,256,640]{1,2,0:T(8,128)(2,1)} %bitcast.151), channel_id=1, source_target_pairs={{0,16},{8,24},{16,32},{24,40},{32,48},{40,56},{48,64},{56,72},{64,... | collective-permute-start | bytes 1966088 | tf_op jit(solution)/shard_map/ppermute | solution.py:16
  166.9 28.6 %copy-start.19 = (bf16[512,320]{0,1:T(8,128)(2,1)}, bf16[512,320]{0,1:T(8,128)(2,1)S(1)}, u32[]{:S(2)}) copy-start(bf16[512,320]{0,1:T(8,128)(2,1)S(1)} %fusion.50) | copy-start | bytes 983044
  201.5 10.9 %collective-permute-start.4 = (bf16[8,320,1280]{2,1,0:T(8,128)(2,1)}, bf16[8,320,1280]{2,1,0:T(8,128)(2,1)}, u32[]{:S(2)}, u32[]{:S(2)}) collective-permute-start(bf16[8,320,1280]{2,1,0:T(8,128)(2,1)} %dynamic-slice_bitcast_fusion), channel_id=1, source_target_pairs={{0,8},{8,0},{1,9},{9,1},{2,10},{10,2},{3,11},{11,3},{4,12},{12,4},... | collective-permute-start | bytes 19660808 | tf_op jit(solution)/shard_map/ppermute | solution.py:54
  237.3 12.3 %all-to-all-start.2 = ((bf16[16,8,320]{2,1,0:T(8,128)(2,1)}), bf16[16,8,320]{2,1,0:T(8,128)(2,1)S(1)}, u32[]{:S(2)}, u32[]{:S(2)}) async-start(bf16[16,8,320]{2,1,0:T(8,128)(2,1)} %bitcast.44), calls=%async_computation.3 | async-start | bytes 196608 | tf_op jit(solution)/shard_map/all_to_all | solution.py:180
  249.5 5.0 %copy-start.2 = (bf16[5120,320]{0,1:T(8,128)(2,1)S(1)}, bf16[5120,320]{0,1:T(8,128)(2,1)}, u32[]{:S(2)}) copy-start(bf16[5120,320]{0,1:T(8,128)(2,1)} %param.18) | copy-start | bytes 9830404
  249.5 72.4 %all-to-all-start = ((bf16[512,8,640]{2,0,1:T(8,128)(2,1)}), bf16[512,8,640]{2,0,1:T(8,128)(2,1)}, u32[]{:S(2)}, u32[]{:S(2)}) async-start(bf16[512,8,640]{2,0,1:T(8,128)(2,1)} %bitcast.116), calls=%async_computation | async-start | bytes 10485760 | tf_op jit(solution)/shard_map/all_to_all | solution.py:63
  321.9 89.1 %all-to-all-start.1 = ((bf16[512,8,640]{2,0,1:T(8,128)(2,1)}), bf16[512,8,640]{2,0,1:T(8,128)(2,1)}, u32[]{:S(2)}, u32[]{:S(2)}) async-start(bf16[512,8,640]{2,0,1:T(8,128)(2,1)} %bitcast.115), calls=%async_computation.1 | async-start | bytes 10485760 | tf_op jit(solution)/shard_map/all_to_all | solution.py:63
  348.9 8.3 %copy-start.7 = (bf16[1,2,256,640]{2,3,1,0:T(8,128)(2,1)S(1)}, bf16[1,2,256,640]{2,3,1,0:T(8,128)(2,1)}, u32[]{:S(2)}) copy-start(bf16[1,2,256,640]{2,3,1,0:T(8,128)(2,1)} %copy.90) | copy-start | bytes 1966084
  348.9 8.3 %copy-start.14 = (bf16[2,256,5,128]{1,3,2,0:T(8,128)(2,1)S(1)}, bf16[2,256,5,128]{1,3,2,0:T(8,128)(2,1)}, u32[]{:S(2)}) copy-start(bf16[2,256,5,128]{1,3,2,0:T(8,128)(2,1)} %copy-done.13) | copy-start | bytes 1966084
  348.9 8.3 %copy-start.16 = (bf16[2,256,5,128]{1,3,2,0:T(8,128)(2,1)S(1)}, bf16[2,256,5,128]{1,3,2,0:T(8,128)(2,1)}, u32[]{:S(2)}) copy-start(bf16[2,256,5,128]{1,3,2,0:T(8,128)(2,1)} %copy-done.15) | copy-start | bytes 1966084
  361.5 16.3 %copy-start.21 = (bf16[256,640]{0,1:T(8,128)(2,1)S(1)}, bf16[256,640]{0,1:T(8,128)(2,1)}, u32[]{:S(2)}) copy-start(bf16[256,640]{0,1:T(8,128)(2,1)} %get-tuple-element.43) | copy-start | bytes 983044
  361.5 18.5 %copy-start.20 = (bf16[256,640]{0,1:T(8,128)(2,1)S(1)}, bf16[256,640]{0,1:T(8,128)(2,1)}, u32[]{:S(2)}) copy-start(bf16[256,640]{0,1:T(8,128)(2,1)} %get-tuple-element.42) | copy-start | bytes 983044
  375.7 9.3 %copy-start.4 = (bf16[2,256,5,128]{3,1,2,0:T(8,128)(2,1)S(1)}, bf16[2,256,5,128]{3,1,2,0:T(8,128)(2,1)}, u32[]{:S(2)}) copy-start(bf16[2,256,5,128]{3,1,2,0:T(8,128)(2,1)} %copy.94) | copy-start | bytes 1966084
  375.7 9.3 %copy-start.10 = (bf16[2,256,5,128]{3,1,2,0:T(8,128)(2,1)S(1)}, bf16[2,256,5,128]{3,1,2,0:T(8,128)(2,1)}, u32[]{:S(2)}) copy-start(bf16[2,256,5,128]{3,1,2,0:T(8,128)(2,1)} %copy-done.9) | copy-start | bytes 1966084
  375.7 9.3 %copy-start.12 = (bf16[2,256,5,128]{3,1,2,0:T(8,128)(2,1)S(1)}, bf16[2,256,5,128]{3,1,2,0:T(8,128)(2,1)}, u32[]{:S(2)}) copy-start(bf16[2,256,5,128]{3,1,2,0:T(8,128)(2,1)} %copy-done.11) | copy-start | bytes 1966084
  378.7 24.9 %collective-permute-start.3 = (bf16[2,256,640]{1,2,0:T(8,128)(2,1)}, bf16[2,256,640]{1,2,0:T(8,128)(2,1)}, u32[]{:S(2)}, u32[]{:S(2)}) collective-permute-start(bf16[2,256,640]{1,2,0:T(8,128)(2,1)} %pad_maximum_fusion.14), channel_id=1, source_target_pairs={{16,0},{24,8},{32,16},{40,24},{48,32},{56,40},{64,48},{72,56},{80,... | collective-permute-start | bytes 1966088 | tf_op jit(solution)/shard_map/ppermute | solution.py:16
  380.9 22.8 %collective-permute-start.2 = (bf16[2,256,640]{1,2,0:T(8,128)(2,1)}, bf16[2,256,640]{1,2,0:T(8,128)(2,1)}, u32[]{:S(2)}, u32[]{:S(2)}) collective-permute-start(bf16[2,256,640]{1,2,0:T(8,128)(2,1)} %pad_maximum_fusion.13), channel_id=1, source_target_pairs={{8,0},{16,8},{24,16},{32,24},{40,32},{48,40},{56,48},{64,56},{72,6... | collective-permute-start | bytes 1966088 | tf_op jit(solution)/shard_map/ppermute | solution.py:16
  411.0 33.7 %copy-start.1 = (bf16[320,5120]{1,0:T(8,128)(2,1)S(1)}, bf16[320,5120]{1,0:T(8,128)(2,1)}, u32[]{:S(2)}) copy-start(bf16[320,5120]{1,0:T(8,128)(2,1)} %param.19) | copy-start | bytes 9830404
  (13 other events, 41.4 us)
Sparse Core Ops, SparseCore 0:
  10.2 131.9 all-gather.1
  221.7 217.6 reduce-scatter.1

commit v6 on v5

--- a/solution.py
+++ b/solution.py
@@ -87,11 +87,6 @@
     row_count = steps_here * tokens_here
     action_count = actions.shape[1]
     score_scale = HD ** (-0.5)
-    full_both = lax.all_gather(
-        jnp.concatenate([hidden_in, out_grad], axis=0), "tensor", axis=3, tiled=True
-    )
-    input_rows = full_both[0].reshape(row_count, model_width)
-    grad_rows = full_both[1].reshape(row_count, model_width)
     own_cache = clean_cache[0]
     nearer = from_behind(own_cache, TM, 1)
     farther = from_behind(own_cache, TM, 2)
@@ -135,48 +130,100 @@
     attended = (
         jnp.einsum("shqk,skhe->sqhe", probs_low, value_heads, preferred_element_type=jnp.float32)
         .astype(jnp.bfloat16)
-        .reshape(row_count, head_width)
+        .reshape(steps_here, tokens_here, head_width)
     )
     onehot = (actions[0][:, None] == jnp.arange(action_table.shape[0])[None, :]).astype(
         jnp.bfloat16
     )
     action_rows = jnp.dot(onehot, action_table, preferred_element_type=jnp.float32)
     branch_width = branch_in.shape[1]
-    pre_act = (
-        jnp.dot(input_rows, branch_in, preferred_element_type=jnp.float32).reshape(
-            steps_here, action_count, tokens_here // action_count, branch_width
-        )
-        + action_rows[None, :, None, :]
-    )
-    pre_act = pre_act.reshape(row_count, branch_width)
-    branch_act = gelu_value(pre_act).astype(jnp.bfloat16)
-    partial_value = jnp.dot(attended, out_proj, preferred_element_type=jnp.float32) + jnp.dot(
-        branch_act, branch_out, preferred_element_type=jnp.float32
-    )
-    layer_sum = sum_over_groups(partial_value.astype(jnp.bfloat16), steps_here, tokens_here)
+    run_length = tokens_here // action_count
+    tm_count = lax.axis_size(TM)
+    partials, input_terms, terms, grouped = [], [], None, None
+    query_parts, own_keys, own_values, far_parts, near_parts = [], [], [], [], []
+    gathered = [
+        lax.all_gather(
+            jnp.stack([hidden_in[0, step], out_grad[0, step]]), "tensor", axis=2, tiled=True
+        )
+        for step in range(steps_here)
+    ]
+    for step in range(steps_here):
+        both = gathered[step]
+        pre_act = (
+            jnp.dot(both[0], branch_in, preferred_element_type=jnp.float32).reshape(
+                action_count, run_length, branch_width
+            )
+            + action_rows[:, None, :]
+        ).reshape(tokens_here, branch_width)
+        branch_act = gelu_value(pre_act).astype(jnp.bfloat16)
+        attended_here = attended[step]
+        partials.append(
+            jnp.dot(attended_here, out_proj, preferred_element_type=jnp.float32)
+            + jnp.dot(branch_act, branch_out, preferred_element_type=jnp.float32)
+        )
+        attended_grad = contract_cols(both[1], out_proj).astype(jnp.bfloat16)
+        pre_grad = (contract_cols(both[1], branch_out) * gelu_slope(pre_act)).astype(
+            jnp.bfloat16
+        )
+        input_terms.append(contract_cols(pre_grad, branch_in))
+        head_cols = attended_here.shape[1]
+        input_side = jnp.concatenate(
+            [jnp.zeros((tokens_here, head_cols + branch_width), jnp.bfloat16), pre_grad], axis=1
+        )
+        grad_side = jnp.concatenate(
+            [attended_here, branch_act, jnp.zeros((tokens_here, branch_width), jnp.bfloat16)],
+            axis=1,
+        )
+        term = contract_rows(
+            both.reshape(2 * tokens_here, model_width),
+            jnp.concatenate([input_side, grad_side], axis=0),
+        )
+        terms = term if terms is None else terms + term
+        runs = jnp.sum(
+            pre_grad.reshape(action_count, run_length, branch_width).astype(jnp.float32), axis=1
+        )
+        grouped = runs if grouped is None else grouped + runs
+        window = slice(step, step + 1)
+        grad_heads = attended_grad.reshape(1, tokens_here, heads_here, HD)
+        value_all = jnp.einsum(
+            "shqk,sqhe->skhe", probs_low[window], grad_heads, preferred_element_type=jnp.float32
+        )
+        prob_grad = jnp.einsum(
+            "sqhe,skhe->shqk", grad_heads, value_heads[window], preferred_element_type=jnp.float32
+        )
+        centre = jnp.sum(prob_grad * probs[window], axis=-1, keepdims=True)
+        score_grad = (probs[window] * (prob_grad - centre) * score_scale).astype(jnp.bfloat16)
+        query_parts.append(
+            jnp.einsum(
+                "shqk,skhe->sqhe", score_grad, key_heads[window], preferred_element_type=jnp.float32
+            )
+            .astype(jnp.bfloat16)
+            .reshape(1, tokens_here, head_width)
+        )
+        key_all = jnp.einsum(
+            "shqk,sqhe->skhe", score_grad, query_heads[window], preferred_element_type=jnp.float32
+        ).reshape(3 * tokens_here, head_width)
+        value_all = value_all.reshape(3 * tokens_here, head_width)
+        own_keys.append(key_all[2 * tokens_here :].astype(jnp.bfloat16))
+        own_values.append(value_all[2 * tokens_here :].astype(jnp.bfloat16))
+        far_parts.append(jnp.stack([key_all[:tokens_here], value_all[:tokens_here]]))
+        near_parts.append(
+            jnp.stack(
+                [key_all[tokens_here : 2 * tokens_here], value_all[tokens_here : 2 * tokens_here]]
+            )
+        )
+        if step + 1 < steps_here:
+            carried = (partials, input_terms, terms, grouped, query_parts, own_keys, own_values)
+            gathered[step + 1], carried, far_parts, near_parts = lax.optimization_barrier(
+                (gathered[step + 1], carried, far_parts, near_parts)
+            )
+            partials, input_terms, terms, grouped, query_parts, own_keys, own_values = carried
+    layer_sum = sum_over_groups(
+        jnp.concatenate(partials, axis=0).astype(jnp.bfloat16), steps_here, tokens_here
+    )
     layer_out = (hidden_in.astype(jnp.float32) + layer_sum).astype(jnp.bfloat16)
-    attended_grad = contract_cols(grad_rows, out_proj).astype(jnp.bfloat16)
-    pre_grad = (contract_cols(grad_rows, branch_out) * gelu_slope(pre_act)).astype(jnp.bfloat16)
-    tm_count = lax.axis_size(TM)
-    grouped = jnp.sum(
-        pre_grad.reshape(
-            steps_here, action_count, tokens_here // action_count, branch_width
-        ).astype(jnp.float32),
-        axis=(0, 2),
-    )
     table_term = jnp.dot(onehot.astype(jnp.float32).T, grouped, precision=lax.Precision.HIGHEST)
-    head_cols = attended.shape[1]
-    input_side = jnp.concatenate(
-        [jnp.zeros((row_count, head_cols + branch_width), jnp.bfloat16), pre_grad], axis=1
-    )
-    grad_side = jnp.concatenate(
-        [attended, branch_act, jnp.zeros((row_count, branch_width), jnp.bfloat16)], axis=1
-    )
-    terms = contract_rows(
-        full_both.reshape(2 * row_count, model_width),
-        jnp.concatenate([input_side, grad_side], axis=0),
-    ).astype(jnp.bfloat16)
-    merged = two_stage_scatter(terms).astype(jnp.float32)
+    merged = two_stage_scatter(terms.astype(jnp.bfloat16)).astype(jnp.float32)
     table_blocks = lax.all_to_all(
         table_term.astype(jnp.bfloat16).reshape(tm_count, -1, branch_width), TM, 0, 0, tiled=True
     )
@@ -186,45 +233,18 @@
         merged[:, head_cols : head_cols + branch_width].T,
         jnp.sum(table_blocks.astype(jnp.float32), axis=0),
     )
-    input_term = contract_cols(pre_grad, branch_in)
-    input_sum = sum_over_groups(input_term.astype(jnp.bfloat16), steps_here, tokens_here)
+    input_sum = sum_over_groups(
+        jnp.concatenate(input_terms, axis=0).astype(jnp.bfloat16), steps_here, tokens_here
+    )
     input_grad = (out_grad.astype(jnp.float32) + input_sum).astype(jnp.bfloat16)
-    weight_grads = (summed, input_grad)
-    grad_heads = attended_grad.reshape(steps_here, tokens_here, heads_here, HD)
-    value_all = jnp.einsum(
-        "shqk,sqhe->skhe", probs_low, grad_heads, preferred_element_type=jnp.float32
-    )
-    prob_grad = jnp.einsum(
-        "sqhe,skhe->shqk", grad_heads, value_heads, preferred_element_type=jnp.float32
-    )
-    centre = jnp.sum(prob_grad * probs, axis=-1, keepdims=True)
-    score_grad = (probs * (prob_grad - centre) * score_scale).astype(jnp.bfloat16)
-    query_grad = (
-        jnp.einsum("shqk,skhe->sqhe", score_grad, key_heads, preferred_element_type=jnp.float32)
-        .astype(jnp.bfloat16)
-        .reshape(1, steps_here, tokens_here, head_width)
-    )
-    key_all = jnp.einsum(
-        "shqk,sqhe->skhe", score_grad, query_heads, preferred_element_type=jnp.float32
-    ).reshape(steps_here, 3 * tokens_here, head_width)
-    value_all = value_all.reshape(steps_here, 3 * tokens_here, head_width)
-    own_key = key_all[:, 2 * tokens_here :].astype(jnp.bfloat16)[None]
-    own_value = value_all[:, 2 * tokens_here :].astype(jnp.bfloat16)[None]
-    toward_far = jnp.stack(
-        [jnp.sum(key_all[:, :tokens_here], axis=0), jnp.sum(value_all[:, :tokens_here], axis=0)]
-    )
-    toward_near = jnp.stack(
-        [
-            jnp.sum(key_all[:, tokens_here : 2 * tokens_here], axis=0),
-            jnp.sum(value_all[:, tokens_here : 2 * tokens_here], axis=0),
-        ]
-    )
+    query_grad = jnp.concatenate(query_parts, axis=0)[None]
+    own_key = jnp.stack(own_keys)[None]
+    own_value = jnp.stack(own_values)[None]
+    toward_far = sum(far_parts)
+    toward_near = sum(near_parts)
     from_next = from_behind(toward_near.astype(jnp.bfloat16), TM, -1).astype(toward_near.dtype)
     from_after = from_behind(toward_far.astype(jnp.bfloat16), TM, -2).astype(toward_far.dtype)
-    received = from_next + from_after
-    attention_grads = (query_grad, own_key, own_value, received[None])
-    summed, input_grad = weight_grads
-    query_grad, own_key, own_value, cache_grad = attention_grads
+    cache_grad = (from_next + from_after)[None]
     return (
         layer_out,
         input_grad,

time: 458 us -> 464 us (1.013)
  waiting for transfers between devices: 187 us -> 112 us
  local copies, waits for them, and re-layouts: 67.1 us -> 122 us
  other arithmetic: 35.2 us -> 67 us
  matrix products: 113 us -> 101 us
  starting transfers between devices: 34.4 us -> 40.7 us
    all_gather x1 -> x2, waiting for transfers between devices: 91.8 us -> 17.9 us  [body(): lax.all_gather(jnp.stack([hidden_in[0, step], out_grad[0, step]]), 'tenso...]
    dot_general x6 -> x12, matrix products: 56.1 us -> 31 us  [the longest x2 12.1 us: body(): jnp.dot(attended_here, out_proj, preferred_element_type=jnp.float32)]
    another operation x0 -> x10, local copies, waits for them, and re-layouts: none -> 19.7 us  [the longest x4 8.64 us: body(): jnp.stack([key_all[:tokens_here], value_all[:tokens_here]])]
    slice x5 -> x18, local copies, waits for them, and re-layouts: 15.5 us -> 29.6 us  [the longest x3 6.13 us: body(): key_heads[window]]
    another operation x2 -> x6, other arithmetic: 1.79 us -> 14.2 us  [the longest x1 0.9 us: body(): jnp.stack([jnp.sum(key_all[:, tokens_here:2 * tokens_here], axis=0), jnp....]
    convert_element_type x1 -> x4, other arithmetic: 1.25 us -> 11.2 us  [the longest x1 4.54 us: body(): probs_low = probs.astype(jnp.bfloat16)]
    dot_general x3 -> x6, matrix products: 17.8 us -> 26.4 us  [contract_cols(): lax.dot_general(left, right, (((1,), (1,)), ((), ())), preferred_element_...]
    squeeze x0 -> x4, local copies, waits for them, and re-layouts: none -> 8.08 us  [the longest x1 2.18 us: body(): nearer[1]]
  transfers between devices with their start and end apart: 10 -> 11, of which waited for: 5 -> 5; matrix products, arithmetic and copies ran while one was open for 30% -> 50% of each run, Pallas kernels for 0% -> 0%
where the time goes in v6:
time: 464 us; the launch traced here: 458 us
  local copies, waits for them, and re-layouts  122 us (26%)
  waiting for transfers between devices  112 us (24%)
  matrix products  101 us (22%)
  other arithmetic  67 us (14%)
  starting transfers between devices  40.7 us (9%)
  between operations  15.3 us (3%)
    all_to_all x2, waiting for transfers between devices, sum_over_groups(): received = lax.all_to_all(blocks, 'tensor', 1, 1, tiled=True)  55.3 us
    dot_general x2, matrix products, contract_rows(): lax.dot_general(left, right, (((0,), (0,)), ((), ())), preferred_element_...  32.5 us
    dot_general x6, matrix products, contract_cols(): lax.dot_general(left, right, (((1,), (1,)), ((), ())), preferred_element_...  26.4 us
    reduce_scatter x1, waiting for transfers between devices, two_stage_scatter(): return lax.psum_scatter(paired, 'tmo', scatter_dimension=0, tiled=True)[0]  24.4 us
    all_to_all x2, starting transfers between devices, sum_over_groups(): received = lax.all_to_all(blocks, 'tensor', 1, 1, tiled=True)  21.6 us
    unnamed x87, local copies, waits for them, and re-layouts  19.1 us
    all_gather x2, waiting for transfers between devices, body(): lax.all_gather(jnp.stack([hidden_in[0, step], out_grad[0, step]]), 'tenso...  17.9 us
    dot_general x2, matrix products, body(): jnp.dot(attended_here, out_proj, preferred_element_type=jnp.float32)  12.1 us
  transfers between devices with their start and end apart: 11, of which 5 were waited for; matrix products, arithmetic and copies ran while one was open for 50% of the time, Pallas kernels for 0%

profile of v6, /device:TPU:0, one launch (start us, length us, event | category | flops | bytes accessed | tf_op | source)
XLA Modules:
  0.0 457.6 jit_solution(9040242538530107786)
XLA Ops:
  14.9 4.2 collective-permute-start
  61.2 4.5 fusion.117
  71.2 4.6 %fusion.127 = f32[256,5120]{1,0:T(8,128)} fusion(bf16[256,640]{0,1:T(8,128)(2,1)S(1)} %bitcast.294, bf16[640,5120]{1,0:T(8,128)(2,1)S(1)} %bitcast.254), kind=kOutput, calls=%fused_computation.180 | convolution fusion | flops 1677721600 | bytes 12124160 | tf_op jit(solution)/shard_map/dot_general | solution.py:161
  75.8 17.9 %all-gather.5.cloned.1.call-done = bf16[2,256,5120]{2,1,0:T(8,128)(2,1)} async-done(((bf16[2,256,640]{2,1,0:T(8,128)(2,1)}), bf16[2,256,5120]{2,1,0:T(8,128)(2,1)}) %all-gather.5.cloned.1.call-update) | async-done | bytes 5242896 | tf_op jit(solution)/shard_map/all_gather | solution.py:145
  104.5 7.0 %fusion.73 = bf16[256,640]{1,0:T(8,128)(2,1)} fusion(bf16[640,5120]{1,0:T(8,128)(2,1)} %param.17, bf16[2,256,5120]{2,1,0:T(8,128)(2,1)} %all-gather.5.cloned.1.call-done), kind=kOutput, calls=%fused_computation.102 | convolution fusion | flops 1677885440 | bytes 9502720 | tf_op jit(solution)/shard_map/dot_general | solution.py:38
  113.4 3.3 fusion.12
  152.0 12.5 %fusion.52 = f32[5120,1280]{1,0:T(8,128)} fusion(bf16[512,5120]{1,0:T(8,128)(2,1)S(1)} %bitcast.305, bf16[256,320]{0,1:T(8,128)(2,1)S(1)} %broadcast.50, bf16[256,320]{0,1:T(8,128)(2,1)S(1)} %fusion.90, bf16[256,320]{0,1:T(8,128)(2,1)S(1)} %multiply_convert_fusion.1, bf16[256,640]{0,1:T(8,128)(2,1)S(1)} %bitcast.295), kind=kOutput, calls=%fused_computation.80 | convolution fusion | flops 6717440000 | bytes 32276480 | tf_op jit(solution)/shard_map/dot_general | solution.py:32
  175.6 20.0 %add_convert_fusion = bf16[5120,1280]{1,0:T(8,128)(2,1)} fusion(f32[5120,1280]{1,0:T(8,128)} %fusion.52, bf16[512,5120]{1,0:T(8,128)(2,1)} %bitcast.302, bf16[256,320]{0,1:T(8,128)(2,1)S(1)} %copy-done.32, bf16[256,320]{0,1:T(8,128)(2,1)S(1)} %fusion.87, bf16[256,320]{0,1:T(8,128)(2,1)S(1)} %multiply_convert_fusion, bf16[256,640]{0,1:T(8,128)(2,1)S(1)} %bitcast.293), kind=kOutput, calls=%fused_computation.1 | convolution fusion | flops 6730547200 | bytes 45383680 | tf_op jit(solution)/shard_map/dot_general | solution.py:32
  195.5 6.0 %dynamic-slice_bitcast_fusion = bf16[8,320,1280]{2,1,0:T(8,128)(2,1)} fusion(bf16[8,2,320,1280]{3,2,1,0:T(8,128)(2,1)} %bitcast.257, s32[]{:T(128)S(6)} %select_n.17), kind=kLoop, calls=%fused_computation.13 | loop fusion | bytes 13107204 | tf_op jit(solution)/shard_map/jit(dynamic_index_in_dim)/squeeze | solution.py:52
  201.5 10.9 %collective-permute-done.4 = bf16[8,320,1280]{2,1,0:T(8,128)(2,1)} collective-permute-done((bf16[8,320,1280]{2,1,0:T(8,128)(2,1)}, bf16[8,320,1280]{2,1,0:T(8,128)(2,1)}, u32[]{:S(2)}, u32[]{:S(2)}) %collective-permute-start.4) | collective-permute-done | bytes 6553632 | tf_op jit(solution)/shard_map/ppermute | solution.py:54
  212.4 9.0 %fusion.1 = bf16[8,320,1280]{2,1,0:T(8,128)(2,1)} fusion(bf16[8,320,1280]{2,1,0:T(8,128)(2,1)} %collective-permute-done.4, bf16[8,2,320,1280]{3,2,1,0:T(8,128)(2,1)} %bitcast.258, s32[]{:T(128)S(6)} %select_n.16), kind=kLoop, calls=%fused_computation.3 | loop fusion | flops 13107200 | bytes 19660804 | tf_op jit(solution)/shard_map/convert_element_type | solution.py:55
  221.5 7.5 %fusion.129 = f32[256,5120]{1,0:T(8,128)} fusion(bf16[256,640]{0,1:T(8,128)(2,1)} %bitcast.292, bf16[640,5120]{1,0:T(8,128)(2,1)} %param.17), kind=kOutput, calls=%fused_computation.182 | convolution fusion | flops 1677721600 | bytes 12124160 | tf_op jit(solution)/shard_map/dot_general | solution.py:161
  229.8 4.1 fusion.4
  239.5 10.1 %all-to-all-start.2 = ((bf16[16,8,320]{2,1,0:T(8,128)(2,1)}), bf16[16,8,320]{2,1,0:T(8,128)(2,1)S(1)}, u32[]{:S(2)}, u32[]{:S(2)}) async-start(bf16[16,8,320]{2,1,0:T(8,128)(2,1)} %bitcast.316), calls=%async_computation.3 | async-start | bytes 196608 | tf_op jit(solution)/shard_map/all_to_all | solution.py:227
  249.6 5.6 %pad_maximum_fusion = bf16[512,8,640]{2,0,1:T(8,128)(2,1)} fusion(bf16[256,8,640]{2,0,1:T(8,128)(2,1)} %bitcast.259, bf16[256,8,640]{2,0,1:T(8,128)(2,1)} %bitcast.260), kind=kLoop, calls=%fused_computation.16 | loop fusion | flops 10485760 | bytes 10485760 | tf_op jit(solution)/shard_map/concatenate | solution.py:222
  258.1 5.8 %all-to-all-start = ((bf16[512,8,640]{2,0,1:T(8,128)(2,1)}), bf16[512,8,640]{2,0,1:T(8,128)(2,1)}, u32[]{:S(2)}, u32[]{:S(2)}) async-start(bf16[512,8,640]{2,0,1:T(8,128)(2,1)} %pad_maximum_fusion), calls=%async_computation | async-start | bytes 10485760 | tf_op jit(solution)/shard_map/all_to_all | solution.py:63
  268.1 3.5 convolution_convert_fusion
  276.4 55.3 %all-to-all-done = bf16[512,8,640]{2,0,1:T(8,128)(2,1)} async-done(((bf16[512,8,640]{2,0,1:T(8,128)(2,1)}), bf16[512,8,640]{2,0,1:T(8,128)(2,1)}, u32[]{:S(2)}, u32[]{:S(2)}) %all-to-all-start) | async-done | bytes 5242912 | tf_op jit(solution)/shard_map/all_to_all | solution.py:63
  331.8 15.8 %all-to-all-start.1 = ((bf16[512,8,640]{2,0,1:T(8,128)(2,1)}), bf16[512,8,640]{2,0,1:T(8,128)(2,1)}, u32[]{:S(2)}, u32[]{:S(2)}) async-start(bf16[512,8,640]{2,0,1:T(8,128)(2,1)} %pad_maximum_fusion.1), calls=%async_computation.1 | async-start | bytes 10485760 | tf_op jit(solution)/shard_map/all_to_all | solution.py:63
  347.5 6.8 %fusion.74 = bf16[256,640]{1,0:T(8,128)(2,1)} fusion(bf16[640,5120]{1,0:T(8,128)(2,1)} %param.17, bf16[2,256,5120]{2,1,0:T(8,128)(2,1)} %all-gather.3.cloned.1.call-done), kind=kOutput, calls=%fused_computation.103 | convolution fusion | flops 1677885440 | bytes 9502720 | tf_op jit(solution)/shard_map/dot_general | solution.py:38
  363.7 3.3 fusion.9
  412.3 3.5 convert_reduce_fusion.1
  416.7 3.4 convert_reduce_fusion
  421.1 24.4 %reduce-scatter.2.cloned.1.call-done = bf16[1,320,1280]{2,1,0:T(8,128)(2,1)} async-done(((bf16[8,320,1280]{2,1,0:T(8,128)(2,1)}), bf16[1,320,1280]{2,1,0:T(8,128)(2,1)}) %reduce-scatter.2.cloned.1.call-update) | async-done | bytes 819216 | tf_op jit(solution)/shard_map/reduce_scatter | solution.py:56
  (213 shorter events, 193.2 us)
Async XLA Ops:
  7.2 93.5 %copy-start = (bf16[320,5120]{1,0:T(8,128)(2,1)S(1)}, bf16[320,5120]{1,0:T(8,128)(2,1)}, u32[]{:S(2)}) copy-start(bf16[320,5120]{1,0:T(8,128)(2,1)} %param.19) | copy-start | bytes 9830404
  7.2 86.6 %all-gather.5.cloned.1.call-start = ((), (), s32[]{:S(2)}) async-start(), calls=%async_computation.5 | async-start | bytes 5898240 | tf_op jit(solution)/shard_map/all_gather | solution.py:145
  10.5 154.0 %all-gather.3.cloned.1.call-start = ((), (), s32[]{:S(2)}) async-start(), calls=%async_computation.4 | async-start | bytes 5898240 | tf_op jit(solution)/shard_map/all_gather | solution.py:145
  12.8 21.9 %collective-permute-start.1 = (bf16[2,256,640]{1,2,0:T(8,128)(2,1)}, bf16[2,256,640]{1,2,0:T(8,128)(2,1)}, u32[]{:S(2)}, u32[]{:S(2)}) collective-permute-start(bf16[2,256,640]{1,2,0:T(8,128)(2,1)} %bitcast.314), channel_id=1, source_target_pairs={{0,8},{8,16},{16,24},{24,32},{32,40},{40,48},{48,56},{56,64},{64,7... | collective-permute-start | bytes 1966088 | tf_op jit(solution)/shard_map/ppermute | solution.py:16
  14.9 23.8 %collective-permute-start = (bf16[2,256,640]{1,2,0:T(8,128)(2,1)}, bf16[2,256,640]{1,2,0:T(8,128)(2,1)}, u32[]{:S(2)}, u32[]{:S(2)}) collective-permute-start(bf16[2,256,640]{1,2,0:T(8,128)(2,1)} %bitcast.315), channel_id=1, source_target_pairs={{0,16},{8,24},{16,32},{24,40},{32,48},{40,56},{48,64},{56,72},{64,... | collective-permute-start | bytes 1966088 | tf_op jit(solution)/shard_map/ppermute | solution.py:16
  21.1 424.4 %reduce-scatter.2.cloned.1.call-start = ((), (), s32[]{:S(2)}) async-start(), calls=%async_computation.6 | async-start | bytes 7372800 | tf_op jit(solution)/shard_map/reduce_scatter | solution.py:56
  23.2 11.3 %copy-start.33 = (bf16[128,320]{0,1:T(8,128)(2,1)S(1)}, bf16[128,320]{0,1:T(8,128)(2,1)}, u32[]{:S(2)}) copy-start(bf16[128,320]{0,1:T(8,128)(2,1)} %param.20) | copy-start | bytes 245764
  23.2 11.3 %copy-start.34 = (s32[1,4]{1,0:T(1,128)S(1)}, s32[1,4]{1,0:T(1,128)}, u32[]{:S(2)}) copy-start(s32[1,4]{1,0:T(1,128)} %param.21) | copy-start | bytes 52
  67.0 4.2 slice-start
  119.8 4.5 copy-start.1
  120.7 5.7 %copy-start.14 = (f32[1,768,5,128]{1,3,2,0:T(8,128)}, f32[1,768,5,128]{1,3,2,0:T(8,128)S(1)}, u32[]{:S(2)}) copy-start(f32[1,768,5,128]{1,3,2,0:T(8,128)S(1)} %convolution_bitcast_fusion.1) | copy-start | bytes 5898244
  137.4 6.4 %copy-start.27 = (f32[256,320]{0,1:T(8,128)S(1)}, f32[256,320]{0,1:T(8,128)}, u32[]{:S(2)}) copy-start(f32[256,320]{0,1:T(8,128)} %copy.155) | copy-start | bytes 983044
  137.4 6.5 %copy-start.2 = (bf16[5,256,768]{1,2,0:T(8,128)(2,1)S(1)}, bf16[5,256,768]{1,2,0:T(8,128)(2,1)}, u32[]{:S(2)}) copy-start(bf16[5,256,768]{1,2,0:T(8,128)(2,1)} %copy-done.1) | copy-start | bytes 5898244
  137.5 6.5 %copy-start.15 = (bf16[1,768,640]{1,2,0:T(8,128)(2,1)S(1)}, bf16[1,768,640]{1,2,0:T(8,128)(2,1)}, u32[]{:S(2)}) copy-start(bf16[1,768,640]{1,2,0:T(8,128)(2,1)} %copy.165) | copy-start | bytes 2949124
  138.6 6.6 %copy-start.8 = (bf16[5120,320]{0,1:T(8,128)(2,1)S(1)}, bf16[5120,320]{0,1:T(8,128)(2,1)}, u32[]{:S(2)}) copy-start(bf16[5120,320]{0,1:T(8,128)(2,1)} %param.18) | copy-start | bytes 9830404
  141.3 7.1 %slice-start.2 = ((s8[5242880]{0:T(1024)(128)(4,1)}), s8[4194304]{0:T(1024)(128)(4,1)S(1)}, s32[]{:S(2)}) async-start(s8[5242880]{0:T(1024)(128)(4,1)} %bitcast.255), calls=%async_computation.9 | async-start | bytes 8388608
  144.0 4.3 slice-start.3
  145.2 6.8 %slice-start.4 = ((s8[5242880]{0:T(1024)(128)(4,1)}), s8[4194304]{0:T(1024)(128)(4,1)S(1)}, s32[]{:S(2)}) async-start(s8[5242880]{0:T(1024)(128)(4,1)} %bitcast.303), calls=%async_computation.11 | async-start | bytes 8388608
  201.5 10.9 %collective-permute-start.4 = (bf16[8,320,1280]{2,1,0:T(8,128)(2,1)}, bf16[8,320,1280]{2,1,0:T(8,128)(2,1)}, u32[]{:S(2)}, u32[]{:S(2)}) collective-permute-start(bf16[8,320,1280]{2,1,0:T(8,128)(2,1)} %dynamic-slice_bitcast_fusion), channel_id=1, source_target_pairs={{0,8},{8,0},{1,9},{9,1},{2,10},{10,2},{3,11},{11,3},{4,12},{12,4},... | collective-permute-start | bytes 19660808 | tf_op jit(solution)/shard_map/ppermute | solution.py:54
  239.5 18.6 %all-to-all-start.2 = ((bf16[16,8,320]{2,1,0:T(8,128)(2,1)}), bf16[16,8,320]{2,1,0:T(8,128)(2,1)S(1)}, u32[]{:S(2)}, u32[]{:S(2)}) async-start(bf16[16,8,320]{2,1,0:T(8,128)(2,1)} %bitcast.316), calls=%async_computation.3 | async-start | bytes 196608 | tf_op jit(solution)/shard_map/all_to_all | solution.py:227
  258.1 73.6 %all-to-all-start = ((bf16[512,8,640]{2,0,1:T(8,128)(2,1)}), bf16[512,8,640]{2,0,1:T(8,128)(2,1)}, u32[]{:S(2)}, u32[]{:S(2)}) async-start(bf16[512,8,640]{2,0,1:T(8,128)(2,1)} %pad_maximum_fusion), calls=%async_computation | async-start | bytes 10485760 | tf_op jit(solution)/shard_map/all_to_all | solution.py:63
  331.8 84.9 %all-to-all-start.1 = ((bf16[512,8,640]{2,0,1:T(8,128)(2,1)}), bf16[512,8,640]{2,0,1:T(8,128)(2,1)}, u32[]{:S(2)}, u32[]{:S(2)}) async-start(bf16[512,8,640]{2,0,1:T(8,128)(2,1)} %pad_maximum_fusion.1), calls=%async_computation.1 | async-start | bytes 10485760 | tf_op jit(solution)/shard_map/all_to_all | solution.py:63
  377.4 32.4 %collective-permute-start.3 = (bf16[2,256,640]{2,1,0:T(8,128)(2,1)}, bf16[2,256,640]{2,1,0:T(8,128)(2,1)}, u32[]{:S(2)}, u32[]{:S(2)}) collective-permute-start(bf16[2,256,640]{2,1,0:T(8,128)(2,1)} %fusion.66), channel_id=1, source_target_pairs={{16,0},{24,8},{32,16},{40,24},{48,32},{56,40},{64,48},{72,56},{80,... | collective-permute-start | bytes 1966088 | tf_op jit(solution)/shard_map/ppermute | solution.py:16
  385.8 24.0 %collective-permute-start.2 = (bf16[2,256,640]{2,1,0:T(8,128)(2,1)}, bf16[2,256,640]{2,1,0:T(8,128)(2,1)}, u32[]{:S(2)}, u32[]{:S(2)}) collective-permute-start(bf16[2,256,640]{2,1,0:T(8,128)(2,1)} %fusion.65), channel_id=1, source_target_pairs={{8,0},{16,8},{24,16},{32,24},{40,32},{48,40},{56,48},{64,56},{72,6... | collective-permute-start | bytes 1966088 | tf_op jit(solution)/shard_map/ppermute | solution.py:16
  (28 other events, 79.2 us)
Sparse Core Ops, SparseCore 0:
  10.7 83.0 all-gather.4
  96.0 58.7 all-gather.2
  221.6 223.9 reduce-scatter.1

commit v7 on v5

--- a/solution.py
+++ b/solution.py
@@ -57,12 +57,13 @@
 
 
 def sum_over_groups(partial, steps_here, tokens_here):
-    count = lax.axis_size("tensor")
     rows, width = partial.shape
-    blocks = partial.reshape(rows, count, width // count)
-    received = lax.all_to_all(blocks, "tensor", 1, 1, tiled=True)
-    total = jnp.sum(received.astype(jnp.float32), axis=1)
-    return total.reshape(1, steps_here, tokens_here, width // count)
+    return lax.psum_scatter(
+        partial.reshape(1, steps_here, tokens_here, width),
+        "tensor",
+        scatter_dimension=3,
+        tiled=True,
+    ).astype(jnp.float32)
 
 
 def body(

time: 458 us -> 444 us (0.969)
  local copies, waits for them, and re-layouts: 67.1 us -> 110 us
  waiting for transfers between devices: 187 us -> 157 us
  starting transfers between devices: 34.4 us -> 15.6 us
  other arithmetic: 35.2 us -> 29.2 us
    all_to_all x2 -> x0, waiting for transfers between devices: 60.5 us -> none  [sum_over_groups(): received = lax.all_to_all(blocks, 'tensor', 1, 1, tiled=True)]
    unnamed x64 -> x78, local copies, waits for them, and re-layouts: 22.5 us -> 73 us
    reduce_scatter x1, waiting for transfers between devices: 22.8 us -> 53.9 us  [two_stage_scatter(): return lax.psum_scatter(paired, 'tmo', scatter_dimension=0, tiled=True)[0]]
    all_to_all x2 -> x0, starting transfers between devices: 21.9 us -> none  [sum_over_groups(): received = lax.all_to_all(blocks, 'tensor', 1, 1, tiled=True)]
    all_gather x1, waiting for transfers between devices: 91.8 us -> 83.9 us  [body(): lax.all_gather(jnp.concatenate([hidden_in, out_grad], axis=0), 'tensor',...]
    all_to_all x1, waiting for transfers between devices: 0.01 us -> 7.04 us  [body(): lax.all_to_all(table_term.astype(jnp.bfloat16).reshape(tm_count, -1, bran...]
    reduce_sum x2 -> x0, other arithmetic: 6.93 us -> none  [sum_over_groups(): total = jnp.sum(received.astype(jnp.float32), axis=1)]
    reshape x2 -> x0, local copies, waits for them, and re-layouts: 5.56 us -> none  [sum_over_groups(): blocks = partial.reshape(rows, count, width // count)]
  transfers between devices with their start and end apart: 10 -> 10, of which waited for: 5 -> 5; matrix products, arithmetic and copies ran while one was open for 30% -> 43% of each run, Pallas kernels for 0% -> 0%
where the time goes in v7:
time: 444 us; the launch traced here: 437 us
  waiting for transfers between devices  157 us (35%)
  local copies, waits for them, and re-layouts  110 us (25%)
  matrix products  110 us (25%)
  other arithmetic  29.2 us (7%)
  starting transfers between devices  15.6 us (4%)
  between operations  15.2 us (3%)
    all_gather x1, waiting for transfers between devices, body(): lax.all_gather(jnp.concatenate([hidden_in, out_grad], axis=0), 'tensor',...  83.9 us
    unnamed x78, local copies, waits for them, and re-layouts  73 us
    reduce_scatter x1, waiting for transfers between devices, two_stage_scatter(): return lax.psum_scatter(paired, 'tmo', scatter_dimension=0, tiled=True)[0]  53.9 us
    dot_general x1, matrix products, contract_rows(): lax.dot_general(left, right, (((0,), (0,)), ((), ())), preferred_element_...  28.3 us
    dot_general x3, matrix products, contract_cols(): lax.dot_general(left, right, (((1,), (1,)), ((), ())), preferred_element_...  19 us
    dot_general x1, matrix products, body(): jnp.einsum('shqk,sqhe->skhe', score_grad, query_heads, preferred_element_...  14.4 us
    dot_general x1, matrix products, body(): jnp.einsum('shqk,skhe->sqhe', score_grad, key_heads, preferred_element_ty...  13.5 us
    ppermute x1, waiting for transfers between devices, two_stage_scatter(): got = lax.ppermute(given, 'core', [(0, 1), (1, 0)])  10.9 us
  transfers between devices with their start and end apart: 10, of which 5 were waited for; matrix products, arithmetic and copies ran while one was open for 43% of the time, Pallas kernels for 0%

profile of v7, /device:TPU:0, one launch (start us, length us, event | category | flops | bytes accessed | tf_op | source)
XLA Modules:
  0.0 437.0 jit_solution(1695809674958417732)
XLA Ops:
  14.3 4.2 collective-permute-start
  51.5 6.9 %fusion.76 = f32[512,5120]{1,0:T(8,128)} fusion(bf16[512,640]{0,1:T(8,128)(2,1)S(1)} %bitcast.139, bf16[640,5120]{1,0:T(8,128)(2,1)S(1)} %bitcast.126), kind=kOutput, calls=%fused_computation.101 | convolution fusion | flops 3355443200 | bytes 17694720 | tf_op jit(solution)/shard_map/dot_general | solution.py:154
  58.4 83.9 %all-gather.2.cloned.1.call-done = bf16[2,2,256,5120]{3,2,1,0:T(8,128)(2,1)} async-done(((bf16[2,2,256,640]{3,2,1,0:T(8,128)(2,1)}), bf16[2,2,256,5120]{3,2,1,0:T(8,128)(2,1)}) %all-gather.2.cloned.1.call-update) | async-done | bytes 10485776 | tf_op jit(solution)/shard_map/all_gather | solution.py:91
  142.3 8.8 %fusion.72 = (bf16[1,2,256,5120]{3,2,1,0:T(8,128)(2,1)}, bf16[1,2,256,5120]{3,2,1,0:T(8,128)(2,1)}) fusion(bf16[2,2,256,5120]{3,2,1,0:T(8,128)(2,1)} %all-gather.2.cloned.1.call-done), kind=kLoop, calls=%fused_computation.97 | loop fusion | bytes 20971520 | tf_op jit(solution)/shard_map/slice | solution.py:95
  151.0 7.3 %fusion.47 = f32[2,4,64,320]{3,2,1,0:T(8,128)} fusion(bf16[2,4,64,5120]{3,2,1,0:T(8,128)(2,1)} %bitcast.129, bf16[5120,320]{0,1:T(8,128)(2,1)} %param.18, f32[4,320]{1,0:T(4,128)S(1)} %fusion.56), kind=kOutput, calls=%fused_computation.56 | convolution fusion | flops 1677885440 | bytes 9180160 | tf_op jit(solution)/shard_map/dot_general | solution.py:147
  161.9 7.3 %add_convert_fusion = bf16[512,5120]{1,0:T(8,128)(2,1)} fusion(f32[512,5120]{1,0:T(8,128)} %fusion.76, bf16[512,320]{0,1:T(8,128)(2,1)S(1)} %multiply_convert_fusion.1, bf16[320,5120]{1,0:T(8,128)(2,1)S(1)} %copy-done), kind=kOutput, calls=%fused_computation.5 | convolution fusion | flops 1682964480 | bytes 19333120 | tf_op jit(solution)/shard_map/dot_general | solution.py:154
  169.2 13.6 %copy.133 = bf16[1,2,256,5120]{2,1,0,3:T(2,128)(2,1)} copy(bf16[1,2,256,5120]{3,2,1,0:T(8,128)(2,1)} %bitcast.116) | data formatting | bytes 10485760
  182.8 5.6 %copy.143 = bf16[640,8,2,256]{3,1,2,0:T(8,128)(2,1)} copy(bf16[640,8,2,256]{3,2,1,0:T(2,128)(2,1)} %bitcast.119) | data formatting | bytes 10485760
  188.5 4.9 %fusion.50 = bf16[512,320]{0,1:T(8,128)(2,1)S(1)} fusion(bf16[512,5120]{1,0:T(8,128)(2,1)} %bitcast.127, bf16[320,5120]{1,0:T(8,128)(2,1)S(1)} %copy-done, f32[512,320]{0,1:T(8,128)} %copy.99), kind=kOutput, calls=%fused_computation.57 | convolution fusion | flops 1680834560 | bytes 9502720 | tf_op jit(solution)/shard_map/dot_general | solution.py:38
  193.5 5.2 %convolution_convert_fusion.1 = bf16[512,5120]{1,0:T(8,128)(2,1)} fusion(bf16[512,320]{0,1:T(8,128)(2,1)S(1)} %fusion.50, bf16[5120,320]{0,1:T(8,128)(2,1)S(1)} %copy-done.2), kind=kOutput, calls=%fused_computation.14 | convolution fusion | flops 1680343040 | bytes 8847360 | tf_op jit(solution)/shard_map/dot_general | solution.py:38
  198.7 13.6 %copy.135 = bf16[1,2,256,5120]{2,1,0,3:T(2,128)(2,1)} copy(bf16[1,2,256,5120]{3,2,1,0:T(8,128)(2,1)} %bitcast.121) | data formatting | bytes 10485760
  212.3 5.8 %copy.144 = bf16[640,8,2,256]{3,1,2,0:T(8,128)(2,1)} copy(bf16[640,8,2,256]{3,2,1,0:T(2,128)(2,1)} %bitcast.120) | data formatting | bytes 10485760
  219.4 28.3 %convolution_convert_fusion = bf16[5120,1280]{1,0:T(8,128)(2,1)} fusion(bf16[1024,5120]{1,0:T(8,128)(2,1)} %bitcast.124, bf16[512,320]{0,1:T(8,128)(2,1)S(1)} %copy-done.21, bf16[512,320]{0,1:T(8,128)(2,1)S(1)} %broadcast_in_dim.76, bf16[512,320]{0,1:T(8,128)(2,1)S(1)} %copy-done.19, bf16[512,640]{0,1:T(8,128)(2,1)S(1)} %bitcast.140), kind=kOutput, calls=%fused_computation.2 | convolution fusion | flops 13441433600 | bytes 25231360 | tf_op jit(solution)/shard_map/dot_general | solution.py:32
  247.7 6.0 %dynamic-slice_bitcast_fusion = bf16[8,320,1280]{2,1,0:T(8,128)(2,1)} fusion(bf16[8,2,320,1280]{3,2,1,0:T(8,128)(2,1)} %bitcast.122, s32[]{:T(128)S(6)} %select_n.17), kind=kLoop, calls=%fused_computation.15 | loop fusion | bytes 13107204 | tf_op jit(solution)/shard_map/jit(dynamic_index_in_dim)/squeeze | solution.py:52
  253.9 10.9 %collective-permute-done.4 = bf16[8,320,1280]{2,1,0:T(8,128)(2,1)} collective-permute-done((bf16[8,320,1280]{2,1,0:T(8,128)(2,1)}, bf16[8,320,1280]{2,1,0:T(8,128)(2,1)}, u32[]{:S(2)}, u32[]{:S(2)}) %collective-permute-start.4) | collective-permute-done | bytes 6553632 | tf_op jit(solution)/shard_map/ppermute | solution.py:54
  264.7 9.1 %fusion.2 = bf16[8,320,1280]{2,1,0:T(8,128)(2,1)} fusion(bf16[8,320,1280]{2,1,0:T(8,128)(2,1)} %collective-permute-done.4, bf16[8,2,320,1280]{3,2,1,0:T(8,128)(2,1)} %bitcast.123, s32[]{:T(128)S(6)} %select_n.16), kind=kLoop, calls=%fused_computation.4 | loop fusion | flops 13107200 | bytes 19660804 | tf_op jit(solution)/shard_map/convert_element_type | solution.py:55
  273.9 8.8 %convolution_convert_fusion.2 = bf16[512,640]{1,0:T(8,128)(2,1)S(1)} fusion(bf16[512,5120]{1,0:T(8,128)(2,1)} %bitcast.128, bf16[640,5120]{1,0:T(8,128)(2,1)} %param.17), kind=kOutput, calls=%fused_computation.44 | convolution fusion | flops 3355770880 | bytes 12451840 | tf_op jit(solution)/shard_map/dot_general | solution.py:38
  284.0 4.9 %fusion.31 = f32[2,5,128,768]{3,2,1,0:T(8,128)S(1)} fusion(bf16[2,256,5,128]{1,3,2,0:T(8,128)(2,1)S(1)} %copy.115, f32[2,5,256,768]{2,3,1,0:T(8,128)} %copy-done.27, f32[2,5,256]{2,1,0:T(8,128)S(1)} %get-tuple-element.52), kind=kOutput, calls=%fused_computation.36 | convolution fusion | flops 507248640 | bytes 12462080 | tf_op jit(solution)/shard_map/shqk,sqhe->skhe/dot_general | solution.py:195
  291.9 4.3 fusion.36
  296.2 14.4 %fusion.12 = f32[2,5,768,128]{2,3,1,0:T(8,128)} fusion(bf16[2,256,5,128]{1,3,2,0:T(8,128)(2,1)S(1)} %bitcast.136, f32[2,5,256,768]{2,3,1,0:T(8,128)} %fusion.36, f32[2,5,256,768]{2,3,1,0:T(8,128)} %copy-done.27, f32[2,5,256]{2,1,0:T(8,128)S(1)} %get-tuple-element.52), kind=kOutput, calls=%fused_computation.18 | convolution fusion | flops 517082368 | bytes 20326400 | tf_op jit(solution)/shard_map/shqk,sqhe->skhe/dot_general | solution.py:208
  320.5 6.3 %all-to-all-start = ((bf16[16,8,320]{2,1,0:T(8,128)(2,1)}), bf16[16,8,320]{2,1,0:T(8,128)(2,1)S(1)}, u32[]{:S(2)}, u32[]{:S(2)}) async-start(bf16[16,8,320]{2,1,0:T(8,128)(2,1)} %bitcast.44), calls=%async_computation.1 | async-start | bytes 196608 | tf_op jit(solution)/shard_map/all_to_all | solution.py:181
  326.9 13.5 %fusion.40 = bf16[2,5,128,256]{3,2,1,0:T(8,128)(2,1)} fusion(f32[2,5,256,768]{2,3,1,0:T(8,128)} %fusion.36, bf16[2,256,5,128]{3,1,2,0:T(8,128)(2,1)S(1)} %copy-done.4, bf16[2,256,5,128]{3,1,2,0:T(8,128)(2,1)S(1)} %copy-done.11, bf16[2,256,5,128]{3,1,2,0:T(8,128)(2,1)S(1)} %copy-done.13, f32[2,5,256,768]{2,3,1,0:T(8,128)} %copy-done.27, ...), kind=kOutput, calls=%fused_computation.43 | convolution fusion | flops 523308288 | bytes 18360320 | tf_op jit(solution)/shard_map/shqk,skhe->sqhe/dot_general | solution.py:204
  347.5 7.0 %all-to-all-done = bf16[16,8,320]{2,1,0:T(8,128)(2,1)S(1)} async-done(((bf16[16,8,320]{2,1,0:T(8,128)(2,1)}), bf16[16,8,320]{2,1,0:T(8,128)(2,1)S(1)}, u32[]{:S(2)}, u32[]{:S(2)}) %all-to-all-start) | async-done | bytes 81952 | tf_op jit(solution)/shard_map/all_to_all | solution.py:181
  371.0 53.9 %reduce-scatter.8.cloned.1.call-done = bf16[1,320,1280]{2,1,0:T(8,128)(2,1)} async-done(((bf16[8,320,1280]{2,1,0:T(8,128)(2,1)}), bf16[1,320,1280]{2,1,0:T(8,128)(2,1)}) %reduce-scatter.8.cloned.1.call-update) | async-done | bytes 819216 | tf_op jit(solution)/shard_map/reduce_scatter | solution.py:56
  (133 shorter events, 87.2 us)
Async XLA Ops:
  7.2 154.7 %copy-start = (bf16[320,5120]{1,0:T(8,128)(2,1)S(1)}, bf16[320,5120]{1,0:T(8,128)(2,1)}, u32[]{:S(2)}) copy-start(bf16[320,5120]{1,0:T(8,128)(2,1)} %param.19) | copy-start | bytes 9830404
  7.2 20.7 %copy-start.26 = (s32[1,4]{1,0:T(1,128)S(1)}, s32[1,4]{1,0:T(1,128)}, u32[]{:S(2)}) copy-start(s32[1,4]{1,0:T(1,128)} %param.21) | copy-start | bytes 52
  7.2 20.7 %copy-start.25 = (bf16[128,320]{0,1:T(8,128)(2,1)S(1)}, bf16[128,320]{0,1:T(8,128)(2,1)}, u32[]{:S(2)}) copy-start(bf16[128,320]{0,1:T(8,128)(2,1)} %param.20) | copy-start | bytes 245764
  7.2 135.1 %all-gather.2.cloned.1.call-start = ((), (), s32[]{:S(2)}) async-start(), calls=%async_computation.4 | async-start | bytes 11796480 | tf_op jit(solution)/shard_map/all_gather | solution.py:91
  9.9 348.1 %reduce-scatter.10.cloned.1.call-start = ((), (), s32[]{:S(2)}) async-start(), calls=%async_computation.6 | async-start | bytes 5898240
  12.1 16.0 %collective-permute-start.1 = (bf16[2,256,640]{1,2,0:T(8,128)(2,1)}, bf16[2,256,640]{1,2,0:T(8,128)(2,1)}, u32[]{:S(2)}, u32[]{:S(2)}) collective-permute-start(bf16[2,256,640]{1,2,0:T(8,128)(2,1)} %bitcast.156), channel_id=1, source_target_pairs={{0,8},{8,16},{16,24},{24,32},{32,40},{40,48},{48,56},{56,64},{64,7... | collective-permute-start | bytes 1966088 | tf_op jit(solution)/shard_map/ppermute | solution.py:16
  14.3 18.8 %collective-permute-start = (bf16[2,256,640]{1,2,0:T(8,128)(2,1)}, bf16[2,256,640]{1,2,0:T(8,128)(2,1)}, u32[]{:S(2)}, u32[]{:S(2)}) collective-permute-start(bf16[2,256,640]{1,2,0:T(8,128)(2,1)} %bitcast.157), channel_id=1, source_target_pairs={{0,16},{8,24},{16,32},{24,40},{32,48},{40,56},{48,64},{56,72},{64,... | collective-permute-start | bytes 1966088 | tf_op jit(solution)/shard_map/ppermute | solution.py:16
  45.4 6.1 %slice-start = ((s8[6553600]{0:T(1024)(128)(4,1)}), s8[4194304]{0:T(1024)(128)(4,1)S(1)}, s32[]{:S(2)}) async-start(s8[6553600]{0:T(1024)(128)(4,1)} %bitcast.125), calls=%async_computation.8 | async-start | bytes 8388608
  45.5 6.1 %slice-start.1 = ((s8[6553600]{0:T(1024)(128)(4,1)}), s8[2359296]{0:T(1024)(128)(4,1)S(1)}, s32[]{:S(2)}) async-start(s8[6553600]{0:T(1024)(128)(4,1)} %bitcast.125), calls=%async_computation.9 | async-start | bytes 4718592
  161.9 7.3 %copy-start.18 = (bf16[512,320]{0,1:T(8,128)(2,1)}, bf16[512,320]{0,1:T(8,128)(2,1)S(1)}, u32[]{:S(2)}) copy-start(bf16[512,320]{0,1:T(8,128)(2,1)S(1)} %multiply_convert_fusion.1) | copy-start | bytes 983044
  188.4 173.6 %reduce-scatter.12.cloned.1.call-start = ((), (), s32[]{:S(2)}) async-start(), calls=%async_computation.7 | async-start | bytes 5898240
  218.2 206.7 %reduce-scatter.8.cloned.1.call-start = ((), (), s32[]{:S(2)}) async-start(), calls=%async_computation.5 | async-start | bytes 7372800 | tf_op jit(solution)/shard_map/reduce_scatter | solution.py:56
  253.7 11.0 %collective-permute-start.4 = (bf16[8,320,1280]{2,1,0:T(8,128)(2,1)}, bf16[8,320,1280]{2,1,0:T(8,128)(2,1)}, u32[]{:S(2)}, u32[]{:S(2)}) collective-permute-start(bf16[8,320,1280]{2,1,0:T(8,128)(2,1)} %dynamic-slice_bitcast_fusion), channel_id=1, source_target_pairs={{0,8},{8,0},{1,9},{9,1},{2,10},{10,2},{3,11},{11,3},{4,12},{12,4},... | collective-permute-start | bytes 19660808 | tf_op jit(solution)/shard_map/ppermute | solution.py:54
  284.0 7.9 %copy-start.7 = (bf16[1,2,256,640]{2,3,1,0:T(8,128)(2,1)S(1)}, bf16[1,2,256,640]{2,3,1,0:T(8,128)(2,1)}, u32[]{:S(2)}) copy-start(bf16[1,2,256,640]{2,3,1,0:T(8,128)(2,1)} %copy.90) | copy-start | bytes 1966084
  284.0 7.9 %copy-start.15 = (bf16[2,256,5,128]{1,3,2,0:T(8,128)(2,1)S(1)}, bf16[2,256,5,128]{1,3,2,0:T(8,128)(2,1)}, u32[]{:S(2)}) copy-start(bf16[2,256,5,128]{1,3,2,0:T(8,128)(2,1)} %copy-done.14) | copy-start | bytes 1966084
  284.0 7.9 %copy-start.17 = (bf16[2,256,5,128]{1,3,2,0:T(8,128)(2,1)S(1)}, bf16[2,256,5,128]{1,3,2,0:T(8,128)(2,1)}, u32[]{:S(2)}) copy-start(bf16[2,256,5,128]{1,3,2,0:T(8,128)(2,1)} %copy-done.16) | copy-start | bytes 1966084
  310.6 8.5 %copy-start.22 = (bf16[512,320]{0,1:T(8,128)(2,1)S(1)}, bf16[512,320]{0,1:T(8,128)(2,1)}, u32[]{:S(2)}) copy-start(bf16[512,320]{0,1:T(8,128)(2,1)} %copy-done.20) | copy-start | bytes 983044
  310.6 16.2 %copy-start.4 = (bf16[2,256,5,128]{3,1,2,0:T(8,128)(2,1)S(1)}, bf16[2,256,5,128]{3,1,2,0:T(8,128)(2,1)}, u32[]{:S(2)}) copy-start(bf16[2,256,5,128]{3,1,2,0:T(8,128)(2,1)} %copy.94) | copy-start | bytes 1966084
  310.6 16.2 %copy-start.11 = (bf16[2,256,5,128]{3,1,2,0:T(8,128)(2,1)S(1)}, bf16[2,256,5,128]{3,1,2,0:T(8,128)(2,1)}, u32[]{:S(2)}) copy-start(bf16[2,256,5,128]{3,1,2,0:T(8,128)(2,1)} %copy-done.10) | copy-start | bytes 1966084
  310.6 16.2 %copy-start.13 = (bf16[2,256,5,128]{3,1,2,0:T(8,128)(2,1)S(1)}, bf16[2,256,5,128]{3,1,2,0:T(8,128)(2,1)}, u32[]{:S(2)}) copy-start(bf16[2,256,5,128]{3,1,2,0:T(8,128)(2,1)} %copy-done.12) | copy-start | bytes 1966084
  314.7 40.5 %collective-permute-start.3 = (bf16[2,256,640]{1,2,0:T(8,128)(2,1)}, bf16[2,256,640]{1,2,0:T(8,128)(2,1)}, u32[]{:S(2)}, u32[]{:S(2)}) collective-permute-start(bf16[2,256,640]{1,2,0:T(8,128)(2,1)} %pad_maximum_fusion.14), channel_id=1, source_target_pairs={{16,0},{24,8},{32,16},{40,24},{48,32},{56,40},{64,48},{72,56},{80,... | collective-permute-start | bytes 1966088 | tf_op jit(solution)/shard_map/ppermute | solution.py:16
  317.8 37.3 %collective-permute-start.2 = (bf16[2,256,640]{1,2,0:T(8,128)(2,1)}, bf16[2,256,640]{1,2,0:T(8,128)(2,1)}, u32[]{:S(2)}, u32[]{:S(2)}) collective-permute-start(bf16[2,256,640]{1,2,0:T(8,128)(2,1)} %pad_maximum_fusion.13), channel_id=1, source_target_pairs={{8,0},{16,8},{24,16},{32,24},{40,32},{48,40},{56,48},{64,56},{72,6... | collective-permute-start | bytes 1966088 | tf_op jit(solution)/shard_map/ppermute | solution.py:16
  320.5 34.0 %all-to-all-start = ((bf16[16,8,320]{2,1,0:T(8,128)(2,1)}), bf16[16,8,320]{2,1,0:T(8,128)(2,1)S(1)}, u32[]{:S(2)}, u32[]{:S(2)}) async-start(bf16[16,8,320]{2,1,0:T(8,128)(2,1)} %bitcast.44), calls=%async_computation.1 | async-start | bytes 196608 | tf_op jit(solution)/shard_map/all_to_all | solution.py:181
  364.7 65.5 %copy-start.1 = (bf16[320,5120]{1,0:T(8,128)(2,1)S(1)}, bf16[320,5120]{1,0:T(8,128)(2,1)}, u32[]{:S(2)}) copy-start(bf16[320,5120]{1,0:T(8,128)(2,1)} %param.19) | copy-start | bytes 9830404
  (16 other events, 43.9 us)
Sparse Core Ops, SparseCore 0:
  10.2 131.9 all-gather.1
  188.6 59.4 reduce-scatter.9
  250.5 61.7 reduce-scatter.11
  316.1 108.7 reduce-scatter.7

commit v8 on v7

--- a/solution.py
+++ b/solution.py
@@ -57,12 +57,9 @@
 
 
 def sum_over_groups(partial, steps_here, tokens_here):
-    rows, width = partial.shape
-    return lax.psum_scatter(
-        partial.reshape(1, steps_here, tokens_here, width),
-        "tensor",
-        scatter_dimension=3,
-        tiled=True,
+    count, rows, width = partial.shape
+    return lax.psum_scatter(partial, "tensor", scatter_dimension=0, tiled=True).reshape(
+        1, steps_here, tokens_here, width
     ).astype(jnp.float32)
 
 
@@ -151,8 +148,18 @@
     )
     pre_act = pre_act.reshape(row_count, branch_width)
     branch_act = gelu_value(pre_act).astype(jnp.bfloat16)
-    partial_value = jnp.dot(attended, out_proj, preferred_element_type=jnp.float32) + jnp.dot(
-        branch_act, branch_out, preferred_element_type=jnp.float32
+    group_count = lax.axis_size("tensor")
+    group_width = model_width // group_count
+    partial_value = jnp.einsum(
+        "rk,kjn->jrn",
+        attended,
+        out_proj.reshape(-1, group_count, group_width),
+        preferred_element_type=jnp.float32,
+    ) + jnp.einsum(
+        "rk,kjn->jrn",
+        branch_act,
+        branch_out.reshape(-1, group_count, group_width),
+        preferred_element_type=jnp.float32,
     )
     layer_sum = sum_over_groups(partial_value.astype(jnp.bfloat16), steps_here, tokens_here)
     layer_out = (hidden_in.astype(jnp.float32) + layer_sum).astype(jnp.bfloat16)
@@ -187,7 +194,12 @@
         merged[:, head_cols : head_cols + branch_width].T,
         jnp.sum(table_blocks.astype(jnp.float32), axis=0),
     )
-    input_term = contract_cols(pre_grad, branch_in)
+    input_term = jnp.einsum(
+        "rk,jnk->jrn",
+        pre_grad,
+        branch_in.reshape(group_count, group_width, -1),
+        preferred_element_type=jnp.float32,
+    )
     input_sum = sum_over_groups(input_term.astype(jnp.bfloat16), steps_here, tokens_here)
     input_grad = (out_grad.astype(jnp.float32) + input_sum).astype(jnp.bfloat16)
     weight_grads = (summed, input_grad)

time: 444 us -> 429 us (0.966)
  local copies, waits for them, and re-layouts: 110 us -> 49 us
  waiting for transfers between devices: 157 us -> 208 us
    unnamed x78, local copies, waits for them, and re-layouts: 73 us -> 17.8 us
    reduce_scatter x1, waiting for transfers between devices: 53.9 us -> 97.6 us  [two_stage_scatter(): return lax.psum_scatter(paired, 'tmo', scatter_dimension=0, tiled=True)[0]]
    ppermute x4, waiting for transfers between devices: 1.13 us -> 11.2 us  [from_behind(): lax.ppermute(value, axis, [(source, source + steps) for source in range(f...]
    all_to_all x1, waiting for transfers between devices: 7.04 us -> 0.01 us  [body(): lax.all_to_all(table_term.astype(jnp.bfloat16).reshape(tm_count, -1, bran...]
    dot_general x3 -> x2, matrix products: 19 us -> 14.1 us  [contract_cols(): lax.dot_general(left, right, (((1,), (1,)), ((), ())), preferred_element_...]
    all_gather x1, waiting for transfers between devices: 83.9 us -> 88.7 us  [body(): lax.all_gather(jnp.concatenate([hidden_in, out_grad], axis=0), 'tensor',...]
    dot_general x2 -> x3, matrix products: 14.1 us -> 16.1 us  [the longest x1 6.89 us: body(): jnp.einsum('rk,kjn->jrn', attended, out_proj.reshape(-1, group_count, gro...]
  transfers between devices with their start and end apart: 10 -> 10, of which waited for: 5 -> 4; matrix products, arithmetic and copies ran while one was open for 43% -> 35% of each run, Pallas kernels for 0% -> 0%
where the time goes in v8:
time: 429 us; the launch traced here: 423 us
  waiting for transfers between devices  208 us (48%)
  matrix products  106 us (25%)
  local copies, waits for them, and re-layouts  49 us (11%)
  other arithmetic  28.6 us (7%)
  between operations  15.4 us (4%)
  starting transfers between devices  15.3 us (4%)
    reduce_scatter x1, waiting for transfers between devices, two_stage_scatter(): return lax.psum_scatter(paired, 'tmo', scatter_dimension=0, tiled=True)[0]  97.6 us
    all_gather x1, waiting for transfers between devices, body(): lax.all_gather(jnp.concatenate([hidden_in, out_grad], axis=0), 'tensor',...  88.7 us
    dot_general x1, matrix products, contract_rows(): lax.dot_general(left, right, (((0,), (0,)), ((), ())), preferred_element_...  28.6 us
    unnamed x78, local copies, waits for them, and re-layouts  17.8 us
    dot_general x1, matrix products, body(): jnp.einsum('shqk,sqhe->skhe', score_grad, query_heads, preferred_element_...  14.5 us
    dot_general x2, matrix products, contract_cols(): lax.dot_general(left, right, (((1,), (1,)), ((), ())), preferred_element_...  14.1 us
    dot_general x1, matrix products, body(): jnp.einsum('shqk,skhe->sqhe', score_grad, key_heads, preferred_element_ty...  13.5 us
    ppermute x4, waiting for transfers between devices, from_behind(): lax.ppermute(value, axis, [(source, source + steps) for source in range(f...  11.2 us
  transfers between devices with their start and end apart: 10, of which 4 were waited for; matrix products, arithmetic and copies ran while one was open for 35% of the time, Pallas kernels for 0%

profile of v8, /device:TPU:0, one launch (start us, length us, event | category | flops | bytes accessed | tf_op | source)
XLA Modules:
  0.0 423.1 jit_solution(16071455674054686168)
XLA Ops:
  7.3 2.6 pad_maximum_fusion.10
  14.3 4.2 collective-permute-start
  21.9 11.2 %collective-permute-done = bf16[2,256,640]{1,2,0:T(8,128)(2,1)} collective-permute-done((bf16[2,256,640]{1,2,0:T(8,128)(2,1)}, bf16[2,256,640]{1,2,0:T(8,128)(2,1)}, u32[]{:S(2)}, u32[]{:S(2)}) %collective-permute-start) | collective-permute-done | bytes 655392 | tf_op jit(solution)/shard_map/ppermute | solution.py:16
  37.8 2.6 fusion.95
  41.8 2.6 copy-done.31
  46.7 6.9 %fusion.6 = f32[512,8,640]{2,0,1:T(8,128)} fusion(bf16[80,8,8,640]{3,2,1,0:T(8,128)(2,1)S(1)} %bitcast.169, bf16[512,640]{0,1:T(8,128)(2,1)S(1)} %bitcast.159), kind=kOutput, calls=%fused_computation.14 | convolution fusion | flops 3355443200 | bytes 17694720 | tf_op jit(solution)/shard_map/rk,kjn->jrn/dot_general | solution.py:153
  53.6 88.7 %all-gather.2.cloned.1.call-done = bf16[2,2,256,5120]{3,2,1,0:T(8,128)(2,1)} async-done(((bf16[2,2,256,640]{3,2,1,0:T(8,128)(2,1)}), bf16[2,2,256,5120]{3,2,1,0:T(8,128)(2,1)}) %all-gather.2.cloned.1.call-update) | async-done | bytes 10485776 | tf_op jit(solution)/shard_map/all_gather | solution.py:88
  142.3 8.7 %fusion.92 = (bf16[1,2,256,5120]{3,2,1,0:T(8,128)(2,1)}, bf16[1,2,256,5120]{3,2,1,0:T(8,128)(2,1)}) fusion(bf16[2,2,256,5120]{3,2,1,0:T(8,128)(2,1)} %all-gather.2.cloned.1.call-done), kind=kLoop, calls=%fused_computation.116 | loop fusion | bytes 20971520 | tf_op jit(solution)/shard_map/slice | solution.py:92
  151.0 7.5 %fusion.68 = (bf16[2,4,64,320]{3,2,1,0:T(8,128)(2,1)S(1)}, f32[2,4,64,320]{3,2,1,0:T(8,128)}) fusion(f32[4,320]{1,0:T(4,128)S(1)} %fusion.76, bf16[2,4,64,5120]{3,2,1,0:T(8,128)(2,1)} %bitcast.137, bf16[5120,320]{0,1:T(8,128)(2,1)} %param.18), kind=kOutput, calls=%fused_computation.79 | convolution fusion | flops 1679360000 | bytes 9507840 | tf_op jit(solution)/shard_map/dot_general | solution.py:144
  158.6 4.6 %fusion.11 = bf16[8,512,640]{2,1,0:T(8,128)(2,1)} fusion(f32[512,8,640]{2,0,1:T(8,128)S(1)} %copy-done.2, bf16[512,320,1]{1,0,2:T(8,128)(2,1)S(1)} %bitcast.166, bf16[40,8,8,640]{3,2,1,0:T(8,128)(2,1)S(1)} %bitcast.138), kind=kOutput, calls=%fused_computation.18 | convolution fusion | flops 1682964480 | bytes 19333120 | tf_op jit(solution)/shard_map/rk,kjn->jrn/dot_general | solution.py:158
  163.3 2.2 copy.116
  167.5 5.4 %fusion.63 = bf16[512,320]{0,1:T(8,128)(2,1)S(1)} fusion(bf16[512,5120]{1,0:T(8,128)(2,1)} %bitcast.135, bf16[320,5120]{1,0:T(8,128)(2,1)S(1)} %copy-done.3, f32[512,320]{0,1:T(8,128)} %copy.116), kind=kOutput, calls=%fused_computation.68 | convolution fusion | flops 1680834560 | bytes 9502720 | tf_op jit(solution)/shard_map/dot_general | solution.py:38
  173.6 4.6 %convert_bitcast_fusion = bf16[8,512,640]{2,1,0:T(8,128)(2,1)} fusion(bf16[40,8,8,640]{3,2,1,0:T(8,128)(2,1)S(1)} %bitcast.170, bf16[512,320]{0,1:T(8,128)(2,1)S(1)} %fusion.63), kind=kOutput, calls=%fused_computation.20 | convolution fusion | flops 1680343040 | bytes 8847360 | tf_op jit(solution)/shard_map/rk,jnk->jrn/dot_general | solution.py:197
  179.5 28.6 %convolution_convert_fusion = bf16[5120,1280]{1,0:T(8,128)(2,1)} fusion(bf16[1024,5120]{1,0:T(8,128)(2,1)} %bitcast.134, bf16[512,320]{0,1:T(8,128)(2,1)S(1)} %copy-done.27, bf16[512,320]{0,1:T(8,128)(2,1)S(1)} %broadcast_in_dim.76, bf16[512,320]{0,1:T(8,128)(2,1)S(1)} %copy-done.28, bf16[512,640]{0,1:T(8,128)(2,1)S(1)} %bitcast.160), kind=kOutput, calls=%fused_computation.2 | convolution fusion | flops 13441433600 | bytes 25231360 | tf_op jit(solution)/shard_map/dot_general | solution.py:32
  208.1 6.0 %dynamic-slice_bitcast_fusion = bf16[8,320,1280]{2,1,0:T(8,128)(2,1)} fusion(bf16[8,2,320,1280]{3,2,1,0:T(8,128)(2,1)} %bitcast.132, s32[]{:T(128)S(6)} %select_n.17), kind=kLoop, calls=%fused_computation.17 | loop fusion | bytes 13107204 | tf_op jit(solution)/shard_map/jit(dynamic_index_in_dim)/squeeze | solution.py:52
  214.1 10.9 %collective-permute-done.4 = bf16[8,320,1280]{2,1,0:T(8,128)(2,1)} collective-permute-done((bf16[8,320,1280]{2,1,0:T(8,128)(2,1)}, bf16[8,320,1280]{2,1,0:T(8,128)(2,1)}, u32[]{:S(2)}, u32[]{:S(2)}) %collective-permute-start.4) | collective-permute-done | bytes 6553632 | tf_op jit(solution)/shard_map/ppermute | solution.py:54
  225.0 9.0 %fusion.2 = bf16[8,320,1280]{2,1,0:T(8,128)(2,1)} fusion(bf16[8,320,1280]{2,1,0:T(8,128)(2,1)} %collective-permute-done.4, bf16[8,2,320,1280]{3,2,1,0:T(8,128)(2,1)} %bitcast.133, s32[]{:T(128)S(6)} %select_n.16), kind=kLoop, calls=%fused_computation.4 | loop fusion | flops 13107200 | bytes 19660804 | tf_op jit(solution)/shard_map/convert_element_type | solution.py:55
  234.0 8.7 %convolution_convert_fusion.1 = bf16[512,640]{1,0:T(8,128)(2,1)S(1)} fusion(bf16[512,5120]{1,0:T(8,128)(2,1)} %bitcast.136, bf16[640,5120]{1,0:T(8,128)(2,1)} %param.17), kind=kOutput, calls=%fused_computation.53 | convolution fusion | flops 3355770880 | bytes 12451840 | tf_op jit(solution)/shard_map/dot_general | solution.py:38
  244.3 4.9 %fusion.42 = f32[2,5,128,768]{3,2,1,0:T(8,128)S(1)} fusion(bf16[2,256,5,128]{1,3,2,0:T(8,128)(2,1)S(1)} %copy.130, f32[2,5,256,768]{2,3,1,0:T(8,128)} %copy-done.31, f32[2,5,256]{2,1,0:T(8,128)S(1)} %get-tuple-element.52), kind=kOutput, calls=%fused_computation.45 | convolution fusion | flops 507248640 | bytes 12462080 | tf_op jit(solution)/shard_map/shqk,sqhe->skhe/dot_general | solution.py:207
  251.3 4.3 %fusion.47 = f32[2,5,256,768]{2,3,1,0:T(8,128)} fusion(bf16[2,256,5,128]{1,3,2,0:T(8,128)(2,1)S(1)} %copy.130, bf16[2,256,5,128]{1,3,2,0:T(8,128)(2,1)S(1)} %bitcast.147, bf16[2,256,5,128]{1,3,2,0:T(8,128)(2,1)S(1)} %copy-done.16, bf16[2,256,5,128]{1,3,2,0:T(8,128)(2,1)S(1)} %copy-done.18), kind=kOutput, calls=%fused_computation.50 | convolution fusion | flops 509214720 | bytes 10485760 | tf_op jit(solution)/shard_map/sqhe,skhe->shqk/dot_general | solution.py:210
  255.6 14.5 %fusion.16 = f32[2,5,768,128]{2,3,1,0:T(8,128)} fusion(bf16[2,256,5,128]{1,3,2,0:T(8,128)(2,1)S(1)} %bitcast.145, f32[2,5,256,768]{2,3,1,0:T(8,128)} %fusion.47, f32[2,5,256,768]{2,3,1,0:T(8,128)} %copy-done.31, f32[2,5,256]{2,1,0:T(8,128)S(1)} %get-tuple-element.52), kind=kOutput, calls=%fused_computation.22 | convolution fusion | flops 517082368 | bytes 20326400 | tf_op jit(solution)/shard_map/shqk,sqhe->skhe/dot_general | solution.py:220
  278.9 6.2 %all-to-all-start = ((bf16[16,8,320]{2,1,0:T(8,128)(2,1)}), bf16[16,8,320]{2,1,0:T(8,128)(2,1)}, u32[]{:S(2)}, u32[]{:S(2)}) async-start(bf16[16,8,320]{2,1,0:T(8,128)(2,1)} %bitcast.50), calls=%async_computation.3 | async-start | bytes 196608 | tf_op jit(solution)/shard_map/all_to_all | solution.py:188
  285.2 13.5 %fusion.51 = bf16[2,5,128,256]{3,2,1,0:T(8,128)(2,1)} fusion(f32[2,5,256,768]{2,3,1,0:T(8,128)} %fusion.47, bf16[2,256,5,128]{3,1,2,0:T(8,128)(2,1)S(1)} %copy-done.6, bf16[2,256,5,128]{3,1,2,0:T(8,128)(2,1)S(1)} %copy-done.12, bf16[2,256,5,128]{3,1,2,0:T(8,128)(2,1)S(1)} %copy-done.14, f32[2,5,256,768]{2,3,1,0:T(8,128)} %copy-done.31, ...), kind=kOutput, calls=%fused_computation.52 | convolution fusion | flops 523308288 | bytes 18360320 | tf_op jit(solution)/shard_map/shqk,skhe->sqhe/dot_general | solution.py:216
  314.3 97.6 %reduce-scatter.8.cloned.1.call-done = bf16[1,320,1280]{2,1,0:T(8,128)(2,1)} async-done(((bf16[8,320,1280]{2,1,0:T(8,128)(2,1)}), bf16[1,320,1280]{2,1,0:T(8,128)(2,1)}) %reduce-scatter.8.cloned.1.call-update) | async-done | bytes 819216 | tf_op jit(solution)/shard_map/reduce_scatter | solution.py:56
  (134 shorter events, 51.6 us)
Async XLA Ops:
  7.2 13.2 %copy-start = (bf16[128,320]{0,1:T(8,128)(2,1)S(1)}, bf16[128,320]{0,1:T(8,128)(2,1)}, u32[]{:S(2)}) copy-start(bf16[128,320]{0,1:T(8,128)(2,1)} %param.20) | copy-start | bytes 245764
  7.2 11.3 %copy-start.21 = (bf16[1,2,256,640]{3,2,1,0:T(8,128)(2,1)S(1)}, bf16[1,2,256,640]{3,2,1,0:T(8,128)(2,1)}, u32[]{:S(2)}) copy-start(bf16[1,2,256,640]{3,2,1,0:T(8,128)(2,1)} %param.15) | copy-start | bytes 1966084
  7.2 11.6 %copy-start.22 = (bf16[1,2,256,640]{3,2,1,0:T(8,128)(2,1)S(1)}, bf16[1,2,256,640]{3,2,1,0:T(8,128)(2,1)}, u32[]{:S(2)}) copy-start(bf16[1,2,256,640]{3,2,1,0:T(8,128)(2,1)} %param.13) | copy-start | bytes 1966084
  7.2 11.8 %copy-start.23 = (bf16[1,2,256,640]{3,2,1,0:T(8,128)(2,1)S(1)}, bf16[1,2,256,640]{3,2,1,0:T(8,128)(2,1)}, u32[]{:S(2)}) copy-start(bf16[1,2,256,640]{3,2,1,0:T(8,128)(2,1)} %param.14) | copy-start | bytes 1966084
  7.2 13.1 %copy-start.30 = (s32[1,4]{1,0:T(1,128)S(1)}, s32[1,4]{1,0:T(1,128)}, u32[]{:S(2)}) copy-start(s32[1,4]{1,0:T(1,128)} %param.21) | copy-start | bytes 52
  7.2 135.0 %all-gather.2.cloned.1.call-start = ((), (), s32[]{:S(2)}) async-start(), calls=%async_computation.4 | async-start | bytes 11796480 | tf_op jit(solution)/shard_map/all_gather | solution.py:88
  9.9 300.2 %reduce-scatter.4.cloned.1.call-start = ((), (), s32[]{:S(2)}) async-start(), calls=%async_computation.5 | async-start | bytes 5898240 | tf_op jit(solution)/shard_map/reduce_scatter | solution.py:61
  12.1 8.4 %collective-permute-start.1 = (bf16[2,256,640]{1,2,0:T(8,128)(2,1)}, bf16[2,256,640]{1,2,0:T(8,128)(2,1)}, u32[]{:S(2)}, u32[]{:S(2)}) collective-permute-start(bf16[2,256,640]{1,2,0:T(8,128)(2,1)} %bitcast), channel_id=1, source_target_pairs={{0,8},{8,16},{16,24},{24,32},{32,40},{40,48},{48,56},{56,64},{64,7... | collective-permute-start | bytes 1966088 | tf_op jit(solution)/shard_map/ppermute | solution.py:16
  14.3 18.8 %collective-permute-start = (bf16[2,256,640]{1,2,0:T(8,128)(2,1)}, bf16[2,256,640]{1,2,0:T(8,128)(2,1)}, u32[]{:S(2)}, u32[]{:S(2)}) collective-permute-start(bf16[2,256,640]{1,2,0:T(8,128)(2,1)} %bitcast), channel_id=1, source_target_pairs={{0,16},{8,24},{16,32},{24,40},{32,48},{40,56},{48,64},{56,72},{64,... | collective-permute-start | bytes 1966088 | tf_op jit(solution)/shard_map/ppermute | solution.py:16
  18.8 21.8 %copy-start.9 = (bf16[1,2,256,640]{2,3,1,0:T(8,128)(2,1)}, bf16[1,2,256,640]{2,3,1,0:T(8,128)(2,1)S(1)}, u32[]{:S(2)}) copy-start(bf16[1,2,256,640]{2,3,1,0:T(8,128)(2,1)S(1)} %copy.100) | copy-start | bytes 1966084
  19.0 18.7 %copy-start.7 = (bf16[1,2,256,640]{2,3,1,0:T(8,128)(2,1)}, bf16[1,2,256,640]{2,3,1,0:T(8,128)(2,1)S(1)}, u32[]{:S(2)}) copy-start(bf16[1,2,256,640]{2,3,1,0:T(8,128)(2,1)S(1)} %copy.105) | copy-start | bytes 1966084
  19.6 18.1 %copy-start.5 = (bf16[2,256,5,128]{3,1,2,0:T(8,128)(2,1)}, bf16[2,256,5,128]{3,1,2,0:T(8,128)(2,1)S(1)}, u32[]{:S(2)}) copy-start(bf16[2,256,5,128]{3,1,2,0:T(8,128)(2,1)S(1)} %copy.104) | copy-start | bytes 1966084
  163.2 149.0 %reduce-scatter.6.cloned.1.call-start = ((), (), s32[]{:S(2)}) async-start(), calls=%async_computation.6 | async-start | bytes 5898240 | tf_op jit(solution)/shard_map/reduce_scatter | solution.py:61
  178.3 233.6 %reduce-scatter.8.cloned.1.call-start = ((), (), s32[]{:S(2)}) async-start(), calls=%async_computation.7 | async-start | bytes 7372800 | tf_op jit(solution)/shard_map/reduce_scatter | solution.py:56
  214.1 10.9 %collective-permute-start.4 = (bf16[8,320,1280]{2,1,0:T(8,128)(2,1)}, bf16[8,320,1280]{2,1,0:T(8,128)(2,1)}, u32[]{:S(2)}, u32[]{:S(2)}) collective-permute-start(bf16[8,320,1280]{2,1,0:T(8,128)(2,1)} %dynamic-slice_bitcast_fusion), channel_id=1, source_target_pairs={{0,8},{8,0},{1,9},{9,1},{2,10},{10,2},{3,11},{11,3},{4,12},{12,4},... | collective-permute-start | bytes 19660808 | tf_op jit(solution)/shard_map/ppermute | solution.py:54
  270.1 15.1 %copy-start.6 = (bf16[2,256,5,128]{3,1,2,0:T(8,128)(2,1)S(1)}, bf16[2,256,5,128]{3,1,2,0:T(8,128)(2,1)}, u32[]{:S(2)}) copy-start(bf16[2,256,5,128]{3,1,2,0:T(8,128)(2,1)} %copy-done.5) | copy-start | bytes 1966084
  270.1 15.1 %copy-start.12 = (bf16[2,256,5,128]{3,1,2,0:T(8,128)(2,1)S(1)}, bf16[2,256,5,128]{3,1,2,0:T(8,128)(2,1)}, u32[]{:S(2)}) copy-start(bf16[2,256,5,128]{3,1,2,0:T(8,128)(2,1)} %copy-done.11) | copy-start | bytes 1966084
  270.1 15.1 %copy-start.14 = (bf16[2,256,5,128]{3,1,2,0:T(8,128)(2,1)S(1)}, bf16[2,256,5,128]{3,1,2,0:T(8,128)(2,1)}, u32[]{:S(2)}) copy-start(bf16[2,256,5,128]{3,1,2,0:T(8,128)(2,1)} %copy-done.13) | copy-start | bytes 1966084
  273.1 34.3 %collective-permute-start.3 = (bf16[2,256,640]{1,2,0:T(8,128)(2,1)}, bf16[2,256,640]{1,2,0:T(8,128)(2,1)}, u32[]{:S(2)}, u32[]{:S(2)}) collective-permute-start(bf16[2,256,640]{1,2,0:T(8,128)(2,1)} %pad_maximum_fusion.14), channel_id=1, source_target_pairs={{16,0},{24,8},{32,16},{40,24},{48,32},{56,40},{64,48},{72,56},{80,... | collective-permute-start | bytes 1966088 | tf_op jit(solution)/shard_map/ppermute | solution.py:16
  275.3 32.1 %collective-permute-start.2 = (bf16[2,256,640]{1,2,0:T(8,128)(2,1)}, bf16[2,256,640]{1,2,0:T(8,128)(2,1)S(1)}, u32[]{:S(2)}, u32[]{:S(2)}) collective-permute-start(bf16[2,256,640]{1,2,0:T(8,128)(2,1)} %pad_maximum_fusion.13), channel_id=1, source_target_pairs={{8,0},{16,8},{24,16},{32,24},{40,32},{48,40},{56,48},{64,56},{72,6... | collective-permute-start | bytes 1966088 | tf_op jit(solution)/shard_map/ppermute | solution.py:16
  278.9 27.0 %all-to-all-start = ((bf16[16,8,320]{2,1,0:T(8,128)(2,1)}), bf16[16,8,320]{2,1,0:T(8,128)(2,1)}, u32[]{:S(2)}, u32[]{:S(2)}) async-start(bf16[16,8,320]{2,1,0:T(8,128)(2,1)} %bitcast.50), calls=%async_computation.3 | async-start | bytes 196608 | tf_op jit(solution)/shard_map/all_to_all | solution.py:188
  300.1 10.0 %copy-start.19 = (bf16[1,2,256,640]{3,2,1,0:T(8,128)(2,1)S(1)}, bf16[1,2,256,640]{3,2,1,0:T(8,128)(2,1)}, u32[]{:S(2)}) copy-start(bf16[1,2,256,640]{3,2,1,0:T(8,128)(2,1)} %param.12) | copy-start | bytes 1966084
  303.7 8.5 %copy-start.20 = (bf16[1,2,256,640]{3,2,1,0:T(8,128)(2,1)S(1)}, bf16[1,2,256,640]{3,2,1,0:T(8,128)(2,1)}, u32[]{:S(2)}) copy-start(bf16[1,2,256,640]{3,2,1,0:T(8,128)(2,1)} %param.23) | copy-start | bytes 1966084
  310.1 106.0 %copy-start.1 = (bf16[128,320]{0,1:T(8,128)(2,1)S(1)}, bf16[128,320]{0,1:T(8,128)(2,1)}, u32[]{:S(2)}) copy-start(bf16[128,320]{0,1:T(8,128)(2,1)} %param.20) | copy-start | bytes 245764
  (20 other events, 82.3 us)
Sparse Core Ops, SparseCore 0:
  10.3 131.9 all-gather.1
  163.3 59.4 reduce-scatter.3
  225.2 61.7 reduce-scatter.5
  290.9 121.0 reduce-scatter.7

commit v9 on v8

--- a/solution.py
+++ b/solution.py
@@ -85,11 +85,10 @@
     row_count = steps_here * tokens_here
     action_count = actions.shape[1]
     score_scale = HD ** (-0.5)
-    full_both = lax.all_gather(
-        jnp.concatenate([hidden_in, out_grad], axis=0), "tensor", axis=3, tiled=True
-    )
-    input_rows = full_both[0].reshape(row_count, model_width)
-    grad_rows = full_both[1].reshape(row_count, model_width)
+    full_inputs = lax.all_gather(hidden_in, "tensor", axis=3, tiled=True)
+    full_grads = lax.all_gather(out_grad, "tensor", axis=3, tiled=True)
+    input_rows = full_inputs.reshape(row_count, model_width)
+    grad_rows = full_grads.reshape(row_count, model_width)
     own_cache = clean_cache[0]
     nearer = from_behind(own_cache, TM, 1)
     farther = from_behind(own_cache, TM, 2)
@@ -181,7 +180,7 @@
         [attended, branch_act, jnp.zeros((row_count, branch_width), jnp.bfloat16)], axis=1
     )
     terms = contract_rows(
-        full_both.reshape(2 * row_count, model_width),
+        jnp.concatenate([input_rows, grad_rows], axis=0),
         jnp.concatenate([input_side, grad_side], axis=0),
     ).astype(jnp.bfloat16)
     merged = two_stage_scatter(terms).astype(jnp.float32)

time: 429 us -> 422 us (0.984)
  waiting for transfers between devices: 208 us -> 217 us
  matrix products: 106 us -> 97.1 us
  local copies, waits for them, and re-layouts: 49 us -> 41.4 us
    reduce_scatter x1, waiting for transfers between devices: 97.6 us -> 112 us  [two_stage_scatter(): return lax.psum_scatter(paired, 'tmo', scatter_dimension=0, tiled=True)[0]]
    dot_general x1, matrix products: 28.6 us -> 19.6 us  [contract_rows(): lax.dot_general(left, right, (((0,), (0,)), ((), ())), preferred_element_...]
    slice x1 -> x0, local copies, waits for them, and re-layouts: 8.75 us -> none  [body(): grad_rows = full_both[1].reshape(row_count, model_width)]
    all_gather x1 -> x2, waiting for transfers between devices: 88.7 us -> 83.6 us  [the longest x1 44 us: body(): full_grads = lax.all_gather(out_grad, 'tensor', axis=3, tiled=True)]
    unnamed x78 -> x74, local copies, waits for them, and re-layouts: 17.8 us -> 20.2 us
  transfers between devices with their start and end apart: 10 -> 11, of which waited for: 4 -> 5; matrix products, arithmetic and copies ran while one was open for 35% -> 37% of each run, Pallas kernels for 0% -> 0%
where the time goes in v9:
time: 422 us; the launch traced here: 417 us
  waiting for transfers between devices  217 us (51%)
  matrix products  97.1 us (23%)
  local copies, waits for them, and re-layouts  41.4 us (10%)
  other arithmetic  26.2 us (6%)
  starting transfers between devices  19.2 us (5%)
  between operations  15.5 us (4%)
    reduce_scatter x1, waiting for transfers between devices, two_stage_scatter(): return lax.psum_scatter(paired, 'tmo', scatter_dimension=0, tiled=True)[0]  112 us
    all_gather x1, waiting for transfers between devices, body(): full_grads = lax.all_gather(out_grad, 'tensor', axis=3, tiled=True)  44 us
    all_gather x1, waiting for transfers between devices, body(): full_inputs = lax.all_gather(hidden_in, 'tensor', axis=3, tiled=True)  39.6 us
    unnamed x74, local copies, waits for them, and re-layouts  20.2 us
    dot_general x1, matrix products, contract_rows(): lax.dot_general(left, right, (((0,), (0,)), ((), ())), preferred_element_...  19.6 us
    dot_general x1, matrix products, body(): jnp.einsum('shqk,sqhe->skhe', score_grad, query_heads, preferred_element_...  14.5 us
    dot_general x2, matrix products, contract_cols(): lax.dot_general(left, right, (((1,), (1,)), ((), ())), preferred_element_...  13.7 us
    dot_general x1, matrix products, body(): jnp.einsum('shqk,skhe->sqhe', score_grad, key_heads, preferred_element_ty...  13.6 us
  transfers between devices with their start and end apart: 11, of which 5 were waited for; matrix products, arithmetic and copies ran while one was open for 37% of the time, Pallas kernels for 0%

profile of v9, /device:TPU:0, one launch (start us, length us, event | category | flops | bytes accessed | tf_op | source)
XLA Modules:
  0.0 416.8 jit_solution(6765324282256745506)
XLA Ops:
  12.2 5.0 %collective-permute-start = (bf16[2,256,640]{1,2,0:T(8,128)(2,1)}, bf16[2,256,640]{1,2,0:T(8,128)(2,1)}, u32[]{:S(2)}, u32[]{:S(2)}) collective-permute-start(bf16[2,256,640]{1,2,0:T(8,128)(2,1)} %bitcast), channel_id=1, source_target_pairs={{0,16},{8,24},{16,32},{24,40},{32,48},{40,56},{48,64},{56,72},{64,... | collective-permute-start | bytes 1966088 | tf_op jit(solution)/shard_map/ppermute | solution.py:16
  22.0 9.9 %collective-permute-done = bf16[2,256,640]{1,2,0:T(8,128)(2,1)} collective-permute-done((bf16[2,256,640]{1,2,0:T(8,128)(2,1)}, bf16[2,256,640]{1,2,0:T(8,128)(2,1)}, u32[]{:S(2)}, u32[]{:S(2)}) %collective-permute-start) | collective-permute-done | bytes 655392 | tf_op jit(solution)/shard_map/ppermute | solution.py:16
  36.5 2.6 fusion.97
  40.6 2.6 copy-done.29
  45.4 6.9 %fusion.9 = f32[512,8,640]{2,0,1:T(8,128)} fusion(bf16[80,8,8,640]{3,2,1,0:T(8,128)(2,1)S(1)} %bitcast.164, bf16[512,640]{0,1:T(8,128)(2,1)S(1)} %bitcast.154), kind=kOutput, calls=%fused_computation.17 | convolution fusion | flops 3355443200 | bytes 17694720 | tf_op jit(solution)/shard_map/rk,kjn->jrn/dot_general | solution.py:152
  52.3 39.6 %all-gather.3.cloned.1.call-done = bf16[1,2,256,5120]{3,2,1,0:T(8,128)(2,1)} async-done(((bf16[1,2,256,640]{3,2,1,0:T(8,128)(2,1)}), bf16[1,2,256,5120]{3,2,1,0:T(8,128)(2,1)}) %all-gather.3.cloned.1.call-update) | async-done | bytes 5242896 | tf_op jit(solution)/shard_map/all_gather | solution.py:88
  91.9 7.5 %fusion.71 = (bf16[2,4,64,320]{3,2,1,0:T(8,128)(2,1)S(1)}, f32[2,4,64,320]{3,2,1,0:T(8,128)}) fusion(f32[4,320]{1,0:T(4,128)S(1)} %fusion.79, bf16[2,4,64,5120]{3,2,1,0:T(8,128)(2,1)} %bitcast.168, bf16[5120,320]{0,1:T(8,128)(2,1)} %param.18), kind=kOutput, calls=%fused_computation.81 | convolution fusion | flops 1679360000 | bytes 9507840 | tf_op jit(solution)/shard_map/dot_general | solution.py:143
  99.4 4.6 %fusion.14 = bf16[8,512,640]{2,1,0:T(8,128)(2,1)} fusion(f32[512,8,640]{2,0,1:T(8,128)S(1)} %copy-done.2, bf16[512,320,1]{1,0,2:T(8,128)(2,1)S(1)} %bitcast.161, bf16[40,8,8,640]{3,2,1,0:T(8,128)(2,1)S(1)} %bitcast.133), kind=kOutput, calls=%fused_computation.21 | convolution fusion | flops 1682964480 | bytes 19333120 | tf_op jit(solution)/shard_map/rk,kjn->jrn/dot_general | solution.py:157
  104.1 2.2 copy.116
  108.4 44.0 %all-gather.5.cloned.1.call-done = bf16[1,2,256,5120]{3,2,1,0:T(8,128)(2,1)} async-done(((bf16[1,2,256,640]{3,2,1,0:T(8,128)(2,1)}), bf16[1,2,256,5120]{3,2,1,0:T(8,128)(2,1)}) %all-gather.5.cloned.1.call-update) | async-done | bytes 5242896 | tf_op jit(solution)/shard_map/all_gather | solution.py:89
  152.4 4.9 %fusion.66 = bf16[512,320]{0,1:T(8,128)(2,1)S(1)} fusion(bf16[512,5120]{1,0:T(8,128)(2,1)} %bitcast.165, bf16[320,5120]{1,0:T(8,128)(2,1)S(1)} %copy-done.3, f32[512,320]{0,1:T(8,128)} %copy.116), kind=kOutput, calls=%fused_computation.70 | convolution fusion | flops 1680834560 | bytes 9502720 | tf_op jit(solution)/shard_map/dot_general | solution.py:38
  158.1 4.6 %convert_bitcast_fusion = bf16[8,512,640]{2,1,0:T(8,128)(2,1)} fusion(bf16[40,8,8,640]{3,2,1,0:T(8,128)(2,1)S(1)} %bitcast.170, bf16[512,320]{0,1:T(8,128)(2,1)S(1)} %fusion.66), kind=kOutput, calls=%fused_computation.23 | convolution fusion | flops 1680343040 | bytes 8847360 | tf_op jit(solution)/shard_map/rk,jnk->jrn/dot_general | solution.py:196
  164.0 19.6 %convolution_convert_fusion = bf16[5120,1280]{1,0:T(8,128)(2,1)} fusion(bf16[512,5120]{1,0:T(8,128)(2,1)} %bitcast.166, bf16[512,5120]{1,0:T(8,128)(2,1)} %bitcast.169, bf16[512,320]{0,1:T(8,128)(2,1)S(1)} %copy-done.25, bf16[512,320]{0,1:T(8,128)(2,1)S(1)} %broadcast_in_dim.76, bf16[512,320]{0,1:T(8,128)(2,1)S(1)} %copy-done.26, ...), kind=kOutput, calls=%fused_computation.2 | convolution fusion | flops 13462405120 | bytes 25231360 | tf_op jit(solution)/shard_map/dot_general | solution.py:32
  183.6 6.1 %dynamic-slice_bitcast_fusion = bf16[8,320,1280]{2,1,0:T(8,128)(2,1)} fusion(bf16[8,2,320,1280]{3,2,1,0:T(8,128)(2,1)} %bitcast.131, s32[]{:T(128)S(6)} %select_n.17), kind=kLoop, calls=%fused_computation.20 | loop fusion | bytes 13107204 | tf_op jit(solution)/shard_map/jit(dynamic_index_in_dim)/squeeze | solution.py:52
  190.0 10.9 %collective-permute-done.4 = bf16[8,320,1280]{2,1,0:T(8,128)(2,1)} collective-permute-done((bf16[8,320,1280]{2,1,0:T(8,128)(2,1)}, bf16[8,320,1280]{2,1,0:T(8,128)(2,1)}, u32[]{:S(2)}, u32[]{:S(2)}) %collective-permute-start.4) | collective-permute-done | bytes 6553632 | tf_op jit(solution)/shard_map/ppermute | solution.py:54
  200.8 9.2 %fusion.2 = bf16[8,320,1280]{2,1,0:T(8,128)(2,1)} fusion(bf16[8,320,1280]{2,1,0:T(8,128)(2,1)} %collective-permute-done.4, bf16[8,2,320,1280]{3,2,1,0:T(8,128)(2,1)} %bitcast.132, s32[]{:T(128)S(6)} %select_n.16), kind=kLoop, calls=%fused_computation.4 | loop fusion | flops 13107200 | bytes 19660804 | tf_op jit(solution)/shard_map/convert_element_type | solution.py:55
  210.1 8.8 %convolution_convert_fusion.1 = bf16[512,640]{1,0:T(8,128)(2,1)S(1)} fusion(bf16[512,5120]{1,0:T(8,128)(2,1)} %bitcast.167, bf16[640,5120]{1,0:T(8,128)(2,1)} %param.17), kind=kOutput, calls=%fused_computation.56 | convolution fusion | flops 3355770880 | bytes 12451840 | tf_op jit(solution)/shard_map/dot_general | solution.py:38
  220.3 4.8 %fusion.45 = f32[2,5,128,768]{3,2,1,0:T(8,128)S(1)} fusion(bf16[2,256,5,128]{1,3,2,0:T(8,128)(2,1)S(1)} %copy.130, f32[2,5,256,768]{2,3,1,0:T(8,128)} %copy-done.29, f32[2,5,256]{2,1,0:T(8,128)S(1)} %get-tuple-element.50), kind=kOutput, calls=%fused_computation.48 | convolution fusion | flops 507248640 | bytes 12462080 | tf_op jit(solution)/shard_map/shqk,sqhe->skhe/dot_general | solution.py:206
  227.2 4.3 %fusion.50 = f32[2,5,256,768]{2,3,1,0:T(8,128)} fusion(bf16[2,256,5,128]{1,3,2,0:T(8,128)(2,1)S(1)} %copy.130, bf16[2,256,5,128]{1,3,2,0:T(8,128)(2,1)S(1)} %bitcast.142, bf16[2,256,5,128]{1,3,2,0:T(8,128)(2,1)S(1)} %copy-done.16, bf16[2,256,5,128]{1,3,2,0:T(8,128)(2,1)S(1)} %copy-done.18), kind=kOutput, calls=%fused_computation.53 | convolution fusion | flops 509214720 | bytes 10485760 | tf_op jit(solution)/shard_map/sqhe,skhe->shqk/dot_general | solution.py:209
  231.4 14.5 %fusion.19 = f32[2,5,768,128]{2,3,1,0:T(8,128)} fusion(bf16[2,256,5,128]{1,3,2,0:T(8,128)(2,1)S(1)} %bitcast.140, f32[2,5,256,768]{2,3,1,0:T(8,128)} %fusion.50, f32[2,5,256,768]{2,3,1,0:T(8,128)} %copy-done.29, f32[2,5,256]{2,1,0:T(8,128)S(1)} %get-tuple-element.50), kind=kOutput, calls=%fused_computation.25 | convolution fusion | flops 517082368 | bytes 20326400 | tf_op jit(solution)/shard_map/shqk,sqhe->skhe/dot_general | solution.py:219
  254.8 9.9 %all-to-all-start = ((bf16[16,8,320]{2,1,0:T(8,128)(2,1)}), bf16[16,8,320]{2,1,0:T(8,128)(2,1)}, u32[]{:S(2)}, u32[]{:S(2)}) async-start(bf16[16,8,320]{2,1,0:T(8,128)(2,1)} %bitcast.50), calls=%async_computation.3 | async-start | bytes 196608 | tf_op jit(solution)/shard_map/all_to_all | solution.py:187
  264.7 13.6 %fusion.54 = bf16[2,5,128,256]{3,2,1,0:T(8,128)(2,1)} fusion(f32[2,5,256,768]{2,3,1,0:T(8,128)} %fusion.50, bf16[2,256,5,128]{3,1,2,0:T(8,128)(2,1)S(1)} %copy-done.6, bf16[2,256,5,128]{3,1,2,0:T(8,128)(2,1)S(1)} %copy-done.12, bf16[2,256,5,128]{3,1,2,0:T(8,128)(2,1)S(1)} %copy-done.14, f32[2,5,256,768]{2,3,1,0:T(8,128)} %copy-done.29, ...), kind=kOutput, calls=%fused_computation.55 | convolution fusion | flops 523308288 | bytes 18360320 | tf_op jit(solution)/shard_map/shqk,skhe->sqhe/dot_general | solution.py:215
  281.2 2.2 copy.136
  294.0 111.6 %reduce-scatter.8.cloned.1.call-done = bf16[1,320,1280]{2,1,0:T(8,128)(2,1)} async-done(((bf16[8,320,1280]{2,1,0:T(8,128)(2,1)}), bf16[1,320,1280]{2,1,0:T(8,128)(2,1)}) %reduce-scatter.8.cloned.1.call-update) | async-done | bytes 819216 | tf_op jit(solution)/shard_map/reduce_scatter | solution.py:56
  (131 shorter events, 51.2 us)
Async XLA Ops:
  7.2 14.3 %copy-start = (bf16[128,320]{0,1:T(8,128)(2,1)S(1)}, bf16[128,320]{0,1:T(8,128)(2,1)}, u32[]{:S(2)}) copy-start(bf16[128,320]{0,1:T(8,128)(2,1)} %param.20) | copy-start | bytes 245764
  7.2 13.0 %copy-start.21 = (bf16[1,2,256,640]{3,2,1,0:T(8,128)(2,1)S(1)}, bf16[1,2,256,640]{3,2,1,0:T(8,128)(2,1)}, u32[]{:S(2)}) copy-start(bf16[1,2,256,640]{3,2,1,0:T(8,128)(2,1)} %param.14) | copy-start | bytes 1966084
  7.2 14.3 %copy-start.28 = (s32[1,4]{1,0:T(1,128)S(1)}, s32[1,4]{1,0:T(1,128)}, u32[]{:S(2)}) copy-start(s32[1,4]{1,0:T(1,128)} %param.21) | copy-start | bytes 52
  7.2 84.7 %all-gather.3.cloned.1.call-start = ((), (), s32[]{:S(2)}) async-start(), calls=%async_computation.4 | async-start | bytes 5898240 | tf_op jit(solution)/shard_map/all_gather | solution.py:88
  7.9 144.4 %all-gather.5.cloned.1.call-start = ((), (), s32[]{:S(2)}) async-start(), calls=%async_computation.6 | async-start | bytes 5898240 | tf_op jit(solution)/shard_map/all_gather | solution.py:89
  8.7 281.1 %reduce-scatter.4.cloned.1.call-start = ((), (), s32[]{:S(2)}) async-start(), calls=%async_computation.5 | async-start | bytes 5898240 | tf_op jit(solution)/shard_map/reduce_scatter | solution.py:61
  10.9 10.8 %collective-permute-start.1 = (bf16[2,256,640]{1,2,0:T(8,128)(2,1)}, bf16[2,256,640]{1,2,0:T(8,128)(2,1)S(1)}, u32[]{:S(2)}, u32[]{:S(2)}) collective-permute-start(bf16[2,256,640]{1,2,0:T(8,128)(2,1)} %bitcast), channel_id=1, source_target_pairs={{0,8},{8,16},{16,24},{24,32},{32,40},{40,48},{48,56},{56,64},{64,7... | collective-permute-start | bytes 1966088 | tf_op jit(solution)/shard_map/ppermute | solution.py:16
  12.2 19.6 %collective-permute-start = (bf16[2,256,640]{1,2,0:T(8,128)(2,1)}, bf16[2,256,640]{1,2,0:T(8,128)(2,1)}, u32[]{:S(2)}, u32[]{:S(2)}) collective-permute-start(bf16[2,256,640]{1,2,0:T(8,128)(2,1)} %bitcast), channel_id=1, source_target_pairs={{0,16},{8,24},{16,32},{24,40},{32,48},{40,56},{48,64},{56,72},{64,... | collective-permute-start | bytes 1966088 | tf_op jit(solution)/shard_map/ppermute | solution.py:16
  18.6 20.7 %copy-start.9 = (bf16[1,2,256,640]{2,3,1,0:T(8,128)(2,1)}, bf16[1,2,256,640]{2,3,1,0:T(8,128)(2,1)S(1)}, u32[]{:S(2)}) copy-start(bf16[1,2,256,640]{2,3,1,0:T(8,128)(2,1)S(1)} %copy.100) | copy-start | bytes 1966084
  20.2 16.3 %copy-start.7 = (bf16[1,2,256,640]{2,3,1,0:T(8,128)(2,1)}, bf16[1,2,256,640]{2,3,1,0:T(8,128)(2,1)S(1)}, u32[]{:S(2)}) copy-start(bf16[1,2,256,640]{2,3,1,0:T(8,128)(2,1)S(1)} %copy.105) | copy-start | bytes 1966084
  20.8 15.7 %copy-start.5 = (bf16[2,256,5,128]{3,1,2,0:T(8,128)(2,1)}, bf16[2,256,5,128]{3,1,2,0:T(8,128)(2,1)S(1)}, u32[]{:S(2)}) copy-start(bf16[2,256,5,128]{3,1,2,0:T(8,128)(2,1)S(1)} %copy.104) | copy-start | bytes 1966084
  91.9 7.5 %copy-start.3 = (bf16[320,5120]{1,0:T(8,128)(2,1)S(1)}, bf16[320,5120]{1,0:T(8,128)(2,1)}, u32[]{:S(2)}) copy-start(bf16[320,5120]{1,0:T(8,128)(2,1)} %param.19) | copy-start | bytes 9830404
  104.1 187.8 %reduce-scatter.6.cloned.1.call-start = ((), (), s32[]{:S(2)}) async-start(), calls=%async_computation.7 | async-start | bytes 5898240 | tf_op jit(solution)/shard_map/reduce_scatter | solution.py:61
  162.7 242.9 %reduce-scatter.8.cloned.1.call-start = ((), (), s32[]{:S(2)}) async-start(), calls=%async_computation.8 | async-start | bytes 7372800 | tf_op jit(solution)/shard_map/reduce_scatter | solution.py:56
  189.7 11.1 %collective-permute-start.4 = (bf16[8,320,1280]{2,1,0:T(8,128)(2,1)}, bf16[8,320,1280]{2,1,0:T(8,128)(2,1)}, u32[]{:S(2)}, u32[]{:S(2)}) collective-permute-start(bf16[8,320,1280]{2,1,0:T(8,128)(2,1)} %dynamic-slice_bitcast_fusion), channel_id=1, source_target_pairs={{0,8},{8,0},{1,9},{9,1},{2,10},{10,2},{3,11},{11,3},{4,12},{12,4},... | collective-permute-start | bytes 19660808 | tf_op jit(solution)/shard_map/ppermute | solution.py:54
  246.0 18.7 %copy-start.6 = (bf16[2,256,5,128]{3,1,2,0:T(8,128)(2,1)S(1)}, bf16[2,256,5,128]{3,1,2,0:T(8,128)(2,1)}, u32[]{:S(2)}) copy-start(bf16[2,256,5,128]{3,1,2,0:T(8,128)(2,1)} %copy-done.5) | copy-start | bytes 1966084
  246.0 18.7 %copy-start.12 = (bf16[2,256,5,128]{3,1,2,0:T(8,128)(2,1)S(1)}, bf16[2,256,5,128]{3,1,2,0:T(8,128)(2,1)}, u32[]{:S(2)}) copy-start(bf16[2,256,5,128]{3,1,2,0:T(8,128)(2,1)} %copy-done.11) | copy-start | bytes 1966084
  246.0 18.7 %copy-start.14 = (bf16[2,256,5,128]{3,1,2,0:T(8,128)(2,1)S(1)}, bf16[2,256,5,128]{3,1,2,0:T(8,128)(2,1)}, u32[]{:S(2)}) copy-start(bf16[2,256,5,128]{3,1,2,0:T(8,128)(2,1)} %copy-done.13) | copy-start | bytes 1966084
  249.0 38.1 %collective-permute-start.3 = (bf16[2,256,640]{1,2,0:T(8,128)(2,1)}, bf16[2,256,640]{1,2,0:T(8,128)(2,1)}, u32[]{:S(2)}, u32[]{:S(2)}) collective-permute-start(bf16[2,256,640]{1,2,0:T(8,128)(2,1)} %pad_maximum_fusion.13), channel_id=1, source_target_pairs={{16,0},{24,8},{32,16},{40,24},{48,32},{56,40},{64,48},{72,56},{80,... | collective-permute-start | bytes 1966088 | tf_op jit(solution)/shard_map/ppermute | solution.py:16
  251.2 35.9 %collective-permute-start.2 = (bf16[2,256,640]{1,2,0:T(8,128)(2,1)}, bf16[2,256,640]{1,2,0:T(8,128)(2,1)S(1)}, u32[]{:S(2)}, u32[]{:S(2)}) collective-permute-start(bf16[2,256,640]{1,2,0:T(8,128)(2,1)} %pad_maximum_fusion.12), channel_id=1, source_target_pairs={{8,0},{16,8},{24,16},{32,24},{40,32},{48,40},{56,48},{64,56},{72,6... | collective-permute-start | bytes 1966088 | tf_op jit(solution)/shard_map/ppermute | solution.py:16
  254.8 30.8 %all-to-all-start = ((bf16[16,8,320]{2,1,0:T(8,128)(2,1)}), bf16[16,8,320]{2,1,0:T(8,128)(2,1)}, u32[]{:S(2)}, u32[]{:S(2)}) async-start(bf16[16,8,320]{2,1,0:T(8,128)(2,1)} %bitcast.50), calls=%async_computation.3 | async-start | bytes 196608 | tf_op jit(solution)/shard_map/all_to_all | solution.py:187
  279.7 10.0 %copy-start.19 = (bf16[1,2,256,640]{3,2,1,0:T(8,128)(2,1)S(1)}, bf16[1,2,256,640]{3,2,1,0:T(8,128)(2,1)}, u32[]{:S(2)}) copy-start(bf16[1,2,256,640]{3,2,1,0:T(8,128)(2,1)} %param.12) | copy-start | bytes 1966084
  283.4 8.5 %copy-start.20 = (bf16[1,2,256,640]{3,2,1,0:T(8,128)(2,1)S(1)}, bf16[1,2,256,640]{3,2,1,0:T(8,128)(2,1)}, u32[]{:S(2)}) copy-start(bf16[1,2,256,640]{3,2,1,0:T(8,128)(2,1)} %param.23) | copy-start | bytes 1966084
  289.8 120.0 %copy-start.1 = (bf16[128,320]{0,1:T(8,128)(2,1)S(1)}, bf16[128,320]{0,1:T(8,128)(2,1)}, u32[]{:S(2)}) copy-start(bf16[128,320]{0,1:T(8,128)(2,1)} %param.20) | copy-start | bytes 245764
  (19 other events, 73.9 us)
Sparse Core Ops, SparseCore 0:
  9.7 82.1 all-gather.2
  93.5 58.7 all-gather.4
  154.8 61.7 reduce-scatter.3
  218.9 62.6 reduce-scatter.5
  285.4 120.1 reduce-scatter.7

commit v10 on v9

--- a/solution.py
+++ b/solution.py
@@ -160,8 +160,6 @@
         branch_out.reshape(-1, group_count, group_width),
         preferred_element_type=jnp.float32,
     )
-    layer_sum = sum_over_groups(partial_value.astype(jnp.bfloat16), steps_here, tokens_here)
-    layer_out = (hidden_in.astype(jnp.float32) + layer_sum).astype(jnp.bfloat16)
     attended_grad = contract_cols(grad_rows, out_proj).astype(jnp.bfloat16)
     pre_grad = (contract_cols(grad_rows, branch_out) * gelu_slope(pre_act)).astype(jnp.bfloat16)
     tm_count = lax.axis_size(TM)
@@ -199,7 +197,16 @@
         branch_in.reshape(group_count, group_width, -1),
         preferred_element_type=jnp.float32,
     )
-    input_sum = sum_over_groups(input_term.astype(jnp.bfloat16), steps_here, tokens_here)
+    layer_sum, input_sum = jnp.split(
+        sum_over_groups(
+            jnp.concatenate([partial_value, input_term], axis=1).astype(jnp.bfloat16),
+            2 * steps_here,
+            tokens_here,
+        ),
+        2,
+        axis=1,
+    )
+    layer_out = (hidden_in.astype(jnp.float32) + layer_sum).astype(jnp.bfloat16)
     input_grad = (out_grad.astype(jnp.float32) + input_sum).astype(jnp.bfloat16)
     weight_grads = (summed, input_grad)
     grad_heads = attended_grad.reshape(steps_here, tokens_here, heads_here, HD)

time: 422 us -> 438 us (1.038)
  waiting for transfers between devices: 217 us -> 230 us
    reduce_scatter x1, waiting for transfers between devices: 112 us -> 0.01 us  [two_stage_scatter(): return lax.psum_scatter(paired, 'tmo', scatter_dimension=0, tiled=True)[0]]
    reduce_scatter x2 -> x1, waiting for transfers between devices: 0.01 us -> 106 us  [sum_over_groups(): lax.psum_scatter(partial, 'tensor', scatter_dimension=0, tiled=True)]
    all_gather x1, waiting for transfers between devices: 39.6 us -> 47.5 us  [body(): full_inputs = lax.all_gather(hidden_in, 'tensor', axis=3, tiled=True)]
    all_to_all x1, waiting for transfers between devices: 0.01 us -> 5.94 us  [body(): lax.all_to_all(table_term.astype(jnp.bfloat16).reshape(tm_count, -1, bran...]
    concatenate x0 -> x1, other arithmetic: none -> 5.35 us  [body(): jnp.concatenate([partial_value, input_term], axis=1).astype(jnp.bfloat16)]
    all_gather x1, waiting for transfers between devices: 44 us -> 48.6 us  [body(): full_grads = lax.all_gather(out_grad, 'tensor', axis=3, tiled=True)]
    unnamed x74 -> x64, local copies, waits for them, and re-layouts: 20.2 us -> 17.9 us
  transfers between devices with their start and end apart: 11 -> 10, of which waited for: 5 -> 6; matrix products, arithmetic and copies ran while one was open for 37% -> 28% of each run, Pallas kernels for 0% -> 0%
where the time goes in v10:
time: 438 us; the launch traced here: 432 us
  waiting for transfers between devices  230 us (53%)
  matrix products  97.8 us (22%)
  local copies, waits for them, and re-layouts  39.1 us (9%)
  other arithmetic  30.3 us (7%)
  starting transfers between devices  18.8 us (4%)
  between operations  15.3 us (3%)
    reduce_scatter x1, waiting for transfers between devices, sum_over_groups(): lax.psum_scatter(partial, 'tensor', scatter_dimension=0, tiled=True)  106 us
    all_gather x1, waiting for transfers between devices, body(): full_grads = lax.all_gather(out_grad, 'tensor', axis=3, tiled=True)  48.6 us
    all_gather x1, waiting for transfers between devices, body(): full_inputs = lax.all_gather(hidden_in, 'tensor', axis=3, tiled=True)  47.5 us
    dot_general x1, matrix products, contract_rows(): lax.dot_general(left, right, (((0,), (0,)), ((), ())), preferred_element_...  19.9 us
    unnamed x64, local copies, waits for them, and re-layouts  17.9 us
    dot_general x1, matrix products, body(): jnp.einsum('shqk,sqhe->skhe', score_grad, query_heads, preferred_element_...  14.5 us
    dot_general x2, matrix products, contract_cols(): lax.dot_general(left, right, (((1,), (1,)), ((), ())), preferred_element_...  14.4 us
    dot_general x1, matrix products, body(): jnp.einsum('shqk,skhe->sqhe', score_grad, key_heads, preferred_element_ty...  13.6 us
  transfers between devices with their start and end apart: 10, of which 6 were waited for; matrix products, arithmetic and copies ran while one was open for 28% of the time, Pallas kernels for 0%

profile of v10, /device:TPU:0, one launch (start us, length us, event | category | flops | bytes accessed | tf_op | source)
XLA Modules:
  0.0 431.7 jit_solution(10747974195949025902)
XLA Ops:
  12.2 5.0 %collective-permute-start = (bf16[2,256,640]{1,2,0:T(8,128)(2,1)}, bf16[2,256,640]{1,2,0:T(8,128)(2,1)}, u32[]{:S(2)}, u32[]{:S(2)}) collective-permute-start(bf16[2,256,640]{1,2,0:T(8,128)(2,1)} %bitcast), channel_id=1, source_target_pairs={{0,16},{8,24},{16,32},{24,40},{32,48},{40,56},{48,64},{56,72},{64,... | collective-permute-start | bytes 1966088 | tf_op jit(solution)/shard_map/ppermute | solution.py:16
  22.0 9.8 %collective-permute-done = bf16[2,256,640]{1,2,0:T(8,128)(2,1)} collective-permute-done((bf16[2,256,640]{1,2,0:T(8,128)(2,1)}, bf16[2,256,640]{1,2,0:T(8,128)(2,1)}, u32[]{:S(2)}, u32[]{:S(2)}) %collective-permute-start) | collective-permute-done | bytes 655392 | tf_op jit(solution)/shard_map/ppermute | solution.py:16
  36.5 2.6 fusion.97
  44.4 47.5 %all-gather.3.cloned.1.call-done = bf16[1,2,256,5120]{3,2,1,0:T(8,128)(2,1)} async-done(((bf16[1,2,256,640]{3,2,1,0:T(8,128)(2,1)}), bf16[1,2,256,5120]{3,2,1,0:T(8,128)(2,1)}) %all-gather.3.cloned.1.call-update) | async-done | bytes 5242896 | tf_op jit(solution)/shard_map/all_gather | solution.py:88
  91.9 7.7 %fusion.71 = (bf16[2,4,64,320]{3,2,1,0:T(8,128)(2,1)}, f32[2,4,64,320]{3,2,1,0:T(8,128)}) fusion(f32[4,320]{1,0:T(4,128)S(1)} %fusion.79, bf16[2,4,64,5120]{3,2,1,0:T(8,128)(2,1)} %bitcast.163, bf16[5120,320]{0,1:T(8,128)(2,1)} %param.18), kind=kOutput, calls=%fused_computation.82 | convolution fusion | flops 1679360000 | bytes 9507840 | tf_op jit(solution)/shard_map/dot_general | solution.py:143
  99.6 2.2 copy.116
  103.8 48.6 %all-gather.5.cloned.1.call-done = bf16[1,2,256,5120]{3,2,1,0:T(8,128)(2,1)} async-done(((bf16[1,2,256,640]{3,2,1,0:T(8,128)(2,1)}), bf16[1,2,256,5120]{3,2,1,0:T(8,128)(2,1)}) %all-gather.5.cloned.1.call-update) | async-done | bytes 5242896 | tf_op jit(solution)/shard_map/all_gather | solution.py:89
  152.4 5.5 %fusion.66 = bf16[512,320]{0,1:T(8,128)(2,1)} fusion(bf16[512,5120]{1,0:T(8,128)(2,1)} %bitcast.160, bf16[320,5120]{1,0:T(8,128)(2,1)S(1)} %copy-done.2, f32[512,320]{0,1:T(8,128)} %copy.116), kind=kOutput, calls=%fused_computation.71 | convolution fusion | flops 1680834560 | bytes 9502720 | tf_op jit(solution)/shard_map/dot_general | solution.py:38
  157.9 19.9 %convolution_convert_fusion = bf16[5120,1280]{1,0:T(8,128)(2,1)} fusion(bf16[512,5120]{1,0:T(8,128)(2,1)} %bitcast.161, bf16[512,5120]{1,0:T(8,128)(2,1)} %bitcast.164, bf16[512,320]{0,1:T(8,128)(2,1)} %fusion.66, bf16[512,320]{0,1:T(8,128)(2,1)S(1)} %broadcast_in_dim.76, bf16[512,320]{0,1:T(8,128)(2,1)} %multiply_convert_fusion.1, ...), kind=kOutput, calls=%fused_computation.2 | convolution fusion | flops 13462405120 | bytes 25231360 | tf_op jit(solution)/shard_map/dot_general | solution.py:32
  177.9 6.0 %dynamic-slice_bitcast_fusion = bf16[8,320,1280]{2,1,0:T(8,128)(2,1)} fusion(bf16[8,2,320,1280]{3,2,1,0:T(8,128)(2,1)} %bitcast.129, s32[]{:T(128)S(6)} %select_n.17), kind=kLoop, calls=%fused_computation.21 | loop fusion | bytes 13107204 | tf_op jit(solution)/shard_map/jit(dynamic_index_in_dim)/squeeze | solution.py:52
  183.9 10.9 %collective-permute-done.4 = bf16[8,320,1280]{2,1,0:T(8,128)(2,1)} collective-permute-done((bf16[8,320,1280]{2,1,0:T(8,128)(2,1)}, bf16[8,320,1280]{2,1,0:T(8,128)(2,1)}, u32[]{:S(2)}, u32[]{:S(2)}) %collective-permute-start.4) | collective-permute-done | bytes 6553632 | tf_op jit(solution)/shard_map/ppermute | solution.py:54
  194.7 9.1 %fusion.2 = bf16[8,320,1280]{2,1,0:T(8,128)(2,1)} fusion(bf16[8,320,1280]{2,1,0:T(8,128)(2,1)} %collective-permute-done.4, bf16[8,2,320,1280]{3,2,1,0:T(8,128)(2,1)} %bitcast.130, s32[]{:T(128)S(6)} %select_n.16), kind=kLoop, calls=%fused_computation.4 | loop fusion | flops 13107200 | bytes 19660804 | tf_op jit(solution)/shard_map/convert_element_type | solution.py:55
  204.9 6.9 %fusion.9 = f32[512,8,640]{2,0,1:T(8,128)S(1)} fusion(bf16[80,8,8,640]{3,2,1,0:T(8,128)(2,1)} %bitcast.159, bf16[512,640]{0,1:T(8,128)(2,1)S(1)} %bitcast.156), kind=kOutput, calls=%fused_computation.18 | convolution fusion | flops 3355443200 | bytes 17694720 | tf_op jit(solution)/shard_map/rk,kjn->jrn/dot_general | solution.py:152
  211.9 3.2 convert_bitcast_fusion
  215.0 5.3 %fusion.14 = bf16[8,512,640]{2,1,0:T(8,128)(2,1)S(1)} fusion(f32[512,8,640]{2,0,1:T(8,128)S(1)} %fusion.9, bf16[512,320,1]{1,0,2:T(8,128)(2,1)S(1)} %bitcast.158, bf16[40,8,8,640]{3,2,1,0:T(8,128)(2,1)} %bitcast.131), kind=kOutput, calls=%fused_computation.22 | convolution fusion | flops 1682964480 | bytes 19333120 | tf_op jit(solution)/shard_map/rk,kjn->jrn/dot_general | solution.py:157
  220.3 5.3 %pad_maximum_fusion = bf16[8,1024,640]{2,1,0:T(8,128)(2,1)} fusion(bf16[8,512,640]{2,1,0:T(8,128)(2,1)S(1)} %convert_bitcast_fusion, bf16[8,512,640]{2,1,0:T(8,128)(2,1)S(1)} %fusion.14), kind=kLoop, calls=%fused_computation.5 | loop fusion | flops 20971520 | bytes 20971520 | tf_op jit(solution)/shard_map/concatenate | solution.py:202
  225.7 8.9 %convolution_convert_fusion.1 = bf16[512,640]{1,0:T(8,128)(2,1)S(1)} fusion(bf16[512,5120]{1,0:T(8,128)(2,1)} %bitcast.162, bf16[640,5120]{1,0:T(8,128)(2,1)} %param.17), kind=kOutput, calls=%fused_computation.57 | convolution fusion | flops 3355770880 | bytes 12451840 | tf_op jit(solution)/shard_map/dot_general | solution.py:38
  236.2 4.8 %fusion.45 = f32[2,5,128,768]{3,2,1,0:T(8,128)S(1)} fusion(bf16[2,256,5,128]{1,3,2,0:T(8,128)(2,1)S(1)} %copy.130, f32[2,5,256,768]{2,3,1,0:T(8,128)} %copy-done.26, f32[2,5,256]{2,1,0:T(8,128)S(1)} %get-tuple-element.52), kind=kOutput, calls=%fused_computation.49 | convolution fusion | flops 507248640 | bytes 12462080 | tf_op jit(solution)/shard_map/shqk,sqhe->skhe/dot_general | solution.py:213
  243.1 4.3 %fusion.50 = f32[2,5,256,768]{2,3,1,0:T(8,128)} fusion(bf16[2,256,5,128]{1,3,2,0:T(8,128)(2,1)S(1)} %copy.130, bf16[2,256,5,128]{1,3,2,0:T(8,128)(2,1)S(1)} %bitcast.140, bf16[2,256,5,128]{1,3,2,0:T(8,128)(2,1)S(1)} %copy-done.15, bf16[2,256,5,128]{1,3,2,0:T(8,128)(2,1)S(1)} %copy-done.17), kind=kOutput, calls=%fused_computation.54 | convolution fusion | flops 509214720 | bytes 10485760 | tf_op jit(solution)/shard_map/sqhe,skhe->shqk/dot_general | solution.py:216
  247.5 14.5 %fusion.19 = f32[2,5,768,128]{2,3,1,0:T(8,128)} fusion(bf16[2,256,5,128]{1,3,2,0:T(8,128)(2,1)S(1)} %bitcast.138, f32[2,5,256,768]{2,3,1,0:T(8,128)} %fusion.50, f32[2,5,256,768]{2,3,1,0:T(8,128)} %copy-done.26, f32[2,5,256]{2,1,0:T(8,128)S(1)} %get-tuple-element.52), kind=kOutput, calls=%fused_computation.26 | convolution fusion | flops 517082368 | bytes 20326400 | tf_op jit(solution)/shard_map/shqk,sqhe->skhe/dot_general | solution.py:226
  270.8 9.7 %all-to-all-start = ((bf16[16,8,320]{2,1,0:T(8,128)(2,1)}), bf16[16,8,320]{2,1,0:T(8,128)(2,1)}, u32[]{:S(2)}, u32[]{:S(2)}) async-start(bf16[16,8,320]{2,1,0:T(8,128)(2,1)} %bitcast.50), calls=%async_computation.2 | async-start | bytes 196608 | tf_op jit(solution)/shard_map/all_to_all | solution.py:185
  280.6 13.6 %fusion.54 = bf16[2,5,128,256]{3,2,1,0:T(8,128)(2,1)} fusion(f32[2,5,256,768]{2,3,1,0:T(8,128)} %fusion.50, bf16[2,256,5,128]{3,1,2,0:T(8,128)(2,1)S(1)} %copy-done.5, bf16[2,256,5,128]{3,1,2,0:T(8,128)(2,1)S(1)} %copy-done.11, bf16[2,256,5,128]{3,1,2,0:T(8,128)(2,1)S(1)} %copy-done.13, f32[2,5,256,768]{2,3,1,0:T(8,128)} %copy-done.26, ...), kind=kOutput, calls=%fused_computation.56 | convolution fusion | flops 523308288 | bytes 18360320 | tf_op jit(solution)/shard_map/shqk,skhe->sqhe/dot_general | solution.py:222
  301.3 5.9 %all-to-all-done = bf16[16,8,320]{2,1,0:T(8,128)(2,1)} async-done(((bf16[16,8,320]{2,1,0:T(8,128)(2,1)}), bf16[16,8,320]{2,1,0:T(8,128)(2,1)}, u32[]{:S(2)}, u32[]{:S(2)}) %all-to-all-start) | async-done | bytes 81952 | tf_op jit(solution)/shard_map/all_to_all | solution.py:185
  315.8 106.3 %reduce-scatter.3.cloned.1.call-done = bf16[1,1024,640]{2,1,0:T(8,128)(2,1)} async-done(((bf16[8,1024,640]{2,1,0:T(8,128)(2,1)}), bf16[1,1024,640]{2,1,0:T(8,128)(2,1)}) %reduce-scatter.3.cloned.1.call-update) | async-done | bytes 1310736 | tf_op jit(solution)/shard_map/reduce_scatter | solution.py:61
  (118 shorter events, 52.8 us)
Async XLA Ops:
  7.2 14.4 %copy-start = (bf16[128,320]{0,1:T(8,128)(2,1)S(1)}, bf16[128,320]{0,1:T(8,128)(2,1)}, u32[]{:S(2)}) copy-start(bf16[128,320]{0,1:T(8,128)(2,1)} %param.20) | copy-start | bytes 245764
  7.2 13.0 %copy-start.20 = (bf16[1,2,256,640]{3,2,1,0:T(8,128)(2,1)S(1)}, bf16[1,2,256,640]{3,2,1,0:T(8,128)(2,1)}, u32[]{:S(2)}) copy-start(bf16[1,2,256,640]{3,2,1,0:T(8,128)(2,1)} %param.14) | copy-start | bytes 1966084
  7.2 14.3 %copy-start.25 = (s32[1,4]{1,0:T(1,128)S(1)}, s32[1,4]{1,0:T(1,128)}, u32[]{:S(2)}) copy-start(s32[1,4]{1,0:T(1,128)} %param.21) | copy-start | bytes 52
  7.2 84.7 %all-gather.3.cloned.1.call-start = ((), (), s32[]{:S(2)}) async-start(), calls=%async_computation.3 | async-start | bytes 5898240 | tf_op jit(solution)/shard_map/all_gather | solution.py:88
  7.9 144.4 %all-gather.5.cloned.1.call-start = ((), (), s32[]{:S(2)}) async-start(), calls=%async_computation.4 | async-start | bytes 5898240 | tf_op jit(solution)/shard_map/all_gather | solution.py:89
  8.7 302.8 %reduce-scatter.5.cloned.1.call-start = ((), (), s32[]{:S(2)}) async-start(), calls=%async_computation.6 | async-start | bytes 7372800 | tf_op jit(solution)/shard_map/reduce_scatter | solution.py:56
  10.9 10.8 %collective-permute-start.1 = (bf16[2,256,640]{1,2,0:T(8,128)(2,1)}, bf16[2,256,640]{1,2,0:T(8,128)(2,1)S(1)}, u32[]{:S(2)}, u32[]{:S(2)}) collective-permute-start(bf16[2,256,640]{1,2,0:T(8,128)(2,1)} %bitcast), channel_id=1, source_target_pairs={{0,8},{8,16},{16,24},{24,32},{32,40},{40,48},{48,56},{56,64},{64,7... | collective-permute-start | bytes 1966088 | tf_op jit(solution)/shard_map/ppermute | solution.py:16
  12.2 19.6 %collective-permute-start = (bf16[2,256,640]{1,2,0:T(8,128)(2,1)}, bf16[2,256,640]{1,2,0:T(8,128)(2,1)}, u32[]{:S(2)}, u32[]{:S(2)}) collective-permute-start(bf16[2,256,640]{1,2,0:T(8,128)(2,1)} %bitcast), channel_id=1, source_target_pairs={{0,16},{8,24},{16,32},{24,40},{32,48},{40,56},{48,64},{56,72},{64,... | collective-permute-start | bytes 1966088 | tf_op jit(solution)/shard_map/ppermute | solution.py:16
  18.6 20.7 %copy-start.8 = (bf16[1,2,256,640]{2,3,1,0:T(8,128)(2,1)}, bf16[1,2,256,640]{2,3,1,0:T(8,128)(2,1)S(1)}, u32[]{:S(2)}) copy-start(bf16[1,2,256,640]{2,3,1,0:T(8,128)(2,1)S(1)} %copy.100) | copy-start | bytes 1966084
  20.2 16.3 %copy-start.6 = (bf16[1,2,256,640]{2,3,1,0:T(8,128)(2,1)}, bf16[1,2,256,640]{2,3,1,0:T(8,128)(2,1)S(1)}, u32[]{:S(2)}) copy-start(bf16[1,2,256,640]{2,3,1,0:T(8,128)(2,1)S(1)} %copy.105) | copy-start | bytes 1966084
  20.8 15.7 %copy-start.4 = (bf16[2,256,5,128]{3,1,2,0:T(8,128)(2,1)}, bf16[2,256,5,128]{3,1,2,0:T(8,128)(2,1)S(1)}, u32[]{:S(2)}) copy-start(bf16[2,256,5,128]{3,1,2,0:T(8,128)(2,1)S(1)} %copy.104) | copy-start | bytes 1966084
  91.9 60.5 %copy-start.2 = (bf16[320,5120]{1,0:T(8,128)(2,1)S(1)}, bf16[320,5120]{1,0:T(8,128)(2,1)}, u32[]{:S(2)}) copy-start(bf16[320,5120]{1,0:T(8,128)(2,1)} %param.19) | copy-start | bytes 9830404
  183.9 10.9 %collective-permute-start.4 = (bf16[8,320,1280]{2,1,0:T(8,128)(2,1)}, bf16[8,320,1280]{2,1,0:T(8,128)(2,1)}, u32[]{:S(2)}, u32[]{:S(2)}) collective-permute-start(bf16[8,320,1280]{2,1,0:T(8,128)(2,1)} %dynamic-slice_bitcast_fusion), channel_id=1, source_target_pairs={{0,8},{8,0},{1,9},{9,1},{2,10},{10,2},{3,11},{11,3},{4,12},{12,4},... | collective-permute-start | bytes 19660808 | tf_op jit(solution)/shard_map/ppermute | solution.py:54
  203.9 218.2 %reduce-scatter.3.cloned.1.call-start = ((), (), s32[]{:S(2)}) async-start(), calls=%async_computation.5 | async-start | bytes 11796480 | tf_op jit(solution)/shard_map/reduce_scatter | solution.py:61
  204.9 6.9 %copy-start.24 = (bf16[5120,320]{0,1:T(8,128)(2,1)S(1)}, bf16[5120,320]{0,1:T(8,128)(2,1)}, u32[]{:S(2)}) copy-start(bf16[5120,320]{0,1:T(8,128)(2,1)} %param.18) | copy-start | bytes 9830404
  261.9 18.6 %copy-start.5 = (bf16[2,256,5,128]{3,1,2,0:T(8,128)(2,1)S(1)}, bf16[2,256,5,128]{3,1,2,0:T(8,128)(2,1)}, u32[]{:S(2)}) copy-start(bf16[2,256,5,128]{3,1,2,0:T(8,128)(2,1)} %copy-done.4) | copy-start | bytes 1966084
  261.9 18.6 %copy-start.11 = (bf16[2,256,5,128]{3,1,2,0:T(8,128)(2,1)S(1)}, bf16[2,256,5,128]{3,1,2,0:T(8,128)(2,1)}, u32[]{:S(2)}) copy-start(bf16[2,256,5,128]{3,1,2,0:T(8,128)(2,1)} %copy-done.10) | copy-start | bytes 1966084
  261.9 18.7 %copy-start.13 = (bf16[2,256,5,128]{3,1,2,0:T(8,128)(2,1)S(1)}, bf16[2,256,5,128]{3,1,2,0:T(8,128)(2,1)}, u32[]{:S(2)}) copy-start(bf16[2,256,5,128]{3,1,2,0:T(8,128)(2,1)} %copy-done.12) | copy-start | bytes 1966084
  265.0 43.8 %collective-permute-start.3 = (bf16[2,256,640]{1,2,0:T(8,128)(2,1)}, bf16[2,256,640]{1,2,0:T(8,128)(2,1)}, u32[]{:S(2)}, u32[]{:S(2)}) collective-permute-start(bf16[2,256,640]{1,2,0:T(8,128)(2,1)} %pad_maximum_fusion.14), channel_id=1, source_target_pairs={{16,0},{24,8},{32,16},{40,24},{48,32},{56,40},{64,48},{72,56},{80,... | collective-permute-start | bytes 1966088 | tf_op jit(solution)/shard_map/ppermute | solution.py:16
  267.2 41.6 %collective-permute-start.2 = (bf16[2,256,640]{1,2,0:T(8,128)(2,1)}, bf16[2,256,640]{1,2,0:T(8,128)(2,1)S(1)}, u32[]{:S(2)}, u32[]{:S(2)}) collective-permute-start(bf16[2,256,640]{1,2,0:T(8,128)(2,1)} %pad_maximum_fusion.13), channel_id=1, source_target_pairs={{8,0},{16,8},{24,16},{32,24},{40,32},{48,40},{56,48},{64,56},{72,6... | collective-permute-start | bytes 1966088 | tf_op jit(solution)/shard_map/ppermute | solution.py:16
  270.8 36.4 %all-to-all-start = ((bf16[16,8,320]{2,1,0:T(8,128)(2,1)}), bf16[16,8,320]{2,1,0:T(8,128)(2,1)}, u32[]{:S(2)}, u32[]{:S(2)}) async-start(bf16[16,8,320]{2,1,0:T(8,128)(2,1)} %bitcast.50), calls=%async_computation.2 | async-start | bytes 196608 | tf_op jit(solution)/shard_map/all_to_all | solution.py:185
  311.5 112.1 %copy-start.18 = (bf16[1,2,256,640]{3,2,1,0:T(8,128)(2,1)S(1)}, bf16[1,2,256,640]{3,2,1,0:T(8,128)(2,1)}, u32[]{:S(2)}) copy-start(bf16[1,2,256,640]{3,2,1,0:T(8,128)(2,1)} %param.12) | copy-start | bytes 1966084
  311.5 112.1 %copy-start.19 = (bf16[1,2,256,640]{3,2,1,0:T(8,128)(2,1)S(1)}, bf16[1,2,256,640]{3,2,1,0:T(8,128)(2,1)}, u32[]{:S(2)}) copy-start(bf16[1,2,256,640]{3,2,1,0:T(8,128)(2,1)} %param.23) | copy-start | bytes 1966084
  313.8 111.1 %copy-start.1 = (bf16[128,320]{0,1:T(8,128)(2,1)S(1)}, bf16[128,320]{0,1:T(8,128)(2,1)}, u32[]{:S(2)}) copy-start(bf16[128,320]{0,1:T(8,128)(2,1)} %param.20) | copy-start | bytes 245764
  (13 other events, 51.6 us)
Sparse Core Ops, SparseCore 0:
  9.7 82.1 all-gather.2
  93.5 58.7 all-gather.4
  204.0 106.5 reduce-scatter.4
  312.9 109.1 reduce-scatter.2
